TPU v7x, 512 devices: a whole 4x8x8 slice. The times are simulated.
512 devices in a mesh: dp: 64 (over z, y), tensor: 4 (over x), sect: 2 (over core).
Axes of the slice: x: 4, y: 8, z: 8, core: 2. Of those that a mesh axis runs over, the one named last changes fastest.
Arguments:
- tokens: bfloat16 [4096, 2048], P(('dp', 'sect'), 'tensor'), may hold values from -6 to 6
- route_experts: int32 [4096, 8], P(('dp', 'sect')), may hold values from 0 to 127, all different within a row; in each aligned block of 32 rows (0 to 31, 32 to 63, ...) at most 5 rows name the same one
- route_weights: float32 [4096, 8], P(('dp', 'sect')), may hold values from 0.05 to 1
- gate_weight: bfloat16 [128, 2048, 768], P(('dp', 'sect'), None, 'tensor'), may hold values from -0.125 to 0.125
- up_weight: bfloat16 [128, 2048, 768], P(('dp', 'sect'), None, 'tensor'), may hold values from -0.125 to 0.125
- down_weight: bfloat16 [128, 768, 2048], P(('dp', 'sect'), 'tensor'), may hold values from -0.21875 to 0.21875
- query: bfloat16 [4096, 64, 128], P(('dp', 'sect'), 'tensor'), may hold values from -48 to 48
- cache_keys: bfloat16 [4096, 128, 4, 128], P(('dp', 'sect'), None, 'tensor'), may hold values from -16 to 16
- cache_values: bfloat16 [4096, 128, 4, 128], P(('dp', 'sect'), None, 'tensor'), may hold values from -6 to 6
- lengths: int32 [4096], P(('dp', 'sect')), may hold values from 2 to 128, as said below
Outputs:
- mixture: bfloat16 [4096, 2048], P(('dp', 'sect'), 'tensor')
- attention: bfloat16 [4096, 64, 128], P(('dp', 'sect'), 'tensor')
Inputs may be any that keep to these rules, and one draw needn't show every extreme that they name: `route_experts`: each row names 8 different experts; in each block of 32 rows no expert is named more than 5 times, a bound that some block reaches. `lengths`: every block's first row has all 128 positions filled.
All inputs are finite; a program needn't handle non-finite values.
Results may differ from a plain program's by a relative error of at most 0.015.
Values may be sent and summed in bfloat16 or wider, within the bound.
No kernel may reach another device: no remote copies, remote signals or barrier semaphores. Data moves between devices by JAX's collectives and lax.ppermute only.
A program may use at most 64 MiB of HBM per device.

v0:
```python
import jax
import jax.numpy as jnp
from jax import lax
from jax.sharding import PartitionSpec as P

EXPERTS = 128
CAP = 5


def route_tables(expert_ids, weights, experts, capacity):
    row_count, top_count = expert_ids.shape
    pair_count = row_count * top_count
    flat_ids = expert_ids.reshape(pair_count)
    one_hot = (flat_ids[:, None] == jnp.arange(experts, dtype=jnp.int32)[None, :]).astype(
        jnp.float32
    )
    ordinal = jnp.arange(pair_count, dtype=jnp.int32)
    earlier = (ordinal[:, None] > ordinal[None, :]).astype(jnp.float32)
    counts = jnp.dot(earlier, one_hot, preferred_element_type=jnp.float32)
    slot_index = jnp.sum(counts * one_hot, axis=1).astype(jnp.int32)
    target = flat_ids * capacity + slot_index
    select = (jnp.arange(experts * capacity, dtype=jnp.int32)[:, None] == target[None, :]).astype(
        jnp.float32
    )
    select = select.reshape(experts * capacity, row_count, top_count)
    share_norm = (weights / jnp.sum(weights, axis=1, keepdims=True)).astype(jnp.bfloat16)
    share_norm = lax.optimization_barrier(share_norm).astype(jnp.float32)
    dispatch = jnp.sum(select, axis=2).astype(jnp.bfloat16)
    combine = jnp.sum(select * share_norm[None, :, :], axis=2).astype(jnp.bfloat16)
    return (dispatch, combine)


def attend(query, cache_keys, cache_values, lengths):
    row_count, head_count, head_size = query.shape
    kv_count = cache_keys.shape[2]
    group_size = head_count // kv_count
    queries = query.reshape(row_count, kv_count, group_size, head_size)
    scores = jnp.einsum(
        "rkgd,rlkd->rkgl", queries, cache_keys, preferred_element_type=jnp.float32
    ) * head_size ** (-0.5)
    valid = jnp.arange(cache_keys.shape[1], dtype=jnp.int32)[None, :] < lengths[:, None]
    scores = jnp.where(valid[:, None, None, :], scores, -1e30)
    highest = jnp.max(scores, axis=3, keepdims=True)
    expo = jnp.exp(scores - highest)
    probs = (expo / jnp.sum(expo, axis=3, keepdims=True)).astype(jnp.bfloat16)
    result = jnp.einsum("rkgl,rlkd->rkgd", probs, cache_values, preferred_element_type=jnp.float32)
    return result.astype(jnp.bfloat16).reshape(row_count, head_count, head_size)


def local(
    tokens,
    route_experts,
    route_weights,
    gate_weight,
    up_weight,
    down_weight,
    query,
    cache_keys,
    cache_values,
    lengths,
):
    owners = lax.axis_size("dp") * lax.axis_size("sect")
    dispatch, combine = route_tables(route_experts, route_weights, EXPERTS, CAP)
    slot_total = EXPERTS * CAP
    per_owner = slot_total // owners
    full_rows = lax.all_gather(tokens, "tensor", axis=1, tiled=True)
    local_buffer = jnp.dot(dispatch, full_rows, preferred_element_type=jnp.float32).astype(
        jnp.bfloat16
    )
    local_buffer = local_buffer.reshape(owners, per_owner, local_buffer.shape[1])
    arrived = lax.all_to_all(local_buffer, ("dp", "sect"), split_axis=0, concat_axis=0, tiled=True)
    own_experts = gate_weight.shape[0]
    width = arrived.shape[2]
    inputs = (
        arrived.reshape(owners, own_experts, CAP, width)
        .transpose(1, 0, 2, 3)
        .reshape(own_experts, owners * CAP, width)
    )
    gate_part = jnp.einsum("end,edf->enf", inputs, gate_weight, preferred_element_type=jnp.float32)
    up_part = jnp.einsum("end,edf->enf", inputs, up_weight, preferred_element_type=jnp.float32)
    hidden = (jax.nn.silu(gate_part) * up_part).astype(jnp.bfloat16)
    partial_sum = jnp.einsum(
        "enf,efd->end", hidden, down_weight, preferred_element_type=jnp.float32
    )
    summed = lax.psum_scatter(
        partial_sum.astype(jnp.bfloat16), "tensor", scatter_dimension=2, tiled=True
    )
    last = summed.shape[2]
    returned = lax.all_to_all(
        summed.reshape(own_experts, owners, CAP, last)
        .transpose(1, 0, 2, 3)
        .reshape(owners, own_experts * CAP, last),
        ("dp", "sect"),
        split_axis=0,
        concat_axis=0,
        tiled=True,
    )
    expert_out = returned.reshape(slot_total, returned.shape[2])
    mixture = jnp.dot(combine.T, expert_out, preferred_element_type=jnp.float32).astype(
        jnp.bfloat16
    )
    attention = attend(query, cache_keys, cache_values, lengths)
    return (mixture, attention)


def solution(mesh):
    placed = (
        P(("dp", "sect"), "tensor"),
        P(("dp", "sect"), None),
        P(("dp", "sect"), None),
        P(("dp", "sect"), None, "tensor"),
        P(("dp", "sect"), None, "tensor"),
        P(("dp", "sect"), "tensor", None),
        P(("dp", "sect"), "tensor", None),
        P(("dp", "sect"), None, "tensor", None),
        P(("dp", "sect"), None, "tensor", None),
        P(("dp", "sect")),
    )
    return jax.shard_map(
        local,
        mesh=mesh,
        in_specs=placed,
        out_specs=(P(("dp", "sect"), "tensor"), P(("dp", "sect"), "tensor", None)),
        check_vma=False,
    )
```

profile of v0, /device:TPU:1, one launch (start us, length us, event | category | flops | bytes accessed | tf_op | source)
XLA Modules:
  0.0 257.8 jit_solution(12946429351181998566)
XLA Ops:
  7.2 0.8 copy.17
  8.1 0.1 eq.30
  8.2 0.2 fusion.6
  8.4 0.1 convert_element_type.53
  8.5 0.7 reduce_sum.46
  9.2 0.7 divide_convert_fusion.2
  9.9 0.1 copy.19
  10.0 10.5 %all_gather.3 = bf16[32,2048]{1,0:T(8,128)(2,1)S(1)} all-gather(bf16[32,512]{1,0:T(8,128)(2,1)} %param.10), channel_id=1, replica_groups=mesh['dp'=64,'tensor'=4,'sect'=2] {'tensor'}, dimensions={1}, use_global_device_ids=true | all-gather | bytes 163840 | tf_op jit(solution)/shard_map/all_gather | solution.py:66
  20.5 0.5 select_reduce_fusion
  21.0 2.4 convolution_convert_fusion
  23.4 5.5 %reshape.112 = bf16[128,5,2048]{2,1,0:T(8,128)(2,1)} reshape(bf16[640,2048]{1,0:T(8,128)(2,1)} %convolution_convert_fusion) | data formatting | bytes 5242880 | tf_op jit(solution)/shard_map/reshape | solution.py:70
  28.8 117.5 %all_to_all.10 = bf16[128,5,2048]{2,1,0:T(8,128)(2,1)} all-to-all(bf16[128,5,2048]{2,1,0:T(8,128)(2,1)} %reshape.112), channel_id=1, replica_groups=mesh['dp'=64,'tensor'=4,'sect'=2] {'dp','sect'}, dimensions={0} | all-to-all | bytes 5242880 | tf_op jit(solution)/shard_map/all_to_all | solution.py:71
  146.3 5.7 %reshape.113 = bf16[640,2048]{1,0:T(8,128)(2,1)} reshape(bf16[128,5,2048]{2,1,0:T(8,128)(2,1)} %all_to_all.10) | data formatting | bytes 5242880 | tf_op jit(solution)/shard_map/reshape
  152.0 2.8 %fusion.11 = f32[640,192]{0,1:T(8,128)S(1)} fusion(bf16[640,2048]{1,0:T(8,128)(2,1)} %reshape.113, bf16[1,2048,192]{1,2,0:T(8,128)(2,1)S(1)} %copy-done.3), kind=kOutput, calls=%fused_computation.18 | convolution fusion | flops 503316480 | bytes 3899392 | tf_op jit(solution)/shard_map/end,edf->enf/dot_general | solution.py:79
  154.8 5.6 %fusion.1 = bf16[1,640,2048]{2,1,0:T(8,128)(2,1)} fusion(bf16[1,192,2048]{2,1,0:T(8,128)(2,1)S(1)} %copy-done.4, bf16[640,2048]{1,0:T(8,128)(2,1)} %reshape.113, bf16[1,2048,192]{1,2,0:T(8,128)(2,1)} %param.14, f32[640,192]{0,1:T(8,128)S(1)} %fusion.11), kind=kOutput, calls=%fused_computation.3 | convolution fusion | flops 1008680960 | bytes 7307264 | tf_op jit(solution)/shard_map/enf,efd->end/dot_general | solution.py:82
  160.5 42.1 %reduce-scatter.2.cloned.1.call-done = bf16[1,640,512]{2,1,0:T(8,128)(2,1)} async-done(((bf16[1,640,2048]{2,1,0:T(8,128)(2,1)}), bf16[1,640,512]{2,1,0:T(8,128)(2,1)}) %reduce-scatter.2.cloned.1.call-update) | async-done | bytes 655376 | tf_op jit(solution)/shard_map/reduce_scatter | solution.py:85
  202.6 2.2 reshape_transpose_reshape.4
  204.7 14.2 %all-to-all-start.1 = ((bf16[128,5,512]{2,1,0:T(8,128)(2,1)}), bf16[128,5,512]{2,1,0:T(8,128)(2,1)S(1)}, u32[]{:S(2)}, u32[]{:S(2)}) async-start(bf16[128,5,512]{2,1,0:T(8,128)(2,1)} %reshape_transpose_reshape.4), calls=%async_computation.2 | async-start | bytes 2097152 | tf_op jit(solution)/shard_map/all_to_all | solution.py:89
  219.1 0.7 fusion.5
  219.7 0.2 fusion.27
  220.0 2.8 %convolution_convert_fusion.2 = bf16[32,16,128]{2,1,0:T(8,128)(2,1)} fusion(bf16[32,128,1,128]{3,1,2,0:T(8,128)(2,1)} %param.18, f32[32,16]{1,0:T(8,128)S(1)} %fusion.27, f32[32,16,128]{2,1,0:T(8,128)S(1)} %fusion.5), kind=kOutput, calls=%fused_computation.10 | convolution fusion | flops 17040000 | bytes 1443840 | tf_op jit(solution)/shard_map/rkgl,rlkd->rkgd/dot_general | solution.py:46
  222.8 27.1 %all-to-all-done.1 = bf16[128,5,512]{2,1,0:T(8,128)(2,1)S(1)} async-done(((bf16[128,5,512]{2,1,0:T(8,128)(2,1)}), bf16[128,5,512]{2,1,0:T(8,128)(2,1)S(1)}, u32[]{:S(2)}, u32[]{:S(2)}) %all-to-all-start.1) | async-done | bytes 655392 | tf_op jit(solution)/shard_map/all_to_all | solution.py:89
  249.9 0.3 reshape.117
  250.2 0.8 convolution_convert_fusion.3
  (15 shorter events, 0.2 us)
Async XLA Ops:
  7.2 211.9 %copy-start = (bf16[32,128,1,128]{3,1,2,0:T(8,128)(2,1)S(1)}, bf16[32,128,1,128]{3,1,2,0:T(8,128)(2,1)}, u32[]{:S(2)}) copy-start(bf16[32,128,1,128]{3,1,2,0:T(8,128)(2,1)} %param.17) | copy-start | bytes 3145732
  7.2 195.4 %reduce-scatter.2.cloned.1.call-start = ((), (), s32[]{:S(2)}) async-start(), calls=%async_computation.3 | async-start | bytes 3276800 | tf_op jit(solution)/shard_map/reduce_scatter | solution.py:85
  146.3 5.7 %copy-start.3 = (bf16[1,2048,192]{1,2,0:T(8,128)(2,1)S(1)}, bf16[1,2048,192]{1,2,0:T(8,128)(2,1)}, u32[]{:S(2)}) copy-start(bf16[1,2048,192]{1,2,0:T(8,128)(2,1)} %param.13) | copy-start | bytes 2359300
  152.0 2.8 %copy-start.4 = (bf16[1,192,2048]{2,1,0:T(8,128)(2,1)S(1)}, bf16[1,192,2048]{2,1,0:T(8,128)(2,1)}, u32[]{:S(2)}) copy-start(bf16[1,192,2048]{2,1,0:T(8,128)(2,1)} %param.15) | copy-start | bytes 2359300
  160.5 58.5 %copy-start.2 = (s32[32]{0:T(128)S(1)}, s32[32]{0:T(128)}, u32[]{:S(2)}) copy-start(s32[32]{0:T(128)} %param.19) | copy-start | bytes 388
  160.5 58.6 %copy-start.1 = (bf16[32,16,128]{2,1,0:T(8,128)(2,1)S(1)}, bf16[32,16,128]{2,1,0:T(8,128)(2,1)}, u32[]{:S(2)}) copy-start(bf16[32,16,128]{2,1,0:T(8,128)(2,1)} %param.16) | copy-start | bytes 393220
  204.7 45.2 %all-to-all-start.1 = ((bf16[128,5,512]{2,1,0:T(8,128)(2,1)}), bf16[128,5,512]{2,1,0:T(8,128)(2,1)S(1)}, u32[]{:S(2)}, u32[]{:S(2)}) async-start(bf16[128,5,512]{2,1,0:T(8,128)(2,1)} %reshape_transpose_reshape.4), calls=%async_computation.2 | async-start | bytes 2097152 | tf_op jit(solution)/shard_map/all_to_all | solution.py:89
Sparse Core Ops, SparseCore 0:
  160.6 41.9 reduce-scatter.1
where the time goes:
time: 259 us; the launch traced here: 258 us
  blocking collectives  128 us (49%)
  waiting for transfers between devices  69.2 us (27%)
  matrix products  15.4 us (6%)
  local copies, waits for them, and re-layouts  14.7 us (6%)
  starting transfers between devices  14.3 us (6%)
  between operations  14.1 us (5%)
    all_to_all x1, blocking collectives, local(): lax.all_to_all(local_buffer, ('dp', 'sect'), split_axis=0, concat_axis=0,...  117 us
    reduce_scatter x1, waiting for transfers between devices, local(): lax.psum_scatter(partial_sum.astype(jnp.bfloat16), 'tensor', scatter_dime...  42.1 us
    all_to_all x1, waiting for transfers between devices, local(): lax.all_to_all(summed.reshape(own_experts, owners, CAP, last).transpose(1...  27.1 us
    all_to_all x1, starting transfers between devices, local(): lax.all_to_all(summed.reshape(own_experts, owners, CAP, last).transpose(1...  14.2 us
    all_gather x1, blocking collectives, local(): full_rows = lax.all_gather(tokens, 'tensor', axis=1, tiled=True)  10.5 us
    reshape x1, local copies, waits for them, and re-layouts  5.67 us
    dot_general x1, matrix products, local(): jnp.einsum('enf,efd->end', hidden, down_weight, preferred_element_type=jn...  5.64 us
    reshape x1, local copies, waits for them, and re-layouts, local(): local_buffer.reshape(owners, per_owner, local_buffer.shape[1])  5.46 us
  transfers between devices with their start and end apart: 2, of which 2 were waited for; matrix products, arithmetic and copies ran while one was open for 1% of the time, Pallas kernels for 0%

commit v1 on v0

--- a/solution.py
+++ b/solution.py
@@ -63,21 +63,27 @@
     dispatch, combine = route_tables(route_experts, route_weights, EXPERTS, CAP)
     slot_total = EXPERTS * CAP
     per_owner = slot_total // owners
-    full_rows = lax.all_gather(tokens, "tensor", axis=1, tiled=True)
-    local_buffer = jnp.dot(dispatch, full_rows, preferred_element_type=jnp.float32).astype(
+    local_buffer = jnp.dot(dispatch, tokens, preferred_element_type=jnp.float32).astype(
         jnp.bfloat16
     )
     local_buffer = local_buffer.reshape(owners, per_owner, local_buffer.shape[1])
     arrived = lax.all_to_all(local_buffer, ("dp", "sect"), split_axis=0, concat_axis=0, tiled=True)
     own_experts = gate_weight.shape[0]
     width = arrived.shape[2]
+    pieces = lax.axis_size("tensor")
     inputs = (
         arrived.reshape(owners, own_experts, CAP, width)
         .transpose(1, 0, 2, 3)
         .reshape(own_experts, owners * CAP, width)
     )
-    gate_part = jnp.einsum("end,edf->enf", inputs, gate_weight, preferred_element_type=jnp.float32)
-    up_part = jnp.einsum("end,edf->enf", inputs, up_weight, preferred_element_type=jnp.float32)
+    gathered = lax.all_gather(inputs, "tensor", axis=0, tiled=False)
+    hidden_width = gate_weight.shape[2]
+    gate_view = gate_weight.reshape(own_experts, pieces, width, hidden_width)
+    up_view = up_weight.reshape(own_experts, pieces, width, hidden_width)
+    gate_part = jnp.einsum(
+        "tend,etdf->enf", gathered, gate_view, preferred_element_type=jnp.float32
+    )
+    up_part = jnp.einsum("tend,etdf->enf", gathered, up_view, preferred_element_type=jnp.float32)
     hidden = (jax.nn.silu(gate_part) * up_part).astype(jnp.bfloat16)
     partial_sum = jnp.einsum(
         "enf,efd->end", hidden, down_weight, preferred_element_type=jnp.float32

time: 259 us -> 201 us (0.78)
  blocking collectives: 128 us -> 49.1 us
  waiting for transfers between devices: 69.2 us -> 99.3 us
  local copies, waits for them, and re-layouts: 14.7 us -> 6.54 us
    all_to_all x1, blocking collectives: 117 us -> 49.1 us  [local(): lax.all_to_all(local_buffer, ('dp', 'sect'), split_axis=0, concat_axis=0,...]
    all_gather x0 -> x1, waiting for transfers between devices: none -> 32.5 us  [local(): gathered = lax.all_gather(inputs, 'tensor', axis=0, tiled=False)]
    all_gather x1 -> x0, blocking collectives: 10.5 us -> none  [local(): full_rows = lax.all_gather(tokens, 'tensor', axis=1, tiled=True)]
    reshape x1 -> x0, local copies, waits for them, and re-layouts: 5.67 us -> none
    reshape x1, local copies, waits for them, and re-layouts: 5.46 us -> 0.25 us  [local(): local_buffer.reshape(owners, per_owner, local_buffer.shape[1])]
  transfers between devices with their start and end apart: 2 -> 3, of which waited for: 2 -> 3; matrix products, arithmetic and copies ran while one was open for 1% -> 2% of each run, Pallas kernels for 0% -> 0%
where the time goes in v1:
time: 201 us; the launch traced here: 200 us
  waiting for transfers between devices  99.3 us (49%)
  blocking collectives  49.1 us (24%)
  matrix products  14.7 us (7%)
  starting transfers between devices  14.3 us (7%)
  between operations  14.1 us (7%)
  local copies, waits for them, and re-layouts  6.54 us (3%)
  other arithmetic  2.2 us (1%)
    all_to_all x1, blocking collectives, local(): lax.all_to_all(local_buffer, ('dp', 'sect'), split_axis=0, concat_axis=0,...  49.1 us
    reduce_scatter x1, waiting for transfers between devices, local(): lax.psum_scatter(partial_sum.astype(jnp.bfloat16), 'tensor', scatter_dime...  39.7 us
    all_gather x1, waiting for transfers between devices, local(): gathered = lax.all_gather(inputs, 'tensor', axis=0, tiled=False)  32.5 us
    all_to_all x1, waiting for transfers between devices, local(): lax.all_to_all(summed.reshape(own_experts, owners, CAP, last).transpose(1...  27.1 us
    all_to_all x1, starting transfers between devices, local(): lax.all_to_all(summed.reshape(own_experts, owners, CAP, last).transpose(1...  14.2 us
    dot_general x1, matrix products, local(): jnp.einsum('enf,efd->end', hidden, down_weight, preferred_element_type=jn...  5.54 us
  transfers between devices with their start and end apart: 3, of which 3 were waited for; matrix products, arithmetic and copies ran while one was open for 2% of the time, Pallas kernels for 0%

profile of v1, /device:TPU:1, one launch (start us, length us, event | category | flops | bytes accessed | tf_op | source)
XLA Modules:
  0.0 200.3 jit_solution(56039022843777184)
XLA Ops:
  7.2 0.8 copy.25
  8.2 0.2 fusion.21
  8.5 0.7 reduce_sum.46
  9.2 0.7 divide_convert_fusion.2
  10.0 0.5 select_reduce_fusion
  10.5 1.1 convolution_convert_fusion.1
  11.6 0.3 reshape.114
  11.9 49.1 %all_to_all.10 = bf16[128,5,512]{2,1,0:T(8,128)(2,1)S(1)} all-to-all(bf16[128,5,512]{2,1,0:T(8,128)(2,1)S(1)} %reshape.114), channel_id=1, replica_groups=mesh['dp'=64,'tensor'=4,'sect'=2] {'dp','sect'}, dimensions={0} | all-to-all | bytes 1310720 | tf_op jit(solution)/shard_map/all_to_all | solution.py:70
  61.0 1.1 all_gather_reshape_transpose_reshape.3
  62.2 0.6 reshape.116
  62.8 0.5 copy-done.2
  63.2 0.6 reshape.117
  63.8 32.5 %all-gather.2.cloned.1.call-done = bf16[4,1,640,512]{3,2,1,0:T(8,128)(2,1)} async-done(((bf16[1,1,640,512]{3,2,1,0:T(8,128)(2,1)}), bf16[4,1,640,512]{3,2,1,0:T(8,128)(2,1)}) %all-gather.2.cloned.1.call-update) | async-done | bytes 2621456 | tf_op jit(solution)/shard_map/all_gather | solution.py:79
  96.3 3.5 %fusion.6 = f32[640,192]{0,1:T(8,128)} fusion(bf16[4,1,640,512]{3,2,1,0:T(8,128)(2,1)} %all-gather.2.cloned.1.call-done, bf16[4,512,192]{1,0,2:T(4,128)(2,1)S(1)} %reshape.116), kind=kOutput, calls=%fused_computation.8 | convolution fusion | flops 503316480 | bytes 3899392 | tf_op jit(solution)/shard_map/tend,etdf->enf/dot_general | solution.py:83
  99.8 5.5 %fusion.1 = bf16[1,640,2048]{2,1,0:T(8,128)(2,1)} fusion(bf16[1,192,2048]{2,1,0:T(8,128)(2,1)S(1)} %copy-done.5, bf16[4,1,640,512]{3,2,1,0:T(8,128)(2,1)} %all-gather.2.cloned.1.call-done, bf16[4,512,192]{1,0,2:T(4,128)(2,1)S(1)} %reshape.117, f32[640,192]{0,1:T(8,128)} %fusion.6), kind=kOutput, calls=%fused_computation.2 | convolution fusion | flops 1008680960 | bytes 7307264 | tf_op jit(solution)/shard_map/enf,efd->end/dot_general | solution.py:88
  105.4 39.7 %reduce-scatter.2.cloned.1.call-done = bf16[1,640,512]{2,1,0:T(8,128)(2,1)} async-done(((bf16[1,640,2048]{2,1,0:T(8,128)(2,1)}), bf16[1,640,512]{2,1,0:T(8,128)(2,1)}) %reduce-scatter.2.cloned.1.call-update) | async-done | bytes 655376 | tf_op jit(solution)/shard_map/reduce_scatter | solution.py:91
  145.1 2.2 %reshape_transpose_reshape.3 = bf16[128,5,512]{2,1,0:T(8,128)(2,1)} reshape(bf16[1,640,512]{2,1,0:T(8,128)(2,1)} %reduce-scatter.2.cloned.1.call-done) | data formatting | bytes 1310720 | tf_op jit(solution)/shard_map/reshape;transpose;reshape | solution.py:98
  147.2 14.2 %all-to-all-start.1 = ((bf16[128,5,512]{2,1,0:T(8,128)(2,1)}), bf16[128,5,512]{2,1,0:T(8,128)(2,1)S(1)}, u32[]{:S(2)}, u32[]{:S(2)}) async-start(bf16[128,5,512]{2,1,0:T(8,128)(2,1)} %reshape_transpose_reshape.3), calls=%async_computation.2 | async-start | bytes 2097152 | tf_op jit(solution)/shard_map/all_to_all | solution.py:95
  161.6 0.7 fusion.20
  162.2 0.2 fusion.43
  162.5 2.8 %convolution_convert_fusion.2 = bf16[32,16,128]{2,1,0:T(8,128)(2,1)} fusion(bf16[32,128,1,128]{3,1,2,0:T(8,128)(2,1)} %param.18, f32[32,16]{1,0:T(8,128)S(1)} %fusion.43, f32[32,16,128]{2,1,0:T(8,128)S(1)} %fusion.20), kind=kOutput, calls=%fused_computation.16 | convolution fusion | flops 17040000 | bytes 1443840 | tf_op jit(solution)/shard_map/rkgl,rlkd->rkgd/dot_general | solution.py:46
  165.3 27.1 %all-to-all-done.1 = bf16[128,5,512]{2,1,0:T(8,128)(2,1)S(1)} async-done(((bf16[128,5,512]{2,1,0:T(8,128)(2,1)}), bf16[128,5,512]{2,1,0:T(8,128)(2,1)S(1)}, u32[]{:S(2)}, u32[]{:S(2)}) %all-to-all-start.1) | async-done | bytes 655392 | tf_op jit(solution)/shard_map/all_to_all | solution.py:95
  192.4 0.3 reshape.119
  192.7 0.8 convolution_convert_fusion.3
  (21 shorter events, 0.5 us)
Async XLA Ops:
  7.2 154.4 %copy-start = (bf16[32,128,1,128]{3,1,2,0:T(8,128)(2,1)S(1)}, bf16[32,128,1,128]{3,1,2,0:T(8,128)(2,1)}, u32[]{:S(2)}) copy-start(bf16[32,128,1,128]{3,1,2,0:T(8,128)(2,1)} %param.17) | copy-start | bytes 3145732
  7.2 89.2 %all-gather.2.cloned.1.call-start = ((), (), s32[]{:S(2)}) async-start(), calls=%async_computation.3 | async-start | bytes 3276800 | tf_op jit(solution)/shard_map/all_gather | solution.py:79
  61.0 1.2 copy-start.1
  62.1 1.1 copy-start.2
  62.1 82.9 %reduce-scatter.2.cloned.1.call-start = ((), (), s32[]{:S(2)}) async-start(), calls=%async_computation.4 | async-start | bytes 3276800 | tf_op jit(solution)/shard_map/reduce_scatter | solution.py:91
  63.8 36.0 %copy-start.5 = (bf16[1,192,2048]{2,1,0:T(8,128)(2,1)S(1)}, bf16[1,192,2048]{2,1,0:T(8,128)(2,1)}, u32[]{:S(2)}) copy-start(bf16[1,192,2048]{2,1,0:T(8,128)(2,1)} %param.15) | copy-start | bytes 2359300
  105.4 56.1 %copy-start.4 = (s32[32]{0:T(128)S(1)}, s32[32]{0:T(128)}, u32[]{:S(2)}) copy-start(s32[32]{0:T(128)} %param.19) | copy-start | bytes 388
  105.4 56.2 %copy-start.3 = (bf16[32,16,128]{2,1,0:T(8,128)(2,1)S(1)}, bf16[32,16,128]{2,1,0:T(8,128)(2,1)}, u32[]{:S(2)}) copy-start(bf16[32,16,128]{2,1,0:T(8,128)(2,1)} %param.16) | copy-start | bytes 393220
  147.2 45.1 %all-to-all-start.1 = ((bf16[128,5,512]{2,1,0:T(8,128)(2,1)}), bf16[128,5,512]{2,1,0:T(8,128)(2,1)S(1)}, u32[]{:S(2)}, u32[]{:S(2)}) async-start(bf16[128,5,512]{2,1,0:T(8,128)(2,1)} %reshape_transpose_reshape.3), calls=%async_computation.2 | async-start | bytes 2097152 | tf_op jit(solution)/shard_map/all_to_all | solution.py:95
Sparse Core Ops, SparseCore 0:
  62.2 34.0 all-gather.1
  105.5 39.4 reduce-scatter.1

commit v2 on v1

--- a/solution.py
+++ b/solution.py
@@ -85,12 +85,19 @@
     )
     up_part = jnp.einsum("tend,etdf->enf", gathered, up_view, preferred_element_type=jnp.float32)
     hidden = (jax.nn.silu(gate_part) * up_part).astype(jnp.bfloat16)
-    partial_sum = jnp.einsum(
-        "enf,efd->end", hidden, down_weight, preferred_element_type=jnp.float32
+    out_width = down_weight.shape[2] // pieces
+    down_mine = lax.all_to_all(
+        down_weight.reshape(own_experts, hidden_width, pieces, out_width).transpose(2, 0, 1, 3),
+        "tensor",
+        split_axis=0,
+        concat_axis=0,
+        tiled=True,
     )
-    summed = lax.psum_scatter(
-        partial_sum.astype(jnp.bfloat16), "tensor", scatter_dimension=2, tiled=True
-    )
+    hidden_all = lax.all_gather(hidden.transpose(0, 2, 1), "tensor", axis=0, tiled=False)
+    group_sums = jnp.einsum(
+        "gefn,gefc->genc", hidden_all, down_mine, preferred_element_type=jnp.float32
+    ).astype(jnp.bfloat16)
+    summed = jnp.sum(group_sums.astype(jnp.float32), axis=0).astype(jnp.bfloat16)
     last = summed.shape[2]
     returned = lax.all_to_all(
         summed.reshape(own_experts, owners, CAP, last)

time: 201 us -> 172 us (0.86)
  waiting for transfers between devices: 99.3 us -> 59.8 us
  blocking collectives: 49.1 us -> 60.7 us
  matrix products: 14.7 us -> 11.7 us
  local copies, waits for them, and re-layouts: 6.54 us -> 8.56 us
    reduce_scatter x1 -> x0, waiting for transfers between devices: 39.7 us -> none  [local(): lax.psum_scatter(partial_sum.astype(jnp.bfloat16), 'tensor', scatter_dime...]
    all_gather x0 -> x1, blocking collectives: none -> 11.5 us  [local(): lax.all_gather(hidden.transpose(0, 2, 1), 'tensor', axis=0, tiled=False)]
    all_to_all x0 -> x1, starting transfers between devices: none -> 4.18 us  [local(): lax.all_to_all(down_weight.reshape(own_experts, hidden_width, pieces, out...]
    all_to_all x1, starting transfers between devices: 14.2 us -> 10.4 us  [local(): lax.all_to_all(summed.reshape(own_experts, owners, CAP, last).transpose(1...]
    dot_general x1 -> x2, matrix products: 5.54 us -> 3.15 us  [the longest x1 2.15 us: local(): jnp.einsum('gefn,gefc->genc', hidden_all, down_mine, preferred_element_ty...]
    reshape x0 -> x1, local copies, waits for them, and re-layouts: none -> 2.36 us  [local(): down_weight.reshape(own_experts, hidden_width, pieces, out_width)]
  transfers between devices with their start and end apart: 3 -> 3, of which waited for: 3 -> 2; matrix products, arithmetic and copies ran while one was open for 2% -> 7% of each run, Pallas kernels for 0% -> 0%
where the time goes in v2:
time: 172 us
  blocking collectives  60.7 us (35%)
  waiting for transfers between devices  59.8 us (35%)
  starting transfers between devices  14.6 us (8%)
  between operations  14.2 us (8%)
  matrix products  11.7 us (7%)
  local copies, waits for them, and re-layouts  8.56 us (5%)
  other arithmetic  2.2 us (1%)
    all_to_all x1, blocking collectives, local(): lax.all_to_all(local_buffer, ('dp', 'sect'), split_axis=0, concat_axis=0,...  49.1 us
    all_gather x1, waiting for transfers between devices, local(): gathered = lax.all_gather(inputs, 'tensor', axis=0, tiled=False)  32.7 us
    all_to_all x1, waiting for transfers between devices, local(): lax.all_to_all(summed.reshape(own_experts, owners, CAP, last).transpose(1...  27.1 us
    all_gather x1, blocking collectives, local(): lax.all_gather(hidden.transpose(0, 2, 1), 'tensor', axis=0, tiled=False)  11.5 us
    all_to_all x1, starting transfers between devices, local(): lax.all_to_all(summed.reshape(own_experts, owners, CAP, last).transpose(1...  10.4 us
    all_to_all x1, starting transfers between devices, local(): lax.all_to_all(down_weight.reshape(own_experts, hidden_width, pieces, out...  4.18 us
  transfers between devices with their start and end apart: 3, of which 2 were waited for; matrix products, arithmetic and copies ran while one was open for 7% of the time, Pallas kernels for 0%

profile of v2, /device:TPU:1, one launch (start us, length us, event | category | flops | bytes accessed | tf_op | source)
XLA Modules:
  0.0 171.7 jit_solution(13192428410018928739)
XLA Ops:
  7.2 0.8 copy.29
  8.5 0.7 reduce_sum.58
  9.2 0.7 divide_convert_fusion.2
  10.0 0.5 select_reduce_fusion
  10.5 1.1 convolution_convert_fusion
  11.9 49.1 %all_to_all.15 = bf16[128,5,512]{2,1,0:T(8,128)(2,1)S(1)} all-to-all(bf16[128,5,512]{2,1,0:T(8,128)(2,1)S(1)} %reshape.120), channel_id=1, replica_groups=mesh['dp'=64,'tensor'=4,'sect'=2] {'dp','sect'}, dimensions={0} | all-to-all | bytes 1310720 | tf_op jit(solution)/shard_map/all_to_all | solution.py:70
  61.0 1.1 all_gather_reshape_transpose_reshape.3
  62.1 2.4 %reshape.125 = bf16[1,192,4,512]{3,2,1,0:T(4,128)(2,1)S(1)} reshape(bf16[1,192,2048]{2,1,0:T(8,128)(2,1)} %param.15) | data formatting | bytes 1572864 | tf_op jit(solution)/shard_map/reshape | solution.py:90
  64.5 1.0 copy.34
  65.5 4.2 %all-to-all-start.1 = ((bf16[4,1,192,512]{3,2,1,0:T(8,128)(2,1)}), bf16[4,1,192,512]{3,2,1,0:T(8,128)(2,1)}, u32[]{:S(2)}, u32[]{:S(2)}) async-start(bf16[4,1,192,512]{3,2,1,0:T(8,128)(2,1)} %copy.34), calls=%async_computation.1 | async-start | bytes 1572864 | tf_op jit(solution)/shard_map/all_to_all | solution.py:89
  69.7 0.6 reshape.122
  70.3 0.6 reshape.123
  70.9 32.7 %all-gather.3.cloned.1.call-done = bf16[4,1,640,512]{3,2,1,0:T(8,128)(2,1)} async-done(((bf16[1,1,640,512]{3,2,1,0:T(8,128)(2,1)}), bf16[4,1,640,512]{3,2,1,0:T(8,128)(2,1)}) %all-gather.3.cloned.1.call-update) | async-done | bytes 2621456 | tf_op jit(solution)/shard_map/all_gather | solution.py:79
  103.7 2.9 %fusion.5 = f32[640,192]{0,1:T(8,128)S(1)} fusion(bf16[4,1,640,512]{3,2,1,0:T(8,128)(2,1)} %all-gather.3.cloned.1.call-done, bf16[4,512,192]{1,0,2:T(4,128)(2,1)S(1)} %reshape.122), kind=kOutput, calls=%fused_computation.7 | convolution fusion | flops 503316480 | bytes 3899392 | tf_op jit(solution)/shard_map/tend,etdf->enf/dot_general | solution.py:83
  106.5 1.0 fusion.20
  107.5 11.5 %all-gather = bf16[4,192,640]{2,1,0:T(8,128)(2,1)S(1)} all-gather(bf16[1,192,640]{2,1,0:T(8,128)(2,1)S(1)} %fusion.20), channel_id=2, replica_groups=mesh['dp'=64,'tensor'=4,'sect'=2] {'tensor'}, dimensions={0}, use_global_device_ids=true | all-gather | bytes 1228800 | tf_op jit(solution)/shard_map/all_gather | solution.py:96
  119.1 2.1 %convert_reduce_fusion = bf16[640,512]{1,0:T(8,128)(2,1)S(1)} fusion(bf16[4,192,640]{2,1,0:T(8,128)(2,1)S(1)} %all-gather, bf16[4,1,192,512]{3,2,1,0:T(8,128)(2,1)} %all-to-all-done.1), kind=kOutput, calls=%fused_computation.5 | convolution fusion | flops 505610240 | bytes 2424832 | tf_op jit(solution)/shard_map/gefn,gefc->genc/dot_general | solution.py:97
  121.2 1.2 reshape_transpose_reshape.3
  122.5 10.4 %all-to-all-start.2 = ((bf16[128,5,512]{2,1,0:T(8,128)(2,1)}), bf16[128,5,512]{2,1,0:T(8,128)(2,1)S(1)}, u32[]{:S(2)}, u32[]{:S(2)}) async-start(bf16[128,5,512]{2,1,0:T(8,128)(2,1)} %reshape_transpose_reshape.3), calls=%async_computation.2 | async-start | bytes 2097152 | tf_op jit(solution)/shard_map/all_to_all | solution.py:102
  133.0 0.7 fusion.19
  133.9 2.8 %convolution_convert_fusion.1 = bf16[32,16,128]{2,1,0:T(8,128)(2,1)} fusion(bf16[32,128,1,128]{3,1,2,0:T(8,128)(2,1)} %param.18, f32[32,16]{1,0:T(8,128)S(1)} %fusion.34, f32[32,16,128]{2,1,0:T(8,128)S(1)} %fusion.19), kind=kOutput, calls=%fused_computation.16 | convolution fusion | flops 17040000 | bytes 1443840 | tf_op jit(solution)/shard_map/rkgl,rlkd->rkgd/dot_general | solution.py:46
  136.7 27.1 %all-to-all-done.2 = bf16[128,5,512]{2,1,0:T(8,128)(2,1)S(1)} async-done(((bf16[128,5,512]{2,1,0:T(8,128)(2,1)}), bf16[128,5,512]{2,1,0:T(8,128)(2,1)S(1)}, u32[]{:S(2)}, u32[]{:S(2)}) %all-to-all-start.2) | async-done | bytes 655392 | tf_op jit(solution)/shard_map/all_to_all | solution.py:102
  163.8 0.3 reshape.127
  164.1 0.8 convolution_convert_fusion.2
  (24 shorter events, 1.2 us)
Async XLA Ops:
  7.2 125.8 %copy-start = (bf16[32,128,1,128]{3,1,2,0:T(8,128)(2,1)S(1)}, bf16[32,128,1,128]{3,1,2,0:T(8,128)(2,1)}, u32[]{:S(2)}) copy-start(bf16[32,128,1,128]{3,1,2,0:T(8,128)(2,1)} %param.17) | copy-start | bytes 3145732
  7.2 96.5 %all-gather.3.cloned.1.call-start = ((), (), s32[]{:S(2)}) async-start(), calls=%async_computation.3 | async-start | bytes 3276800 | tf_op jit(solution)/shard_map/all_gather | solution.py:79
  62.1 7.6 %copy-start.1 = (bf16[1,2048,192]{1,2,0:T(8,128)(2,1)S(1)}, bf16[1,2048,192]{1,2,0:T(8,128)(2,1)}, u32[]{:S(2)}) copy-start(bf16[1,2048,192]{1,2,0:T(8,128)(2,1)} %param.13) | copy-start | bytes 2359300
  64.5 5.8 %copy-start.2 = (bf16[1,2048,192]{1,2,0:T(8,128)(2,1)S(1)}, bf16[1,2048,192]{1,2,0:T(8,128)(2,1)}, u32[]{:S(2)}) copy-start(bf16[1,2048,192]{1,2,0:T(8,128)(2,1)} %param.14) | copy-start | bytes 2359300
  65.5 53.5 %all-to-all-start.1 = ((bf16[4,1,192,512]{3,2,1,0:T(8,128)(2,1)}), bf16[4,1,192,512]{3,2,1,0:T(8,128)(2,1)}, u32[]{:S(2)}, u32[]{:S(2)}) async-start(bf16[4,1,192,512]{3,2,1,0:T(8,128)(2,1)} %copy.34), calls=%async_computation.1 | async-start | bytes 1572864 | tf_op jit(solution)/shard_map/all_to_all | solution.py:89
  103.7 2.9 %copy-start.5 = (bf16[4,1,640,512]{3,2,1,0:T(8,128)(2,1)S(1)}, bf16[4,1,640,512]{3,2,1,0:T(8,128)(2,1)}, u32[]{:S(2)}) copy-start(bf16[4,1,640,512]{3,2,1,0:T(8,128)(2,1)} %all-gather.3.cloned.1.call-done) | copy-start | bytes 7864324
  121.2 11.7 %copy-start.4 = (s32[32]{0:T(128)S(1)}, s32[32]{0:T(128)}, u32[]{:S(2)}) copy-start(s32[32]{0:T(128)} %param.19) | copy-start | bytes 388
  121.2 11.7 %copy-start.3 = (bf16[32,16,128]{2,1,0:T(8,128)(2,1)S(1)}, bf16[32,16,128]{2,1,0:T(8,128)(2,1)}, u32[]{:S(2)}) copy-start(bf16[32,16,128]{2,1,0:T(8,128)(2,1)} %param.16) | copy-start | bytes 393220
  122.5 41.3 %all-to-all-start.2 = ((bf16[128,5,512]{2,1,0:T(8,128)(2,1)}), bf16[128,5,512]{2,1,0:T(8,128)(2,1)S(1)}, u32[]{:S(2)}, u32[]{:S(2)}) async-start(bf16[128,5,512]{2,1,0:T(8,128)(2,1)} %reshape_transpose_reshape.3), calls=%async_computation.2 | async-start | bytes 2097152 | tf_op jit(solution)/shard_map/all_to_all | solution.py:102
Sparse Core Ops, SparseCore 0:
  62.2 41.3 all-gather.2

commit v3 on v2

--- a/solution.py
+++ b/solution.py
@@ -66,10 +66,11 @@
     local_buffer = jnp.dot(dispatch, tokens, preferred_element_type=jnp.float32).astype(
         jnp.bfloat16
     )
-    local_buffer = local_buffer.reshape(owners, per_owner, local_buffer.shape[1])
+    width = local_buffer.shape[1]
+    lanes = 128
+    local_buffer = local_buffer.reshape(owners, per_owner * width // lanes, lanes)
     arrived = lax.all_to_all(local_buffer, ("dp", "sect"), split_axis=0, concat_axis=0, tiled=True)
     own_experts = gate_weight.shape[0]
-    width = arrived.shape[2]
     pieces = lax.axis_size("tensor")
     inputs = (
         arrived.reshape(owners, own_experts, CAP, width)
@@ -102,13 +103,13 @@
     returned = lax.all_to_all(
         summed.reshape(own_experts, owners, CAP, last)
         .transpose(1, 0, 2, 3)
-        .reshape(owners, own_experts * CAP, last),
+        .reshape(owners, own_experts * CAP * last // lanes, lanes),
         ("dp", "sect"),
         split_axis=0,
         concat_axis=0,
         tiled=True,
     )
-    expert_out = returned.reshape(slot_total, returned.shape[2])
+    expert_out = returned.reshape(slot_total, last)
     mixture = jnp.dot(combine.T, expert_out, preferred_element_type=jnp.float32).astype(
         jnp.bfloat16
     )

time: 172 us -> 162 us (0.942)
  blocking collectives: 60.7 us -> 55.7 us
  waiting for transfers between devices: 59.8 us -> 56.1 us
    all_to_all x1, blocking collectives: 49.1 us -> 44.1 us  [local(): lax.all_to_all(local_buffer, ('dp', 'sect'), split_axis=0, concat_axis=0,...]
    all_to_all x1, waiting for transfers between devices: 27.1 us -> 23.3 us  [local(): lax.all_to_all(summed.reshape(own_experts, owners, CAP, last).transpose(1...]
    reshape x1, local copies, waits for them, and re-layouts: 2.36 us -> 0.57 us  [local(): down_weight.reshape(own_experts, hidden_width, pieces, out_width)]
  transfers between devices with their start and end apart: 3 -> 3, of which waited for: 2 -> 2; matrix products, arithmetic and copies ran while one was open for 7% -> 6% of each run, Pallas kernels for 0% -> 0%
where the time goes in v3:
time: 162 us
  waiting for transfers between devices  56.1 us (35%)
  blocking collectives  55.7 us (34%)
  starting transfers between devices  15.6 us (10%)
  between operations  14.2 us (9%)
  matrix products  10.5 us (6%)
  local copies, waits for them, and re-layouts  7.73 us (5%)
  other arithmetic  2.2 us (1%)
    all_to_all x1, blocking collectives, local(): lax.all_to_all(local_buffer, ('dp', 'sect'), split_axis=0, concat_axis=0,...  44.1 us
    all_gather x1, waiting for transfers between devices, local(): gathered = lax.all_gather(inputs, 'tensor', axis=0, tiled=False)  32.7 us
    all_to_all x1, waiting for transfers between devices, local(): lax.all_to_all(summed.reshape(own_experts, owners, CAP, last).transpose(1...  23.3 us
    all_gather x1, blocking collectives, local(): lax.all_gather(hidden.transpose(0, 2, 1), 'tensor', axis=0, tiled=False)  11.5 us
    all_to_all x1, starting transfers between devices, local(): lax.all_to_all(summed.reshape(own_experts, owners, CAP, last).transpose(1...  11.4 us
    all_to_all x1, starting transfers between devices, local(): lax.all_to_all(down_weight.reshape(own_experts, hidden_width, pieces, out...  4.18 us
  transfers between devices with their start and end apart: 3, of which 2 were waited for; matrix products, arithmetic and copies ran while one was open for 6% of the time, Pallas kernels for 0%

profile of v3, /device:TPU:1, one launch (start us, length us, event | category | flops | bytes accessed | tf_op | source)
XLA Modules:
  0.0 162.0 jit_solution(6486190580156336110)
XLA Ops:
  7.2 0.8 copy.29
  8.5 0.7 reduce_sum.58
  9.2 0.7 divide_convert_fusion.2
  10.5 1.1 convolution_convert_fusion
  11.6 0.5 reshape.120
  12.1 44.1 %all_to_all.15 = bf16[128,20,128]{2,1,0:T(8,128)(2,1)S(1)} all-to-all(bf16[128,20,128]{2,1,0:T(8,128)(2,1)S(1)} %reshape.120), channel_id=1, replica_groups=mesh['dp'=64,'tensor'=4,'sect'=2] {'dp','sect'}, dimensions={0} | all-to-all | bytes 1310720 | tf_op jit(solution)/shard_map/all_to_all | solution.py:72
  56.3 1.4 all_gather_reshape_transpose_reshape.3
  57.7 0.6 reshape.125
  58.3 1.0 copy.34
  59.3 4.2 %all-to-all-start.1 = ((bf16[4,1,192,512]{3,2,1,0:T(8,128)(2,1)}), bf16[4,1,192,512]{3,2,1,0:T(8,128)(2,1)}, u32[]{:S(2)}, u32[]{:S(2)}) async-start(bf16[4,1,192,512]{3,2,1,0:T(8,128)(2,1)} %copy.34), calls=%async_computation.1 | async-start | bytes 1572864 | tf_op jit(solution)/shard_map/all_to_all | solution.py:90
  63.5 0.6 reshape.122
  64.1 0.6 reshape.123
  64.7 32.7 %all-gather.3.cloned.1.call-done = bf16[4,1,640,512]{3,2,1,0:T(8,128)(2,1)} async-done(((bf16[1,1,640,512]{3,2,1,0:T(8,128)(2,1)}), bf16[4,1,640,512]{3,2,1,0:T(8,128)(2,1)}) %all-gather.3.cloned.1.call-update) | async-done | bytes 2621456 | tf_op jit(solution)/shard_map/all_gather | solution.py:80
  97.4 2.9 %fusion.5 = f32[640,192]{0,1:T(8,128)S(1)} fusion(bf16[4,1,640,512]{3,2,1,0:T(8,128)(2,1)} %all-gather.3.cloned.1.call-done, bf16[4,512,192]{1,0,2:T(4,128)(2,1)S(1)} %reshape.122), kind=kOutput, calls=%fused_computation.7 | convolution fusion | flops 503316480 | bytes 3899392 | tf_op jit(solution)/shard_map/tend,etdf->enf/dot_general | solution.py:84
  100.3 1.0 fusion.20
  101.3 11.5 %all-gather = bf16[4,192,640]{2,1,0:T(8,128)(2,1)S(1)} all-gather(bf16[1,192,640]{2,1,0:T(8,128)(2,1)S(1)} %fusion.20), channel_id=2, replica_groups=mesh['dp'=64,'tensor'=4,'sect'=2] {'tensor'}, dimensions={0}, use_global_device_ids=true | all-gather | bytes 1228800 | tf_op jit(solution)/shard_map/all_gather | solution.py:97
  112.8 2.2 %convert_reduce_fusion = bf16[640,512]{1,0:T(8,128)(2,1)S(1)} fusion(bf16[4,192,640]{2,1,0:T(8,128)(2,1)S(1)} %all-gather, bf16[4,1,192,512]{3,2,1,0:T(8,128)(2,1)} %all-to-all-done.1), kind=kOutput, calls=%fused_computation.5 | convolution fusion | flops 505610240 | bytes 2424832 | tf_op jit(solution)/shard_map/gefn,gefc->genc/dot_general | solution.py:98
  115.1 1.4 reshape_transpose_reshape.3
  116.5 11.4 %all-to-all-start.2 = ((bf16[128,20,128]{2,1,0:T(8,128)(2,1)}), bf16[128,20,128]{2,1,0:T(8,128)(2,1)S(1)}, u32[]{:S(2)}, u32[]{:S(2)}) async-start(bf16[128,20,128]{2,1,0:T(8,128)(2,1)} %reshape_transpose_reshape.3), calls=%async_computation.2 | async-start | bytes 1572864 | tf_op jit(solution)/shard_map/all_to_all | solution.py:103
  127.9 0.7 fusion.19
  128.8 1.6 convolution_convert_fusion.1
  130.4 23.3 %all-to-all-done.2 = bf16[128,20,128]{2,1,0:T(8,128)(2,1)S(1)} async-done(((bf16[128,20,128]{2,1,0:T(8,128)(2,1)}), bf16[128,20,128]{2,1,0:T(8,128)(2,1)S(1)}, u32[]{:S(2)}, u32[]{:S(2)}) %all-to-all-start.2) | async-done | bytes 655392 | tf_op jit(solution)/shard_map/all_to_all | solution.py:103
  153.8 0.5 reshape.127
  154.3 0.8 convolution_convert_fusion.2
  (28 shorter events, 1.4 us)
Async XLA Ops:
  7.2 120.8 %copy-start = (bf16[32,128,1,128]{3,1,2,0:T(8,128)(2,1)S(1)}, bf16[32,128,1,128]{3,1,2,0:T(8,128)(2,1)}, u32[]{:S(2)}) copy-start(bf16[32,128,1,128]{3,1,2,0:T(8,128)(2,1)} %param.17) | copy-start | bytes 3145732
  7.2 90.3 %all-gather.3.cloned.1.call-start = ((), (), s32[]{:S(2)}) async-start(), calls=%async_computation.3 | async-start | bytes 3276800 | tf_op jit(solution)/shard_map/all_gather | solution.py:80
  11.6 46.1 %copy-start.1 = (bf16[1,192,2048]{2,1,0:T(8,128)(2,1)S(1)}, bf16[1,192,2048]{2,1,0:T(8,128)(2,1)}, u32[]{:S(2)}) copy-start(bf16[1,192,2048]{2,1,0:T(8,128)(2,1)} %param.15) | copy-start | bytes 2359300
  57.7 5.9 %copy-start.2 = (bf16[1,2048,192]{1,2,0:T(8,128)(2,1)S(1)}, bf16[1,2048,192]{1,2,0:T(8,128)(2,1)}, u32[]{:S(2)}) copy-start(bf16[1,2048,192]{1,2,0:T(8,128)(2,1)} %param.13) | copy-start | bytes 2359300
  58.3 5.8 %copy-start.3 = (bf16[1,2048,192]{1,2,0:T(8,128)(2,1)S(1)}, bf16[1,2048,192]{1,2,0:T(8,128)(2,1)}, u32[]{:S(2)}) copy-start(bf16[1,2048,192]{1,2,0:T(8,128)(2,1)} %param.14) | copy-start | bytes 2359300
  59.3 53.5 %all-to-all-start.1 = ((bf16[4,1,192,512]{3,2,1,0:T(8,128)(2,1)}), bf16[4,1,192,512]{3,2,1,0:T(8,128)(2,1)}, u32[]{:S(2)}, u32[]{:S(2)}) async-start(bf16[4,1,192,512]{3,2,1,0:T(8,128)(2,1)} %copy.34), calls=%async_computation.1 | async-start | bytes 1572864 | tf_op jit(solution)/shard_map/all_to_all | solution.py:90
  97.4 2.9 %copy-start.6 = (bf16[4,1,640,512]{3,2,1,0:T(8,128)(2,1)S(1)}, bf16[4,1,640,512]{3,2,1,0:T(8,128)(2,1)}, u32[]{:S(2)}) copy-start(bf16[4,1,640,512]{3,2,1,0:T(8,128)(2,1)} %all-gather.3.cloned.1.call-done) | copy-start | bytes 7864324
  112.8 15.0 %copy-start.5 = (s32[32]{0:T(128)S(1)}, s32[32]{0:T(128)}, u32[]{:S(2)}) copy-start(s32[32]{0:T(128)} %param.19) | copy-start | bytes 388
  112.8 15.1 %copy-start.4 = (bf16[32,16,128]{2,1,0:T(8,128)(2,1)S(1)}, bf16[32,16,128]{2,1,0:T(8,128)(2,1)}, u32[]{:S(2)}) copy-start(bf16[32,16,128]{2,1,0:T(8,128)(2,1)} %param.16) | copy-start | bytes 393220
  115.0 13.8 %copy-start.7 = (bf16[32,128,1,128]{3,1,2,0:T(8,128)(2,1)S(1)}, bf16[32,128,1,128]{3,1,2,0:T(8,128)(2,1)}, u32[]{:S(2)}) copy-start(bf16[32,128,1,128]{3,1,2,0:T(8,128)(2,1)} %param.18) | copy-start | bytes 3145732
  116.5 37.3 %all-to-all-start.2 = ((bf16[128,20,128]{2,1,0:T(8,128)(2,1)}), bf16[128,20,128]{2,1,0:T(8,128)(2,1)S(1)}, u32[]{:S(2)}, u32[]{:S(2)}) async-start(bf16[128,20,128]{2,1,0:T(8,128)(2,1)} %reshape_transpose_reshape.3), calls=%async_computation.2 | async-start | bytes 1572864 | tf_op jit(solution)/shard_map/all_to_all | solution.py:103
Sparse Core Ops, SparseCore 0:
  57.8 39.5 all-gather.2

commit v4 on v3

--- a/solution.py
+++ b/solution.py
@@ -47,6 +47,37 @@
     return result.astype(jnp.bfloat16).reshape(row_count, head_count, head_size)
 
 
+def shifted(x, step, count):
+    return lax.ppermute(x, "tensor", perm=[(i, (i + step) % count) for i in range(count)])
+
+
+def ring_projections(inputs, gate_weight, up_weight, count):
+    width = inputs.shape[2]
+    if count != 4:
+        gathered = lax.all_gather(inputs, "tensor", axis=2, tiled=True)
+        gate = jnp.einsum("end,edf->enf", gathered, gate_weight, preferred_element_type=jnp.float32)
+        up = jnp.einsum("end,edf->enf", gathered, up_weight, preferred_element_type=jnp.float32)
+        return gate, up
+    me = lax.axis_index("tensor")
+    from_left = shifted(inputs, 1, count)
+    from_right = shifted(inputs, -1, count)
+    half = inputs.shape[1] // 2
+    far = jnp.concatenate(
+        [shifted(from_right[:, :half], -1, count), shifted(from_left[:, half:], 1, count)], axis=1
+    )
+    gate = None
+    up = None
+    for piece, offset in ((inputs, 0), (from_left, count - 1), (from_right, 1), (far, 2)):
+        start = ((me + offset) % count) * width
+        gate_rows = lax.dynamic_slice_in_dim(gate_weight, start, width, axis=1)
+        up_rows = lax.dynamic_slice_in_dim(up_weight, start, width, axis=1)
+        g = jnp.einsum("end,edf->enf", piece, gate_rows, preferred_element_type=jnp.float32)
+        u = jnp.einsum("end,edf->enf", piece, up_rows, preferred_element_type=jnp.float32)
+        gate = g if gate is None else gate + g
+        up = u if up is None else up + u
+    return gate, up
+
+
 def local(
     tokens,
     route_experts,
@@ -77,14 +108,8 @@
         .transpose(1, 0, 2, 3)
         .reshape(own_experts, owners * CAP, width)
     )
-    gathered = lax.all_gather(inputs, "tensor", axis=0, tiled=False)
     hidden_width = gate_weight.shape[2]
-    gate_view = gate_weight.reshape(own_experts, pieces, width, hidden_width)
-    up_view = up_weight.reshape(own_experts, pieces, width, hidden_width)
-    gate_part = jnp.einsum(
-        "tend,etdf->enf", gathered, gate_view, preferred_element_type=jnp.float32
-    )
-    up_part = jnp.einsum("tend,etdf->enf", gathered, up_view, preferred_element_type=jnp.float32)
+    gate_part, up_part = ring_projections(inputs, gate_weight, up_weight, pieces)
     hidden = (jax.nn.silu(gate_part) * up_part).astype(jnp.bfloat16)
     out_width = down_weight.shape[2] // pieces
     down_mine = lax.all_to_all(

time: 162 us -> 147 us (0.907)
  waiting for transfers between devices: 56.1 us -> 36.2 us
  between operations: 14.2 us -> 0.94 us
  starting transfers between devices: 15.6 us -> 28 us
  matrix products: 10.5 us -> 14.1 us
  local copies, waits for them, and re-layouts: 7.73 us -> 9.76 us
    all_gather x1 -> x0, waiting for transfers between devices: 32.7 us -> none  [local(): gathered = lax.all_gather(inputs, 'tensor', axis=0, tiled=False)]
    ppermute x0 -> x4, waiting for transfers between devices: none -> 14 us  [shifted(): lax.ppermute(x, 'tensor', perm=[(i, (i + step) % count) for i in range(co...]
    ppermute x0 -> x4, starting transfers between devices: none -> 13.5 us  [shifted(): lax.ppermute(x, 'tensor', perm=[(i, (i + step) % count) for i in range(co...]
    dot_general x2 -> x8, matrix products: 3.85 us -> 6.23 us  [the longest x4 3.62 us: ring_projections(): jnp.einsum('end,edf->enf', piece, up_rows, preferred_element_type=jnp.flo...]
    reshape x1, local copies, waits for them, and re-layouts: 0.57 us -> 2.29 us  [local(): down_weight.reshape(own_experts, hidden_width, pieces, out_width)]
  transfers between devices with their start and end apart: 3 -> 6, of which waited for: 2 -> 4; matrix products, arithmetic and copies ran while one was open for 6% -> 10% of each run, Pallas kernels for 0% -> 0%
where the time goes in v4:
time: 147 us; the launch traced here: 146 us
  blocking collectives  55 us (37%)
  waiting for transfers between devices  36.2 us (25%)
  starting transfers between devices  28 us (19%)
  matrix products  14.1 us (10%)
  local copies, waits for them, and re-layouts  9.76 us (7%)
  other arithmetic  2.29 us (2%)
    all_to_all x1, blocking collectives, local(): lax.all_to_all(local_buffer, ('dp', 'sect'), split_axis=0, concat_axis=0,...  44.1 us
    all_to_all x1, waiting for transfers between devices, local(): lax.all_to_all(summed.reshape(own_experts, owners, CAP, last).transpose(1...  22.2 us
    ppermute x4, waiting for transfers between devices, shifted(): lax.ppermute(x, 'tensor', perm=[(i, (i + step) % count) for i in range(co...  14 us
    ppermute x4, starting transfers between devices, shifted(): lax.ppermute(x, 'tensor', perm=[(i, (i + step) % count) for i in range(co...  13.5 us
    all_gather x1, blocking collectives, local(): lax.all_gather(hidden.transpose(0, 2, 1), 'tensor', axis=0, tiled=False)  10.9 us
    all_to_all x1, starting transfers between devices, local(): lax.all_to_all(summed.reshape(own_experts, owners, CAP, last).transpose(1...  10.3 us
    all_to_all x1, starting transfers between devices, local(): lax.all_to_all(down_weight.reshape(own_experts, hidden_width, pieces, out...  4.19 us
    dot_general x4, matrix products, ring_projections(): jnp.einsum('end,edf->enf', piece, up_rows, preferred_element_type=jnp.flo...  3.62 us
  transfers between devices with their start and end apart: 6, of which 4 were waited for; matrix products, arithmetic and copies ran while one was open for 10% of the time, Pallas kernels for 0%

profile of v4, /device:TPU:1, one launch (start us, length us, event | category | flops | bytes accessed | tf_op | source)
XLA Modules:
  0.0 146.3 jit_solution(12235351790193191290)
XLA Ops:
  3.9 1.1 convolution_convert_fusion
  5.6 44.1 %all_to_all.15 = bf16[128,20,128]{2,1,0:T(8,128)(2,1)S(1)} all-to-all(bf16[128,20,128]{2,1,0:T(8,128)(2,1)S(1)} %reshape.160), channel_id=1, replica_groups=mesh['dp'=64,'tensor'=4,'sect'=2] {'dp','sect'}, dimensions={0} | all-to-all | bytes 1310720 | tf_op jit(solution)/shard_map/all_to_all | solution.py:103
  49.7 1.4 reshape_transpose_reshape.6
  51.1 4.4 %collective-permute-start.1 = (bf16[1,640,512]{2,1,0:T(8,128)(2,1)}, bf16[1,640,512]{2,1,0:T(8,128)(2,1)}, u32[]{:S(2)}, u32[]{:S(2)}) collective-permute-start(bf16[1,640,512]{2,1,0:T(8,128)(2,1)} %reshape_transpose_reshape.6), channel_id=1, source_target_pairs={{0,6},{2,0},{4,2},{6,4},{1,7},{3,1},{5,3},{7,5},{8,14},{10,8},{12,... | collective-permute-start | bytes 1966088 | tf_op jit(solution)/shard_map/ppermute | solution.py:51
  55.5 1.9 %collective-permute-start = (bf16[1,640,512]{2,1,0:T(8,128)(2,1)}, bf16[1,640,512]{2,1,0:T(8,128)(2,1)S(1)}, u32[]{:S(2)}, u32[]{:S(2)}) collective-permute-start(bf16[1,640,512]{2,1,0:T(8,128)(2,1)} %reshape_transpose_reshape.6), channel_id=1, source_target_pairs={{0,2},{2,4},{4,6},{6,0},{1,3},{3,5},{5,7},{7,1},{8,10},{10,12},{12... | collective-permute-start | bytes 1966088 | tf_op jit(solution)/shard_map/ppermute | solution.py:51
  57.4 2.3 %reshape.174 = bf16[1,192,4,512]{3,2,1,0:T(4,128)(2,1)S(1)} reshape(bf16[1,192,2048]{2,1,0:T(8,128)(2,1)} %param.15) | data formatting | bytes 1572864 | tf_op jit(solution)/shard_map/reshape | solution.py:116
  59.7 1.0 copy.25
  60.7 4.2 %all-to-all-start.1 = ((bf16[4,1,192,512]{3,2,1,0:T(8,128)(2,1)}), bf16[4,1,192,512]{3,2,1,0:T(8,128)(2,1)}, u32[]{:S(2)}, u32[]{:S(2)}) async-start(bf16[4,1,192,512]{3,2,1,0:T(8,128)(2,1)} %copy.25), calls=%async_computation.1 | async-start | bytes 1572864 | tf_op jit(solution)/shard_map/all_to_all | solution.py:115
  65.5 1.4 fusion.22
  67.3 2.7 %collective-permute-done.1 = bf16[1,640,512]{2,1,0:T(8,128)(2,1)} collective-permute-done((bf16[1,640,512]{2,1,0:T(8,128)(2,1)}, bf16[1,640,512]{2,1,0:T(8,128)(2,1)}, u32[]{:S(2)}, u32[]{:S(2)}) %collective-permute-start.1) | collective-permute-done | bytes 655392 | tf_op jit(solution)/shard_map/ppermute | solution.py:51
  70.0 1.0 slice.8
  71.0 5.3 %collective-permute-start.2 = (bf16[1,320,512]{2,1,0:T(8,128)(2,1)S(1)}, bf16[1,320,512]{2,1,0:T(8,128)(2,1)S(1)}, u32[]{:S(2)}, u32[]{:S(2)}) collective-permute-start(bf16[1,320,512]{2,1,0:T(8,128)(2,1)S(1)} %slice.8), channel_id=1, source_target_pairs={{0,6},{2,0},{4,2},{6,4},{1,7},{3,1},{5,3},{7,5},{8,14},{10,8},{12,... | collective-permute-start | bytes 983048 | tf_op jit(solution)/shard_map/ppermute | solution.py:51
  76.4 1.9 %collective-permute-start.3 = (bf16[1,320,512]{2,1,0:T(8,128)(2,1)S(1)}, bf16[1,320,512]{2,1,0:T(8,128)(2,1)S(1)}, u32[]{:S(2)}, u32[]{:S(2)}) collective-permute-start(bf16[1,320,512]{2,1,0:T(8,128)(2,1)S(1)} %slice.9), channel_id=1, source_target_pairs={{0,2},{2,4},{4,6},{6,0},{1,3},{3,5},{5,7},{7,1},{8,10},{10,12},{12... | collective-permute-start | bytes 983048 | tf_op jit(solution)/shard_map/ppermute | solution.py:51
  79.1 6.3 %collective-permute-done.2 = bf16[1,320,512]{2,1,0:T(8,128)(2,1)S(1)} collective-permute-done((bf16[1,320,512]{2,1,0:T(8,128)(2,1)S(1)}, bf16[1,320,512]{2,1,0:T(8,128)(2,1)S(1)}, u32[]{:S(2)}, u32[]{:S(2)}) %collective-permute-start.2) | collective-permute-done | bytes 327712 | tf_op jit(solution)/shard_map/ppermute | solution.py:51
  85.3 5.1 %collective-permute-done.3 = bf16[1,320,512]{2,1,0:T(8,128)(2,1)S(1)} collective-permute-done((bf16[1,320,512]{2,1,0:T(8,128)(2,1)S(1)}, bf16[1,320,512]{2,1,0:T(8,128)(2,1)S(1)}, u32[]{:S(2)}, u32[]{:S(2)}) %collective-permute-start.3) | collective-permute-done | bytes 327712 | tf_op jit(solution)/shard_map/ppermute | solution.py:51
  91.2 1.5 %fusion.3 = f32[640,192]{0,1:T(8,128)S(1)} fusion(f32[640,192]{0,1:T(8,128)S(1)} %fusion.18, f32[640,192]{0,1:T(8,128)S(1)} %convolution_add_fusion.3, bf16[1,640,512]{2,1,0:T(8,128)(2,1)} %collective-permute-done.1, bf16[1,2048,192]{1,2,0:T(8,128)(2,1)S(1)} %copy-done.1, s32[]{:T(128)S(6)} %select_n.45), kind=kOutput, calls=%fused_computation.8 | convolution fusion | flops 126074880 | bytes 2326532 | tf_op jit(solution)/shard_map/end,edf->enf/dot_general | solution.py:74
  92.7 1.5 %fusion.8 = bf16[1,192,640]{2,1,0:T(8,128)(2,1)S(1)} fusion(f32[640,192]{0,1:T(8,128)S(1)} %fusion.17, f32[640,192]{0,1:T(8,128)S(1)} %convolution_add_fusion.1, bf16[1,640,512]{2,1,0:T(8,128)(2,1)} %collective-permute-done.1, f32[640,192]{0,1:T(8,128)S(1)} %fusion.3, bf16[1,2048,192]{1,2,0:T(8,128)(2,1)S(1)} %copy-done.2, s32[]{:T(128)S(6)} %select_n.45), kind=kOutput, calls=%fused_computation.15 | convolution fusion | flops 126812160 | bytes 2572292 | tf_op jit(solution)/shard_map/end,edf->enf/dot_general | solution.py:75
  94.2 10.9 %all-gather = bf16[4,192,640]{2,1,0:T(8,128)(2,1)S(1)} all-gather(bf16[1,192,640]{2,1,0:T(8,128)(2,1)S(1)} %fusion.8), channel_id=2, replica_groups=mesh['dp'=64,'tensor'=4,'sect'=2] {'tensor'}, dimensions={0}, use_global_device_ids=true | all-gather | bytes 1228800 | tf_op jit(solution)/shard_map/all_gather | solution.py:122
  105.0 2.1 %convert_reduce_fusion = bf16[640,512]{1,0:T(8,128)(2,1)S(1)} fusion(bf16[4,192,640]{2,1,0:T(8,128)(2,1)S(1)} %all-gather, bf16[4,1,192,512]{3,2,1,0:T(8,128)(2,1)} %all-to-all-done.1), kind=kOutput, calls=%fused_computation.1 | convolution fusion | flops 505610240 | bytes 2424832 | tf_op jit(solution)/shard_map/gefn,gefc->genc/dot_general | solution.py:123
  107.2 1.4 reshape_transpose_reshape.7
  108.6 10.3 %all-to-all-start.2 = ((bf16[128,20,128]{2,1,0:T(8,128)(2,1)}), bf16[128,20,128]{2,1,0:T(8,128)(2,1)S(1)}, u32[]{:S(2)}, u32[]{:S(2)}) async-start(bf16[128,20,128]{2,1,0:T(8,128)(2,1)} %reshape_transpose_reshape.7), calls=%async_computation.2 | async-start | bytes 1572864 | tf_op jit(solution)/shard_map/all_to_all | solution.py:128
  119.9 2.8 %convolution_convert_fusion.1 = bf16[32,16,128]{2,1,0:T(8,128)(2,1)} fusion(bf16[32,128,1,128]{3,1,2,0:T(8,128)(2,1)} %param.18, f32[32,16]{1,0:T(8,128)S(1)} %fusion.52, f32[32,16,128]{2,1,0:T(8,128)S(1)} %fusion.7), kind=kOutput, calls=%fused_computation.16 | convolution fusion | flops 17040000 | bytes 1443840 | tf_op jit(solution)/shard_map/rkgl,rlkd->rkgd/dot_general | solution.py:46
  122.7 22.2 %all-to-all-done.2 = bf16[128,20,128]{2,1,0:T(8,128)(2,1)S(1)} async-done(((bf16[128,20,128]{2,1,0:T(8,128)(2,1)}), bf16[128,20,128]{2,1,0:T(8,128)(2,1)S(1)}, u32[]{:S(2)}, u32[]{:S(2)}) %all-to-all-start.2) | async-done | bytes 655392 | tf_op jit(solution)/shard_map/all_to_all | solution.py:128
  145.5 0.8 convolution_convert_fusion.2
  (34 shorter events, 7.7 us)
Async XLA Ops:
  0.6 118.4 %copy-start = (bf16[32,128,1,128]{3,1,2,0:T(8,128)(2,1)S(1)}, bf16[32,128,1,128]{3,1,2,0:T(8,128)(2,1)}, u32[]{:S(2)}) copy-start(bf16[32,128,1,128]{3,1,2,0:T(8,128)(2,1)} %param.17) | copy-start | bytes 3145732
  51.1 18.9 %collective-permute-start.1 = (bf16[1,640,512]{2,1,0:T(8,128)(2,1)}, bf16[1,640,512]{2,1,0:T(8,128)(2,1)}, u32[]{:S(2)}, u32[]{:S(2)}) collective-permute-start(bf16[1,640,512]{2,1,0:T(8,128)(2,1)} %reshape_transpose_reshape.6), channel_id=1, source_target_pairs={{0,6},{2,0},{4,2},{6,4},{1,7},{3,1},{5,3},{7,5},{8,14},{10,8},{12,... | collective-permute-start | bytes 1966088 | tf_op jit(solution)/shard_map/ppermute | solution.py:51
  55.5 20.9 %collective-permute-start = (bf16[1,640,512]{2,1,0:T(8,128)(2,1)}, bf16[1,640,512]{2,1,0:T(8,128)(2,1)S(1)}, u32[]{:S(2)}, u32[]{:S(2)}) collective-permute-start(bf16[1,640,512]{2,1,0:T(8,128)(2,1)} %reshape_transpose_reshape.6), channel_id=1, source_target_pairs={{0,2},{2,4},{4,6},{6,0},{1,3},{3,5},{5,7},{7,1},{8,10},{10,12},{12... | collective-permute-start | bytes 1966088 | tf_op jit(solution)/shard_map/ppermute | solution.py:51
  60.7 44.3 %all-to-all-start.1 = ((bf16[4,1,192,512]{3,2,1,0:T(8,128)(2,1)}), bf16[4,1,192,512]{3,2,1,0:T(8,128)(2,1)}, u32[]{:S(2)}, u32[]{:S(2)}) async-start(bf16[4,1,192,512]{3,2,1,0:T(8,128)(2,1)} %copy.25), calls=%async_computation.1 | async-start | bytes 1572864 | tf_op jit(solution)/shard_map/all_to_all | solution.py:115
  65.5 1.4 copy-start.1
  66.9 11.4 %copy-start.2 = (bf16[1,2048,192]{1,2,0:T(8,128)(2,1)S(1)}, bf16[1,2048,192]{1,2,0:T(8,128)(2,1)}, u32[]{:S(2)}) copy-start(bf16[1,2048,192]{1,2,0:T(8,128)(2,1)} %param.14) | copy-start | bytes 2359300
  71.0 14.3 %collective-permute-start.2 = (bf16[1,320,512]{2,1,0:T(8,128)(2,1)S(1)}, bf16[1,320,512]{2,1,0:T(8,128)(2,1)S(1)}, u32[]{:S(2)}, u32[]{:S(2)}) collective-permute-start(bf16[1,320,512]{2,1,0:T(8,128)(2,1)S(1)} %slice.8), channel_id=1, source_target_pairs={{0,6},{2,0},{4,2},{6,4},{1,7},{3,1},{5,3},{7,5},{8,14},{10,8},{12,... | collective-permute-start | bytes 983048 | tf_op jit(solution)/shard_map/ppermute | solution.py:51
  76.4 14.1 %collective-permute-start.3 = (bf16[1,320,512]{2,1,0:T(8,128)(2,1)S(1)}, bf16[1,320,512]{2,1,0:T(8,128)(2,1)S(1)}, u32[]{:S(2)}, u32[]{:S(2)}) collective-permute-start(bf16[1,320,512]{2,1,0:T(8,128)(2,1)S(1)} %slice.9), channel_id=1, source_target_pairs={{0,2},{2,4},{4,6},{6,0},{1,3},{3,5},{5,7},{7,1},{8,10},{10,12},{12... | collective-permute-start | bytes 983048 | tf_op jit(solution)/shard_map/ppermute | solution.py:51
  108.6 10.3 %copy-start.4 = (s32[32]{0:T(128)S(1)}, s32[32]{0:T(128)}, u32[]{:S(2)}) copy-start(s32[32]{0:T(128)} %param.19) | copy-start | bytes 388
  108.6 10.4 %copy-start.3 = (bf16[32,16,128]{2,1,0:T(8,128)(2,1)S(1)}, bf16[32,16,128]{2,1,0:T(8,128)(2,1)}, u32[]{:S(2)}) copy-start(bf16[32,16,128]{2,1,0:T(8,128)(2,1)} %param.16) | copy-start | bytes 393220
  108.6 36.4 %all-to-all-start.2 = ((bf16[128,20,128]{2,1,0:T(8,128)(2,1)}), bf16[128,20,128]{2,1,0:T(8,128)(2,1)S(1)}, u32[]{:S(2)}, u32[]{:S(2)}) async-start(bf16[128,20,128]{2,1,0:T(8,128)(2,1)} %reshape_transpose_reshape.7), calls=%async_computation.2 | async-start | bytes 1572864 | tf_op jit(solution)/shard_map/all_to_all | solution.py:128

commit v5 on v4

--- a/solution.py
+++ b/solution.py
@@ -76,6 +76,52 @@
         gate = g if gate is None else gate + g
         up = u if up is None else up + u
     return gate, up
+
+
+def split_down(down_weight, count):
+    width = down_weight.shape[2] // count
+    if count != 4:
+        return lax.all_to_all(
+            down_weight.reshape(down_weight.shape[0], down_weight.shape[1], count, width)
+            .transpose(2, 0, 1, 3),
+            "tensor",
+            split_axis=0,
+            concat_axis=0,
+            tiled=True,
+        )
+    me = lax.axis_index("tensor")
+
+    def columns(offset):
+        start = ((me + offset) % count) * width
+        return lax.dynamic_slice_in_dim(down_weight, start, width, axis=2)
+
+    return (
+        columns(0),
+        shifted(columns(1), 1, count),
+        shifted(columns(count - 1), -1, count),
+        shifted(columns(2), 2, count),
+    )
+
+
+def down_projection(hidden_t, down_pieces, count):
+    if count != 4:
+        hidden_all = lax.all_gather(hidden_t, "tensor", axis=0, tiled=False)
+        group_sums = jnp.einsum(
+            "gefn,gefc->genc", hidden_all, down_pieces, preferred_element_type=jnp.float32
+        ).astype(jnp.bfloat16)
+        return jnp.sum(group_sums.astype(jnp.float32), axis=0).astype(jnp.bfloat16)
+    from_left = shifted(hidden_t, 1, count)
+    from_right = shifted(hidden_t, -1, count)
+    half = hidden_t.shape[1] // 2
+    far = jnp.concatenate(
+        [shifted(from_right[:, :half], -1, count), shifted(from_left[:, half:], 1, count)], axis=1
+    )
+    total = None
+    for piece, weight in zip((hidden_t, from_left, from_right, far), down_pieces):
+        group = jnp.einsum("efn,efc->enc", piece, weight, preferred_element_type=jnp.float32)
+        group = group.astype(jnp.bfloat16).astype(jnp.float32)
+        total = group if total is None else total + group
+    return total.astype(jnp.bfloat16)
 
 
 def local(
@@ -100,9 +146,11 @@
     width = local_buffer.shape[1]
     lanes = 128
     local_buffer = local_buffer.reshape(owners, per_owner * width // lanes, lanes)
+    pieces = lax.axis_size("tensor")
+    down_pieces = split_down(down_weight, pieces)
     arrived = lax.all_to_all(local_buffer, ("dp", "sect"), split_axis=0, concat_axis=0, tiled=True)
+    arrived, down_pieces = lax.optimization_barrier((arrived, down_pieces))
     own_experts = gate_weight.shape[0]
-    pieces = lax.axis_size("tensor")
     inputs = (
         arrived.reshape(owners, own_experts, CAP, width)
         .transpose(1, 0, 2, 3)
@@ -111,19 +159,7 @@
     hidden_width = gate_weight.shape[2]
     gate_part, up_part = ring_projections(inputs, gate_weight, up_weight, pieces)
     hidden = (jax.nn.silu(gate_part) * up_part).astype(jnp.bfloat16)
-    out_width = down_weight.shape[2] // pieces
-    down_mine = lax.all_to_all(
-        down_weight.reshape(own_experts, hidden_width, pieces, out_width).transpose(2, 0, 1, 3),
-        "tensor",
-        split_axis=0,
-        concat_axis=0,
-        tiled=True,
-    )
-    hidden_all = lax.all_gather(hidden.transpose(0, 2, 1), "tensor", axis=0, tiled=False)
-    group_sums = jnp.einsum(
-        "gefn,gefc->genc", hidden_all, down_mine, preferred_element_type=jnp.float32
-    ).astype(jnp.bfloat16)
-    summed = jnp.sum(group_sums.astype(jnp.float32), axis=0).astype(jnp.bfloat16)
+    summed = down_projection(hidden.transpose(0, 2, 1), down_pieces, pieces)
     last = summed.shape[2]
     returned = lax.all_to_all(
         summed.reshape(own_experts, owners, CAP, last)

time: 147 us -> 150 us (1.020)
  blocking collectives: 55 us -> 0 us
  starting transfers between devices: 28 us -> 64.4 us
  waiting for transfers between devices: 36.2 us -> 61.1 us
  local copies, waits for them, and re-layouts: 9.76 us -> 7.51 us
  matrix products: 14.1 us -> 12.4 us
    all_to_all x1 -> x0, blocking collectives: 44.1 us -> none  [local(): lax.all_to_all(local_buffer, ('dp', 'sect'), split_axis=0, concat_axis=0,...]
    ppermute x4 -> x11, starting transfers between devices: 13.5 us -> 36.9 us  [shifted(): lax.ppermute(x, 'tensor', perm=[(i, (i + step) % count) for i in range(co...]
    all_to_all x1, starting transfers between devices: 4.19 us -> 18.4 us  [local(): lax.all_to_all(local_buffer, ('dp', 'sect'), split_axis=0, concat_axis=0,...]
    ppermute x4 -> x11, waiting for transfers between devices: 14 us -> 28 us  [shifted(): lax.ppermute(x, 'tensor', perm=[(i, (i + step) % count) for i in range(co...]
    all_to_all x1, waiting for transfers between devices: 0.01 us -> 10.9 us  [local(): lax.all_to_all(local_buffer, ('dp', 'sect'), split_axis=0, concat_axis=0,...]
    all_gather x1 -> x0, blocking collectives: 10.9 us -> none  [local(): lax.all_gather(hidden.transpose(0, 2, 1), 'tensor', axis=0, tiled=False)]
    reshape x2 -> x1, local copies, waits for them, and re-layouts: 2.82 us -> 0.52 us  [the longest x1 2.29 us: local(): down_weight.reshape(own_experts, hidden_width, pieces, out_width)]
  transfers between devices with their start and end apart: 6 -> 13, of which waited for: 4 -> 9; matrix products, arithmetic and copies ran while one was open for 10% -> 5% of each run, Pallas kernels for 0% -> 0%
where the time goes in v5:
time: 150 us; the launch traced here: 149 us
  starting transfers between devices  64.4 us (43%)
  waiting for transfers between devices  61.1 us (41%)
  matrix products  12.4 us (8%)
  local copies, waits for them, and re-layouts  7.51 us (5%)
  other arithmetic  2.82 us (2%)
    ppermute x11, starting transfers between devices, shifted(): lax.ppermute(x, 'tensor', perm=[(i, (i + step) % count) for i in range(co...  36.9 us
    ppermute x11, waiting for transfers between devices, shifted(): lax.ppermute(x, 'tensor', perm=[(i, (i + step) % count) for i in range(co...  28 us
    all_to_all x1, waiting for transfers between devices, local(): lax.all_to_all(summed.reshape(own_experts, owners, CAP, last).transpose(1...  22.2 us
    all_to_all x1, starting transfers between devices, local(): lax.all_to_all(local_buffer, ('dp', 'sect'), split_axis=0, concat_axis=0,...  18.4 us
    all_to_all x1, waiting for transfers between devices, local(): lax.all_to_all(local_buffer, ('dp', 'sect'), split_axis=0, concat_axis=0,...  10.9 us
    all_to_all x1, starting transfers between devices, local(): lax.all_to_all(summed.reshape(own_experts, owners, CAP, last).transpose(1...  9.15 us
  transfers between devices with their start and end apart: 13, of which 9 were waited for; matrix products, arithmetic and copies ran while one was open for 5% of the time, Pallas kernels for 0%

profile of v5, /device:TPU:1, one launch (start us, length us, event | category | flops | bytes accessed | tf_op | source)
XLA Modules:
  0.0 149.3 jit_solution(6795999751461185472)
XLA Ops:
  7.0 18.4 %all-to-all-start = ((bf16[128,20,128]{2,1,0:T(8,128)(2,1)}), bf16[128,20,128]{2,1,0:T(8,128)(2,1)S(1)}, u32[]{:S(2)}, u32[]{:S(2)}) async-start(bf16[128,20,128]{2,1,0:T(8,128)(2,1)} %reshape.187), calls=%async_computation | async-start | bytes 1572864 | tf_op jit(solution)/shard_map/all_to_all | solution.py:151
  25.6 3.1 %collective-permute-start = (bf16[1,192,512]{2,1,0:T(8,128)(2,1)S(1)}, bf16[1,192,512]{2,1,0:T(8,128)(2,1)S(1)}, u32[]{:S(2)}, u32[]{:S(2)}) collective-permute-start(bf16[1,192,512]{2,1,0:T(8,128)(2,1)S(1)} %get-tuple-element.15), channel_id=1, source_target_pairs={{0,2},{2,4},{4,6},{6,0},{1,3},{3,5},{5,7},{7,1},{8,10},{10,12},{12... | collective-permute-start | bytes 589832 | tf_op jit(solution)/shard_map/ppermute | solution.py:51
  28.8 3.4 %collective-permute-start.1 = (bf16[1,192,512]{2,1,0:T(8,128)(2,1)S(1)}, bf16[1,192,512]{2,1,0:T(8,128)(2,1)S(1)}, u32[]{:S(2)}, u32[]{:S(2)}) collective-permute-start(bf16[1,192,512]{2,1,0:T(8,128)(2,1)S(1)} %get-tuple-element.17), channel_id=1, source_target_pairs={{0,6},{2,0},{4,2},{6,4},{1,7},{3,1},{5,3},{7,5},{8,14},{10,8},{12,... | collective-permute-start | bytes 589832 | tf_op jit(solution)/shard_map/ppermute | solution.py:51
  32.1 3.4 %collective-permute-start.2 = (bf16[1,192,512]{2,1,0:T(8,128)(2,1)S(1)}, bf16[1,192,512]{2,1,0:T(8,128)(2,1)S(1)}, u32[]{:S(2)}, u32[]{:S(2)}) collective-permute-start(bf16[1,192,512]{2,1,0:T(8,128)(2,1)S(1)} %get-tuple-element.14), channel_id=1, source_target_pairs={{0,4},{2,6},{4,0},{6,2},{1,5},{3,7},{5,1},{7,3},{8,12},{10,14},{12... | collective-permute-start | bytes 589832 | tf_op jit(solution)/shard_map/ppermute | solution.py:51
  35.9 4.6 %collective-permute-done.2 = bf16[1,192,512]{2,1,0:T(8,128)(2,1)S(1)} collective-permute-done((bf16[1,192,512]{2,1,0:T(8,128)(2,1)S(1)}, bf16[1,192,512]{2,1,0:T(8,128)(2,1)S(1)}, u32[]{:S(2)}, u32[]{:S(2)}) %collective-permute-start.2) | collective-permute-done | bytes 196640 | tf_op jit(solution)/shard_map/ppermute | solution.py:51
  40.5 10.9 %all-to-all-done = bf16[128,20,128]{2,1,0:T(8,128)(2,1)S(1)} async-done(((bf16[128,20,128]{2,1,0:T(8,128)(2,1)}), bf16[128,20,128]{2,1,0:T(8,128)(2,1)S(1)}, u32[]{:S(2)}, u32[]{:S(2)}) %all-to-all-start) | async-done | bytes 655392 | tf_op jit(solution)/shard_map/all_to_all | solution.py:151
  52.8 4.4 %collective-permute-start.4 = (bf16[1,640,512]{2,1,0:T(8,128)(2,1)}, bf16[1,640,512]{2,1,0:T(8,128)(2,1)}, u32[]{:S(2)}, u32[]{:S(2)}) collective-permute-start(bf16[1,640,512]{2,1,0:T(8,128)(2,1)} %reshape_transpose_reshape.6), channel_id=1, source_target_pairs={{0,6},{2,0},{4,2},{6,4},{1,7},{3,1},{5,3},{7,5},{8,14},{10,8},{12,... | collective-permute-start | bytes 1966088 | tf_op jit(solution)/shard_map/ppermute | solution.py:51
  57.2 1.9 %collective-permute-start.3 = (bf16[1,640,512]{2,1,0:T(8,128)(2,1)}, bf16[1,640,512]{2,1,0:T(8,128)(2,1)S(1)}, u32[]{:S(2)}, u32[]{:S(2)}) collective-permute-start(bf16[1,640,512]{2,1,0:T(8,128)(2,1)} %reshape_transpose_reshape.6), channel_id=1, source_target_pairs={{0,2},{2,4},{4,6},{6,0},{1,3},{3,5},{5,7},{7,1},{8,10},{10,12},{12... | collective-permute-start | bytes 1966088 | tf_op jit(solution)/shard_map/ppermute | solution.py:51
  59.6 12.0 %collective-permute-done.4 = bf16[1,640,512]{2,1,0:T(8,128)(2,1)} collective-permute-done((bf16[1,640,512]{2,1,0:T(8,128)(2,1)}, bf16[1,640,512]{2,1,0:T(8,128)(2,1)}, u32[]{:S(2)}, u32[]{:S(2)}) %collective-permute-start.4) | collective-permute-done | bytes 655392 | tf_op jit(solution)/shard_map/ppermute | solution.py:51
  72.7 5.3 %collective-permute-start.5 = (bf16[1,320,512]{2,1,0:T(8,128)(2,1)S(1)}, bf16[1,320,512]{2,1,0:T(8,128)(2,1)S(1)}, u32[]{:S(2)}, u32[]{:S(2)}) collective-permute-start(bf16[1,320,512]{2,1,0:T(8,128)(2,1)S(1)} %slice.16), channel_id=1, source_target_pairs={{0,6},{2,0},{4,2},{6,4},{1,7},{3,1},{5,3},{7,5},{8,14},{10,8},{12,... | collective-permute-start | bytes 983048 | tf_op jit(solution)/shard_map/ppermute | solution.py:51
  78.1 2.1 %collective-permute-start.6 = (bf16[1,320,512]{2,1,0:T(8,128)(2,1)S(1)}, bf16[1,320,512]{2,1,0:T(8,128)(2,1)S(1)}, u32[]{:S(2)}, u32[]{:S(2)}) collective-permute-start(bf16[1,320,512]{2,1,0:T(8,128)(2,1)S(1)} %slice.17), channel_id=1, source_target_pairs={{0,2},{2,4},{4,6},{6,0},{1,3},{3,5},{5,7},{7,1},{8,10},{10,12},{12... | collective-permute-start | bytes 983048 | tf_op jit(solution)/shard_map/ppermute | solution.py:51
  81.7 2.6 %collective-permute-done.5 = bf16[1,320,512]{2,1,0:T(8,128)(2,1)S(1)} collective-permute-done((bf16[1,320,512]{2,1,0:T(8,128)(2,1)S(1)}, bf16[1,320,512]{2,1,0:T(8,128)(2,1)S(1)}, u32[]{:S(2)}, u32[]{:S(2)}) %collective-permute-start.5) | collective-permute-done | bytes 327712 | tf_op jit(solution)/shard_map/ppermute | solution.py:51
  84.3 5.2 %collective-permute-done.6 = bf16[1,320,512]{2,1,0:T(8,128)(2,1)S(1)} collective-permute-done((bf16[1,320,512]{2,1,0:T(8,128)(2,1)S(1)}, bf16[1,320,512]{2,1,0:T(8,128)(2,1)S(1)}, u32[]{:S(2)}, u32[]{:S(2)}) %collective-permute-start.6) | collective-permute-done | bytes 327712 | tf_op jit(solution)/shard_map/ppermute | solution.py:51
  90.3 1.5 fusion.11
  91.8 1.5 %fusion.13 = bf16[640,192]{0,1:T(8,128)(2,1)S(1)} fusion(f32[640,192]{0,1:T(8,128)S(1)} %fusion.25, f32[640,192]{0,1:T(8,128)S(1)} %convolution_add_fusion.1, bf16[1,640,512]{2,1,0:T(8,128)(2,1)} %collective-permute-done.4, f32[640,192]{0,1:T(8,128)S(1)} %fusion.11, bf16[1,2048,192]{1,2,0:T(8,128)(2,1)S(1)} %copy-done.5, s32[]{:T(128)S(6)} %select_n.55), kind=kOutput, calls=%fused_computation.22 | convolution fusion | flops 126812160 | bytes 2572292 | tf_op jit(solution)/shard_map/end,edf->enf/dot_general | solution.py:75
  93.3 2.1 %collective-permute-start.7 = (bf16[1,192,640]{2,1,0:T(8,128)(2,1)S(1)}, bf16[1,192,640]{2,1,0:T(8,128)(2,1)S(1)}, u32[]{:S(2)}, u32[]{:S(2)}) collective-permute-start(bf16[1,192,640]{2,1,0:T(8,128)(2,1)S(1)} %bitcast.78), channel_id=1, source_target_pairs={{0,2},{2,4},{4,6},{6,0},{1,3},{3,5},{5,7},{7,1},{8,10},{10,12},{12... | collective-permute-start | bytes 737288 | tf_op jit(solution)/shard_map/ppermute | solution.py:51
  95.3 4.6 %collective-permute-start.8 = (bf16[1,192,640]{2,1,0:T(8,128)(2,1)S(1)}, bf16[1,192,640]{2,1,0:T(8,128)(2,1)S(1)}, u32[]{:S(2)}, u32[]{:S(2)}) collective-permute-start(bf16[1,192,640]{2,1,0:T(8,128)(2,1)S(1)} %bitcast.79), channel_id=1, source_target_pairs={{0,6},{2,0},{4,2},{6,4},{1,7},{3,1},{5,3},{7,5},{8,14},{10,8},{12,... | collective-permute-start | bytes 737288 | tf_op jit(solution)/shard_map/ppermute | solution.py:51
  100.3 1.8 %collective-permute-done.7 = bf16[1,192,640]{2,1,0:T(8,128)(2,1)S(1)} collective-permute-done((bf16[1,192,640]{2,1,0:T(8,128)(2,1)S(1)}, bf16[1,192,640]{2,1,0:T(8,128)(2,1)S(1)}, u32[]{:S(2)}, u32[]{:S(2)}) %collective-permute-start.7) | collective-permute-done | bytes 245792 | tf_op jit(solution)/shard_map/ppermute | solution.py:51
  102.1 1.9 %collective-permute-start.10 = (bf16[1,96,640]{2,1,0:T(8,128)(2,1)S(1)}, bf16[1,96,640]{2,1,0:T(8,128)(2,1)S(1)}, u32[]{:S(2)}, u32[]{:S(2)}) collective-permute-start(bf16[1,96,640]{2,1,0:T(8,128)(2,1)S(1)} %slice.19), channel_id=1, source_target_pairs={{0,2},{2,4},{4,6},{6,0},{1,3},{3,5},{5,7},{7,1},{8,10},{10,12},{12... | collective-permute-start | bytes 368648 | tf_op jit(solution)/shard_map/ppermute | solution.py:51
  104.0 4.7 %collective-permute-start.9 = (bf16[1,96,640]{2,1,0:T(8,128)(2,1)S(1)}, bf16[1,96,640]{2,1,0:T(8,128)(2,1)S(1)}, u32[]{:S(2)}, u32[]{:S(2)}) collective-permute-start(bf16[1,96,640]{2,1,0:T(8,128)(2,1)S(1)} %slice.18), channel_id=1, source_target_pairs={{0,6},{2,0},{4,2},{6,4},{1,7},{3,1},{5,3},{7,5},{8,14},{10,8},{12,... | collective-permute-start | bytes 368648 | tf_op jit(solution)/shard_map/ppermute | solution.py:51
  109.1 1.5 collective-permute-done.9
  112.8 9.1 %all-to-all-start.1 = ((bf16[128,20,128]{2,1,0:T(8,128)(2,1)}), bf16[128,20,128]{2,1,0:T(8,128)(2,1)S(1)}, u32[]{:S(2)}, u32[]{:S(2)}) async-start(bf16[128,20,128]{2,1,0:T(8,128)(2,1)} %reshape_transpose_reshape.7), calls=%async_computation.1 | async-start | bytes 1572864 | tf_op jit(solution)/shard_map/all_to_all | solution.py:164
  122.9 2.8 %convolution_convert_fusion.5 = bf16[32,16,128]{2,1,0:T(8,128)(2,1)} fusion(bf16[32,128,1,128]{3,1,2,0:T(8,128)(2,1)} %param.18, f32[32,16]{1,0:T(8,128)S(1)} %fusion.67, f32[32,16,128]{2,1,0:T(8,128)S(1)} %fusion.15), kind=kOutput, calls=%fused_computation.26 | convolution fusion | flops 17040000 | bytes 1443840 | tf_op jit(solution)/shard_map/rkgl,rlkd->rkgd/dot_general | solution.py:46
  125.8 22.2 %all-to-all-done.1 = bf16[128,20,128]{2,1,0:T(8,128)(2,1)S(1)} async-done(((bf16[128,20,128]{2,1,0:T(8,128)(2,1)}), bf16[128,20,128]{2,1,0:T(8,128)(2,1)S(1)}, u32[]{:S(2)}, u32[]{:S(2)}) %all-to-all-start.1) | async-done | bytes 655392 | tf_op jit(solution)/shard_map/all_to_all | solution.py:164
  (62 shorter events, 17.2 us)
Async XLA Ops:
  0.6 121.4 %copy-start = (bf16[32,128,1,128]{3,1,2,0:T(8,128)(2,1)S(1)}, bf16[32,128,1,128]{3,1,2,0:T(8,128)(2,1)}, u32[]{:S(2)}) copy-start(bf16[32,128,1,128]{3,1,2,0:T(8,128)(2,1)} %param.17) | copy-start | bytes 3145732
  5.6 19.9 %copy-start.1 = (bf16[1,192,2048]{2,1,0:T(8,128)(2,1)S(1)}, bf16[1,192,2048]{2,1,0:T(8,128)(2,1)}, u32[]{:S(2)}) copy-start(bf16[1,192,2048]{2,1,0:T(8,128)(2,1)} %param.15) | copy-start | bytes 2359300
  7.0 44.3 %all-to-all-start = ((bf16[128,20,128]{2,1,0:T(8,128)(2,1)}), bf16[128,20,128]{2,1,0:T(8,128)(2,1)S(1)}, u32[]{:S(2)}, u32[]{:S(2)}) async-start(bf16[128,20,128]{2,1,0:T(8,128)(2,1)} %reshape.187), calls=%async_computation | async-start | bytes 1572864 | tf_op jit(solution)/shard_map/all_to_all | solution.py:151
  25.6 10.0 %collective-permute-start = (bf16[1,192,512]{2,1,0:T(8,128)(2,1)S(1)}, bf16[1,192,512]{2,1,0:T(8,128)(2,1)S(1)}, u32[]{:S(2)}, u32[]{:S(2)}) collective-permute-start(bf16[1,192,512]{2,1,0:T(8,128)(2,1)S(1)} %get-tuple-element.15), channel_id=1, source_target_pairs={{0,2},{2,4},{4,6},{6,0},{1,3},{3,5},{5,7},{7,1},{8,10},{10,12},{12... | collective-permute-start | bytes 589832 | tf_op jit(solution)/shard_map/ppermute | solution.py:51
  28.8 7.1 %collective-permute-start.1 = (bf16[1,192,512]{2,1,0:T(8,128)(2,1)S(1)}, bf16[1,192,512]{2,1,0:T(8,128)(2,1)S(1)}, u32[]{:S(2)}, u32[]{:S(2)}) collective-permute-start(bf16[1,192,512]{2,1,0:T(8,128)(2,1)S(1)} %get-tuple-element.17), channel_id=1, source_target_pairs={{0,6},{2,0},{4,2},{6,4},{1,7},{3,1},{5,3},{7,5},{8,14},{10,8},{12,... | collective-permute-start | bytes 589832 | tf_op jit(solution)/shard_map/ppermute | solution.py:51
  32.1 8.3 %collective-permute-start.2 = (bf16[1,192,512]{2,1,0:T(8,128)(2,1)S(1)}, bf16[1,192,512]{2,1,0:T(8,128)(2,1)S(1)}, u32[]{:S(2)}, u32[]{:S(2)}) collective-permute-start(bf16[1,192,512]{2,1,0:T(8,128)(2,1)S(1)} %get-tuple-element.14), channel_id=1, source_target_pairs={{0,4},{2,6},{4,0},{6,2},{1,5},{3,7},{5,1},{7,3},{8,12},{10,14},{12... | collective-permute-start | bytes 589832 | tf_op jit(solution)/shard_map/ppermute | solution.py:51
  35.6 21.5 %copy-start.3 = (bf16[1,192,512]{2,1,0:T(8,128)(2,1)}, bf16[1,192,512]{2,1,0:T(8,128)(2,1)S(1)}, u32[]{:S(2)}) copy-start(bf16[1,192,512]{2,1,0:T(8,128)(2,1)S(1)} %collective-permute-done) | copy-start | bytes 589828
  40.5 16.7 %copy-start.6 = (bf16[1,192,512]{2,1,0:T(8,128)(2,1)}, bf16[1,192,512]{2,1,0:T(8,128)(2,1)S(1)}, u32[]{:S(2)}) copy-start(bf16[1,192,512]{2,1,0:T(8,128)(2,1)S(1)} %collective-permute-done.2) | copy-start | bytes 589828
  52.8 18.9 %collective-permute-start.4 = (bf16[1,640,512]{2,1,0:T(8,128)(2,1)}, bf16[1,640,512]{2,1,0:T(8,128)(2,1)}, u32[]{:S(2)}, u32[]{:S(2)}) collective-permute-start(bf16[1,640,512]{2,1,0:T(8,128)(2,1)} %reshape_transpose_reshape.6), channel_id=1, source_target_pairs={{0,6},{2,0},{4,2},{6,4},{1,7},{3,1},{5,3},{7,5},{8,14},{10,8},{12,... | collective-permute-start | bytes 1966088 | tf_op jit(solution)/shard_map/ppermute | solution.py:51
  57.2 20.8 %collective-permute-start.3 = (bf16[1,640,512]{2,1,0:T(8,128)(2,1)}, bf16[1,640,512]{2,1,0:T(8,128)(2,1)S(1)}, u32[]{:S(2)}, u32[]{:S(2)}) collective-permute-start(bf16[1,640,512]{2,1,0:T(8,128)(2,1)} %reshape_transpose_reshape.6), channel_id=1, source_target_pairs={{0,2},{2,4},{4,6},{6,0},{1,3},{3,5},{5,7},{7,1},{8,10},{10,12},{12... | collective-permute-start | bytes 1966088 | tf_op jit(solution)/shard_map/ppermute | solution.py:51
  59.6 20.5 %copy-start.2 = (bf16[1,2048,192]{1,2,0:T(8,128)(2,1)S(1)}, bf16[1,2048,192]{1,2,0:T(8,128)(2,1)}, u32[]{:S(2)}) copy-start(bf16[1,2048,192]{1,2,0:T(8,128)(2,1)} %param.13) | copy-start | bytes 2359300
  72.7 11.6 %collective-permute-start.5 = (bf16[1,320,512]{2,1,0:T(8,128)(2,1)S(1)}, bf16[1,320,512]{2,1,0:T(8,128)(2,1)S(1)}, u32[]{:S(2)}, u32[]{:S(2)}) collective-permute-start(bf16[1,320,512]{2,1,0:T(8,128)(2,1)S(1)} %slice.16), channel_id=1, source_target_pairs={{0,6},{2,0},{4,2},{6,4},{1,7},{3,1},{5,3},{7,5},{8,14},{10,8},{12,... | collective-permute-start | bytes 983048 | tf_op jit(solution)/shard_map/ppermute | solution.py:51
  78.0 2.9 %copy-start.5 = (bf16[1,2048,192]{1,2,0:T(8,128)(2,1)S(1)}, bf16[1,2048,192]{1,2,0:T(8,128)(2,1)}, u32[]{:S(2)}) copy-start(bf16[1,2048,192]{1,2,0:T(8,128)(2,1)} %param.14) | copy-start | bytes 2359300
  78.1 11.5 %collective-permute-start.6 = (bf16[1,320,512]{2,1,0:T(8,128)(2,1)S(1)}, bf16[1,320,512]{2,1,0:T(8,128)(2,1)S(1)}, u32[]{:S(2)}, u32[]{:S(2)}) collective-permute-start(bf16[1,320,512]{2,1,0:T(8,128)(2,1)S(1)} %slice.17), channel_id=1, source_target_pairs={{0,2},{2,4},{4,6},{6,0},{1,3},{3,5},{5,7},{7,1},{8,10},{10,12},{12... | collective-permute-start | bytes 983048 | tf_op jit(solution)/shard_map/ppermute | solution.py:51
  93.3 15.5 %copy-start.4 = (bf16[1,192,512]{2,1,0:T(8,128)(2,1)S(1)}, bf16[1,192,512]{2,1,0:T(8,128)(2,1)}, u32[]{:S(2)}) copy-start(bf16[1,192,512]{2,1,0:T(8,128)(2,1)} %copy-done.3) | copy-start | bytes 589828
  93.3 8.8 %collective-permute-start.7 = (bf16[1,192,640]{2,1,0:T(8,128)(2,1)S(1)}, bf16[1,192,640]{2,1,0:T(8,128)(2,1)S(1)}, u32[]{:S(2)}, u32[]{:S(2)}) collective-permute-start(bf16[1,192,640]{2,1,0:T(8,128)(2,1)S(1)} %bitcast.78), channel_id=1, source_target_pairs={{0,2},{2,4},{4,6},{6,0},{1,3},{3,5},{5,7},{7,1},{8,10},{10,12},{12... | collective-permute-start | bytes 737288 | tf_op jit(solution)/shard_map/ppermute | solution.py:51
  95.3 8.7 %collective-permute-start.8 = (bf16[1,192,640]{2,1,0:T(8,128)(2,1)S(1)}, bf16[1,192,640]{2,1,0:T(8,128)(2,1)S(1)}, u32[]{:S(2)}, u32[]{:S(2)}) collective-permute-start(bf16[1,192,640]{2,1,0:T(8,128)(2,1)S(1)} %bitcast.79), channel_id=1, source_target_pairs={{0,6},{2,0},{4,2},{6,4},{1,7},{3,1},{5,3},{7,5},{8,14},{10,8},{12,... | collective-permute-start | bytes 737288 | tf_op jit(solution)/shard_map/ppermute | solution.py:51
  102.1 7.1 %collective-permute-start.10 = (bf16[1,96,640]{2,1,0:T(8,128)(2,1)S(1)}, bf16[1,96,640]{2,1,0:T(8,128)(2,1)S(1)}, u32[]{:S(2)}, u32[]{:S(2)}) collective-permute-start(bf16[1,96,640]{2,1,0:T(8,128)(2,1)S(1)} %slice.19), channel_id=1, source_target_pairs={{0,2},{2,4},{4,6},{6,0},{1,3},{3,5},{5,7},{7,1},{8,10},{10,12},{12... | collective-permute-start | bytes 368648 | tf_op jit(solution)/shard_map/ppermute | solution.py:51
  104.0 6.6 %copy-start.7 = (bf16[1,192,512]{2,1,0:T(8,128)(2,1)S(1)}, bf16[1,192,512]{2,1,0:T(8,128)(2,1)}, u32[]{:S(2)}) copy-start(bf16[1,192,512]{2,1,0:T(8,128)(2,1)} %copy-done.6) | copy-start | bytes 589828
  104.0 6.6 %collective-permute-start.9 = (bf16[1,96,640]{2,1,0:T(8,128)(2,1)S(1)}, bf16[1,96,640]{2,1,0:T(8,128)(2,1)S(1)}, u32[]{:S(2)}, u32[]{:S(2)}) collective-permute-start(bf16[1,96,640]{2,1,0:T(8,128)(2,1)S(1)} %slice.18), channel_id=1, source_target_pairs={{0,6},{2,0},{4,2},{6,4},{1,7},{3,1},{5,3},{7,5},{8,14},{10,8},{12,... | collective-permute-start | bytes 368648 | tf_op jit(solution)/shard_map/ppermute | solution.py:51
  111.3 10.6 %copy-start.10 = (s32[32]{0:T(128)S(1)}, s32[32]{0:T(128)}, u32[]{:S(2)}) copy-start(s32[32]{0:T(128)} %param.19) | copy-start | bytes 388
  111.4 10.7 %copy-start.9 = (bf16[32,16,128]{2,1,0:T(8,128)(2,1)S(1)}, bf16[32,16,128]{2,1,0:T(8,128)(2,1)}, u32[]{:S(2)}) copy-start(bf16[32,16,128]{2,1,0:T(8,128)(2,1)} %param.16) | copy-start | bytes 393220
  112.8 35.2 %all-to-all-start.1 = ((bf16[128,20,128]{2,1,0:T(8,128)(2,1)}), bf16[128,20,128]{2,1,0:T(8,128)(2,1)S(1)}, u32[]{:S(2)}, u32[]{:S(2)}) async-start(bf16[128,20,128]{2,1,0:T(8,128)(2,1)} %reshape_transpose_reshape.7), calls=%async_computation.1 | async-start | bytes 1572864 | tf_op jit(solution)/shard_map/all_to_all | solution.py:164
  122.9 25.6 %copy-start.8 = (bf16[640,32]{0,1:T(8,128)(2,1)S(1)}, bf16[640,32]{0,1:T(8,128)(2,1)}, u32[]{:S(2)}) copy-start(bf16[640,32]{0,1:T(8,128)(2,1)} %get-tuple-element.12) | copy-start | bytes 122884

commit v6 on v3

--- a/solution.py
+++ b/solution.py
@@ -77,8 +77,18 @@
         .transpose(1, 0, 2, 3)
         .reshape(own_experts, owners * CAP, width)
     )
-    gathered = lax.all_gather(inputs, "tensor", axis=0, tiled=False)
     hidden_width = gate_weight.shape[2]
+    out_width = down_weight.shape[2] // pieces
+    down_split = down_weight.reshape(own_experts, hidden_width, pieces, out_width).transpose(
+        2, 0, 1, 3
+    )
+    outgoing = jnp.concatenate(
+        [jnp.broadcast_to(inputs[None], (pieces,) + inputs.shape), down_split], axis=2
+    )
+    incoming = lax.all_to_all(outgoing, "tensor", split_axis=0, concat_axis=0, tiled=True)
+    slots = inputs.shape[1]
+    gathered = incoming[:, :, :slots]
+    down_mine = incoming[:, :, slots:]
     gate_view = gate_weight.reshape(own_experts, pieces, width, hidden_width)
     up_view = up_weight.reshape(own_experts, pieces, width, hidden_width)
     gate_part = jnp.einsum(
@@ -86,14 +96,6 @@
     )
     up_part = jnp.einsum("tend,etdf->enf", gathered, up_view, preferred_element_type=jnp.float32)
     hidden = (jax.nn.silu(gate_part) * up_part).astype(jnp.bfloat16)
-    out_width = down_weight.shape[2] // pieces
-    down_mine = lax.all_to_all(
-        down_weight.reshape(own_experts, hidden_width, pieces, out_width).transpose(2, 0, 1, 3),
-        "tensor",
-        split_axis=0,
-        concat_axis=0,
-        tiled=True,
-    )
     hidden_all = lax.all_gather(hidden.transpose(0, 2, 1), "tensor", axis=0, tiled=False)
     group_sums = jnp.einsum(
         "gefn,gefc->genc", hidden_all, down_mine, preferred_element_type=jnp.float32

time: 162 us -> 157 us (0.969)
  blocking collectives: 55.7 us -> 11.3 us
  waiting for transfers between devices: 56.1 us -> 88 us
  starting transfers between devices: 15.6 us -> 32.7 us
  between operations: 14.2 us -> 0.82 us
  other arithmetic: 2.2 us -> 4.19 us
    all_to_all x1 -> x2, waiting for transfers between devices: 0.01 us -> 64.7 us  [the longest x1 39.5 us: local(): lax.all_to_all(outgoing, 'tensor', split_axis=0, concat_axis=0, tiled=True)]
    all_to_all x1 -> x0, blocking collectives: 44.1 us -> none  [local(): lax.all_to_all(local_buffer, ('dp', 'sect'), split_axis=0, concat_axis=0,...]
    all_gather x1 -> x0, waiting for transfers between devices: 32.7 us -> none  [local(): gathered = lax.all_gather(inputs, 'tensor', axis=0, tiled=False)]
    all_to_all x1 -> x2, starting transfers between devices: 4.18 us -> 23.2 us  [the longest x1 18.4 us: local(): lax.all_to_all(local_buffer, ('dp', 'sect'), split_axis=0, concat_axis=0,...]
    concatenate x0 -> x1, other arithmetic: none -> 1.98 us  [local(): jnp.concatenate([jnp.broadcast_to(inputs[None], (pieces,) + inputs.shape)...]
    all_to_all x1, starting transfers between devices: 11.4 us -> 9.5 us  [local(): lax.all_to_all(summed.reshape(own_experts, owners, CAP, last).transpose(1...]
    dot_general x1, matrix products: 1 us -> 2.72 us  [local(): jnp.einsum('tend,etdf->enf', gathered, up_view, preferred_element_type=jn...]
  transfers between devices with their start and end apart: 3 -> 3, of which waited for: 2 -> 3; matrix products, arithmetic and copies ran while one was open for 6% -> 3% of each run, Pallas kernels for 0% -> 0%
where the time goes in v6:
time: 157 us; the launch traced here: 156 us
  waiting for transfers between devices  88 us (56%)
  starting transfers between devices  32.7 us (21%)
  matrix products  12.1 us (8%)
  blocking collectives  11.3 us (7%)
  local copies, waits for them, and re-layouts  7.1 us (5%)
  other arithmetic  4.19 us (3%)
    all_to_all x1, waiting for transfers between devices, local(): lax.all_to_all(outgoing, 'tensor', split_axis=0, concat_axis=0, tiled=True)  39.5 us
    all_to_all x1, waiting for transfers between devices, local(): lax.all_to_all(local_buffer, ('dp', 'sect'), split_axis=0, concat_axis=0,...  25.2 us
    all_to_all x1, waiting for transfers between devices, local(): lax.all_to_all(summed.reshape(own_experts, owners, CAP, last).transpose(1...  23.3 us
    all_to_all x1, starting transfers between devices, local(): lax.all_to_all(local_buffer, ('dp', 'sect'), split_axis=0, concat_axis=0,...  18.4 us
    all_gather x1, blocking collectives, local(): lax.all_gather(hidden.transpose(0, 2, 1), 'tensor', axis=0, tiled=False)  11.3 us
    all_to_all x1, starting transfers between devices, local(): lax.all_to_all(summed.reshape(own_experts, owners, CAP, last).transpose(1...  9.5 us
    all_to_all x1, starting transfers between devices, local(): lax.all_to_all(outgoing, 'tensor', split_axis=0, concat_axis=0, tiled=True)  4.82 us
  transfers between devices with their start and end apart: 3, of which 3 were waited for; matrix products, arithmetic and copies ran while one was open for 3% of the time, Pallas kernels for 0%

profile of v6, /device:TPU:1, one launch (start us, length us, event | category | flops | bytes accessed | tf_op | source)
XLA Modules:
  0.0 156.2 jit_solution(16495988532988987569)
XLA Ops:
  0.7 0.9 copy.30
  2.0 0.7 reduce_sum.58
  2.7 0.7 divide_convert_fusion.2
  4.0 1.1 convolution_convert_fusion
  5.1 1.4 reshape.123
  6.5 18.4 %all-to-all-start = ((bf16[128,20,128]{2,1,0:T(8,128)(2,1)}), bf16[128,20,128]{2,1,0:T(8,128)(2,1)S(1)}, u32[]{:S(2)}, u32[]{:S(2)}) async-start(bf16[128,20,128]{2,1,0:T(8,128)(2,1)} %reshape.123), calls=%async_computation | async-start | bytes 1572864 | tf_op jit(solution)/shard_map/all_to_all | solution.py:72
  24.9 0.6 reshape.124
  25.6 25.2 %all-to-all-done = bf16[128,20,128]{2,1,0:T(8,128)(2,1)S(1)} async-done(((bf16[128,20,128]{2,1,0:T(8,128)(2,1)}), bf16[128,20,128]{2,1,0:T(8,128)(2,1)S(1)}, u32[]{:S(2)}, u32[]{:S(2)}) %all-to-all-start) | async-done | bytes 655392 | tf_op jit(solution)/shard_map/all_to_all | solution.py:72
  50.8 0.5 broadcast_in_dim.12
  51.6 2.0 %pad_maximum_fusion = bf16[4,1,832,512]{3,2,1,0:T(8,128)(2,1)} fusion(bf16[4,1,192,512]{3,2,1,0:T(8,128)(2,1)S(1)} %copy.33, bf16[4,1,640,512]{3,2,1,0:T(8,128)(2,1)S(1)} %broadcast_in_dim.13), kind=kLoop, calls=%fused_computation.1 | loop fusion | flops 6815744 | bytes 6815744 | tf_op jit(solution)/shard_map/concatenate | solution.py:85
  53.6 4.8 %all-to-all-start.1 = ((bf16[4,1,832,512]{3,2,1,0:T(8,128)(2,1)}), bf16[4,1,832,512]{3,2,1,0:T(8,128)(2,1)}, u32[]{:S(2)}, u32[]{:S(2)}) async-start(bf16[4,1,832,512]{3,2,1,0:T(8,128)(2,1)} %pad_maximum_fusion), calls=%async_computation.1 | async-start | bytes 6815744 | tf_op jit(solution)/shard_map/all_to_all | solution.py:88
  58.4 0.6 reshape.126
  59.0 0.6 reshape.127
  59.6 39.5 %all-to-all-done.1 = bf16[4,1,832,512]{3,2,1,0:T(8,128)(2,1)} async-done(((bf16[4,1,832,512]{3,2,1,0:T(8,128)(2,1)}), bf16[4,1,832,512]{3,2,1,0:T(8,128)(2,1)}, u32[]{:S(2)}, u32[]{:S(2)}) %all-to-all-start.1) | async-done | bytes 3407904 | tf_op jit(solution)/shard_map/all_to_all | solution.py:88
  99.1 2.7 %fusion.3 = f32[640,192]{0,1:T(8,128)S(1)} fusion(bf16[4,1,832,512]{3,2,0,1:T(8,128)(2,1)} %bitcast.1, bf16[4,512,192]{1,0,2:T(4,128)(2,1)S(1)} %reshape.126), kind=kOutput, calls=%fused_computation.7 | convolution fusion | flops 503316480 | bytes 3899392 | tf_op jit(solution)/shard_map/tend,etdf->enf/dot_general | solution.py:94
  101.8 2.7 %fusion.10 = bf16[1,192,640]{2,1,0:T(8,128)(2,1)S(1)} fusion(bf16[4,1,832,512]{3,2,0,1:T(8,128)(2,1)} %bitcast.1, bf16[4,512,192]{1,0,2:T(4,128)(2,1)S(1)} %reshape.127, f32[640,192]{0,1:T(8,128)S(1)} %fusion.3), kind=kOutput, calls=%fused_computation.15 | convolution fusion | flops 504053760 | bytes 4145152 | tf_op jit(solution)/shard_map/tend,etdf->enf/dot_general | solution.py:97
  104.5 11.3 %all-gather = bf16[4,192,640]{2,1,0:T(8,128)(2,1)S(1)} all-gather(bf16[1,192,640]{2,1,0:T(8,128)(2,1)S(1)} %fusion.10), channel_id=2, replica_groups=mesh['dp'=64,'tensor'=4,'sect'=2] {'tensor'}, dimensions={0}, use_global_device_ids=true | all-gather | bytes 1228800 | tf_op jit(solution)/shard_map/all_gather | solution.py:99
  115.8 2.2 %convert_reduce_fusion = bf16[640,512]{1,0:T(8,128)(2,1)S(1)} fusion(bf16[4,192,640]{2,1,0:T(8,128)(2,1)S(1)} %all-gather, bf16[4,1,832,512]{3,2,0,1:T(8,128)(2,1)} %bitcast.1), kind=kOutput, calls=%fused_computation.3 | convolution fusion | flops 505610240 | bytes 2424832 | tf_op jit(solution)/shard_map/gefn,gefc->genc/dot_general | solution.py:100
  118.0 1.4 reshape_transpose_reshape.3
  119.4 9.5 %all-to-all-start.2 = ((bf16[128,20,128]{2,1,0:T(8,128)(2,1)}), bf16[128,20,128]{2,1,0:T(8,128)(2,1)S(1)}, u32[]{:S(2)}, u32[]{:S(2)}) async-start(bf16[128,20,128]{2,1,0:T(8,128)(2,1)} %reshape_transpose_reshape.3), calls=%async_computation.2 | async-start | bytes 1572864 | tf_op jit(solution)/shard_map/all_to_all | solution.py:105
  129.0 0.7 fusion.9
  129.9 1.6 %convolution_convert_fusion.1 = bf16[32,16,128]{2,1,0:T(8,128)(2,1)} fusion(bf16[32,128,1,128]{3,1,2,0:T(8,128)(2,1)S(1)} %copy-done.6, f32[32,16]{1,0:T(8,128)S(1)} %fusion.21, f32[32,16,128]{2,1,0:T(8,128)S(1)} %fusion.9), kind=kOutput, calls=%fused_computation.16 | convolution fusion | flops 17040000 | bytes 1443840 | tf_op jit(solution)/shard_map/rkgl,rlkd->rkgd/dot_general | solution.py:46
  131.6 23.3 %all-to-all-done.2 = bf16[128,20,128]{2,1,0:T(8,128)(2,1)S(1)} async-done(((bf16[128,20,128]{2,1,0:T(8,128)(2,1)}), bf16[128,20,128]{2,1,0:T(8,128)(2,1)S(1)}, u32[]{:S(2)}, u32[]{:S(2)}) %all-to-all-start.2) | async-done | bytes 655392 | tf_op jit(solution)/shard_map/all_to_all | solution.py:105
  155.4 0.8 convolution_convert_fusion.2
  (26 shorter events, 2.2 us)
Async XLA Ops:
  0.6 128.4 %copy-start = (bf16[32,128,1,128]{3,1,2,0:T(8,128)(2,1)S(1)}, bf16[32,128,1,128]{3,1,2,0:T(8,128)(2,1)}, u32[]{:S(2)}) copy-start(bf16[32,128,1,128]{3,1,2,0:T(8,128)(2,1)} %param.17) | copy-start | bytes 3145732
  0.6 24.3 %copy-start.1 = (bf16[1,192,2048]{2,1,0:T(8,128)(2,1)S(1)}, bf16[1,192,2048]{2,1,0:T(8,128)(2,1)}, u32[]{:S(2)}) copy-start(bf16[1,192,2048]{2,1,0:T(8,128)(2,1)} %param.15) | copy-start | bytes 2359300
  6.5 44.4 %all-to-all-start = ((bf16[128,20,128]{2,1,0:T(8,128)(2,1)}), bf16[128,20,128]{2,1,0:T(8,128)(2,1)S(1)}, u32[]{:S(2)}, u32[]{:S(2)}) async-start(bf16[128,20,128]{2,1,0:T(8,128)(2,1)} %reshape.123), calls=%async_computation | async-start | bytes 1572864 | tf_op jit(solution)/shard_map/all_to_all | solution.py:72
  53.6 4.8 %copy-start.2 = (bf16[1,2048,192]{1,2,0:T(8,128)(2,1)S(1)}, bf16[1,2048,192]{1,2,0:T(8,128)(2,1)}, u32[]{:S(2)}) copy-start(bf16[1,2048,192]{1,2,0:T(8,128)(2,1)} %param.13) | copy-start | bytes 2359300
  53.6 5.4 %copy-start.3 = (bf16[1,2048,192]{1,2,0:T(8,128)(2,1)S(1)}, bf16[1,2048,192]{1,2,0:T(8,128)(2,1)}, u32[]{:S(2)}) copy-start(bf16[1,2048,192]{1,2,0:T(8,128)(2,1)} %param.14) | copy-start | bytes 2359300
  53.6 45.5 %all-to-all-start.1 = ((bf16[4,1,832,512]{3,2,1,0:T(8,128)(2,1)}), bf16[4,1,832,512]{3,2,1,0:T(8,128)(2,1)}, u32[]{:S(2)}, u32[]{:S(2)}) async-start(bf16[4,1,832,512]{3,2,1,0:T(8,128)(2,1)} %pad_maximum_fusion), calls=%async_computation.1 | async-start | bytes 6815744 | tf_op jit(solution)/shard_map/all_to_all | solution.py:88
  115.8 13.2 %copy-start.5 = (s32[32]{0:T(128)S(1)}, s32[32]{0:T(128)}, u32[]{:S(2)}) copy-start(s32[32]{0:T(128)} %param.19) | copy-start | bytes 388
  115.8 13.3 %copy-start.4 = (bf16[32,16,128]{2,1,0:T(8,128)(2,1)S(1)}, bf16[32,16,128]{2,1,0:T(8,128)(2,1)}, u32[]{:S(2)}) copy-start(bf16[32,16,128]{2,1,0:T(8,128)(2,1)} %param.16) | copy-start | bytes 393220
  115.8 14.2 %copy-start.6 = (bf16[32,128,1,128]{3,1,2,0:T(8,128)(2,1)S(1)}, bf16[32,128,1,128]{3,1,2,0:T(8,128)(2,1)}, u32[]{:S(2)}) copy-start(bf16[32,128,1,128]{3,1,2,0:T(8,128)(2,1)} %param.18) | copy-start | bytes 3145732
  119.4 35.4 %all-to-all-start.2 = ((bf16[128,20,128]{2,1,0:T(8,128)(2,1)}), bf16[128,20,128]{2,1,0:T(8,128)(2,1)S(1)}, u32[]{:S(2)}, u32[]{:S(2)}) async-start(bf16[128,20,128]{2,1,0:T(8,128)(2,1)} %reshape_transpose_reshape.3), calls=%async_computation.2 | async-start | bytes 1572864 | tf_op jit(solution)/shard_map/all_to_all | solution.py:105

commit v7 on v4

--- a/solution.py
+++ b/solution.py
@@ -61,10 +61,7 @@
     me = lax.axis_index("tensor")
     from_left = shifted(inputs, 1, count)
     from_right = shifted(inputs, -1, count)
-    half = inputs.shape[1] // 2
-    far = jnp.concatenate(
-        [shifted(from_right[:, :half], -1, count), shifted(from_left[:, half:], 1, count)], axis=1
-    )
+    far = shifted(inputs, 2, count)
     gate = None
     up = None
     for piece, offset in ((inputs, 0), (from_left, count - 1), (from_right, 1), (far, 2)):
@@ -76,6 +73,24 @@
         gate = g if gate is None else gate + g
         up = u if up is None else up + u
     return gate, up
+
+
+def down_projection(hidden_t, down_mine, count):
+    if count != 4:
+        hidden_all = lax.all_gather(hidden_t, "tensor", axis=0, tiled=False)
+        group_sums = jnp.einsum(
+            "gefn,gefc->genc", hidden_all, down_mine, preferred_element_type=jnp.float32
+        ).astype(jnp.bfloat16)
+        return jnp.sum(group_sums.astype(jnp.float32), axis=0).astype(jnp.bfloat16)
+    me = lax.axis_index("tensor")
+    total = None
+    for step, offset in ((0, 0), (1, count - 1), (-1, 1), (2, 2)):
+        piece = hidden_t if step == 0 else shifted(hidden_t, step, count)
+        weight = lax.dynamic_index_in_dim(down_mine, (me + offset) % count, axis=0, keepdims=False)
+        group = jnp.einsum("efn,efc->enc", piece, weight, preferred_element_type=jnp.float32)
+        group = group.astype(jnp.bfloat16).astype(jnp.float32)
+        total = group if total is None else total + group
+    return total.astype(jnp.bfloat16)
 
 
 def local(
@@ -119,11 +134,7 @@
         concat_axis=0,
         tiled=True,
     )
-    hidden_all = lax.all_gather(hidden.transpose(0, 2, 1), "tensor", axis=0, tiled=False)
-    group_sums = jnp.einsum(
-        "gefn,gefc->genc", hidden_all, down_mine, preferred_element_type=jnp.float32
-    ).astype(jnp.bfloat16)
-    summed = jnp.sum(group_sums.astype(jnp.float32), axis=0).astype(jnp.bfloat16)
+    summed = down_projection(hidden.transpose(0, 2, 1), down_mine, pieces)
     last = summed.shape[2]
     returned = lax.all_to_all(
         summed.reshape(own_experts, owners, CAP, last)

time: 147 us -> 156 us (1.061)
  waiting for transfers between devices: 36.2 us -> 50.9 us
  blocking collectives: 55 us -> 44.3 us
  matrix products: 14.1 us -> 18.6 us
  starting transfers between devices: 28 us -> 31.5 us
  local copies, waits for them, and re-layouts: 9.76 us -> 7.08 us
    ppermute x4 -> x6, waiting for transfers between devices: 14 us -> 28.7 us  [shifted(): lax.ppermute(x, 'tensor', perm=[(i, (i + step) % count) for i in range(co...]
    all_gather x1 -> x0, blocking collectives: 10.9 us -> none  [local(): lax.all_gather(hidden.transpose(0, 2, 1), 'tensor', axis=0, tiled=False)]
    ppermute x4 -> x6, starting transfers between devices: 13.5 us -> 20.8 us  [shifted(): lax.ppermute(x, 'tensor', perm=[(i, (i + step) % count) for i in range(co...]
    all_to_all x1, starting transfers between devices: 10.3 us -> 6.94 us  [local(): lax.all_to_all(summed.reshape(own_experts, owners, CAP, last).transpose(1...]
    dot_general x4, matrix products: 2.61 us -> 5.77 us  [ring_projections(): jnp.einsum('end,edf->enf', piece, gate_rows, preferred_element_type=jnp.f...]
    dot_general x4, matrix products: 3.62 us -> 5.73 us  [ring_projections(): jnp.einsum('end,edf->enf', piece, up_rows, preferred_element_type=jnp.flo...]
    reshape x1, local copies, waits for them, and re-layouts: 2.29 us -> 0.57 us  [local(): down_weight.reshape(own_experts, hidden_width, pieces, out_width)]
  transfers between devices with their start and end apart: 6 -> 8, of which waited for: 4 -> 5; matrix products, arithmetic and copies ran while one was open for 10% -> 12% of each run, Pallas kernels for 0% -> 0%
where the time goes in v7:
time: 156 us
  waiting for transfers between devices  50.9 us (33%)
  blocking collectives  44.3 us (28%)
  starting transfers between devices  31.5 us (20%)
  matrix products  18.6 us (12%)
  local copies, waits for them, and re-layouts  7.08 us (5%)
  other arithmetic  2.2 us (1%)
    all_to_all x1, blocking collectives, local(): lax.all_to_all(local_buffer, ('dp', 'sect'), split_axis=0, concat_axis=0,...  44.3 us
    ppermute x6, waiting for transfers between devices, shifted(): lax.ppermute(x, 'tensor', perm=[(i, (i + step) % count) for i in range(co...  28.7 us
    all_to_all x1, waiting for transfers between devices, local(): lax.all_to_all(summed.reshape(own_experts, owners, CAP, last).transpose(1...  22.2 us
    ppermute x6, starting transfers between devices, shifted(): lax.ppermute(x, 'tensor', perm=[(i, (i + step) % count) for i in range(co...  20.8 us
    all_to_all x1, starting transfers between devices, local(): lax.all_to_all(summed.reshape(own_experts, owners, CAP, last).transpose(1...  6.94 us
    dot_general x4, matrix products, ring_projections(): jnp.einsum('end,edf->enf', piece, gate_rows, preferred_element_type=jnp.f...  5.77 us
    dot_general x4, matrix products, ring_projections(): jnp.einsum('end,edf->enf', piece, up_rows, preferred_element_type=jnp.flo...  5.73 us
    all_to_all x1, starting transfers between devices, local(): lax.all_to_all(down_weight.reshape(own_experts, hidden_width, pieces, out...  3.71 us
  transfers between devices with their start and end apart: 8, of which 5 were waited for; matrix products, arithmetic and copies ran while one was open for 12% of the time, Pallas kernels for 0%

profile of v7, /device:TPU:1, one launch (start us, length us, event | category | flops | bytes accessed | tf_op | source)
XLA Modules:
  0.0 155.6 jit_solution(5771832157580649911)
XLA Ops:
  3.9 1.1 convolution_convert_fusion.4
  5.6 44.3 %all_to_all.15 = bf16[128,20,128]{2,1,0:T(8,128)(2,1)S(1)} all-to-all(bf16[128,20,128]{2,1,0:T(8,128)(2,1)S(1)} %reshape.194), channel_id=1, replica_groups=mesh['dp'=64,'tensor'=4,'sect'=2] {'dp','sect'}, dimensions={0} | all-to-all | bytes 1310720 | tf_op jit(solution)/shard_map/all_to_all | solution.py:118
  49.8 1.4 reshape_transpose_reshape.6
  51.2 3.1 %collective-permute-start = (bf16[1,640,512]{2,1,0:T(8,128)(2,1)}, bf16[1,640,512]{2,1,0:T(8,128)(2,1)}, u32[]{:S(2)}, u32[]{:S(2)}) collective-permute-start(bf16[1,640,512]{2,1,0:T(8,128)(2,1)} %reshape_transpose_reshape.6), channel_id=1, source_target_pairs={{0,2},{2,4},{4,6},{6,0},{1,3},{3,5},{5,7},{7,1},{8,10},{10,12},{12... | collective-permute-start | bytes 1966088 | tf_op jit(solution)/shard_map/ppermute | solution.py:51
  55.9 3.7 %all-to-all-start.1 = ((bf16[4,1,192,512]{3,2,1,0:T(8,128)(2,1)}), bf16[4,1,192,512]{3,2,1,0:T(8,128)(2,1)S(1)}, u32[]{:S(2)}, u32[]{:S(2)}) async-start(bf16[4,1,192,512]{3,2,1,0:T(8,128)(2,1)} %copy.27), calls=%async_computation.1 | async-start | bytes 1572864 | tf_op jit(solution)/shard_map/all_to_all | solution.py:130
  59.6 4.9 %collective-permute-start.2 = (bf16[1,640,512]{2,1,0:T(8,128)(2,1)}, bf16[1,640,512]{2,1,0:T(8,128)(2,1)}, u32[]{:S(2)}, u32[]{:S(2)}) collective-permute-start(bf16[1,640,512]{2,1,0:T(8,128)(2,1)} %reshape_transpose_reshape.6), channel_id=1, source_target_pairs={{0,4},{2,6},{4,0},{6,2},{1,5},{3,7},{5,1},{7,3},{8,12},{10,14},{12... | collective-permute-start | bytes 1966088 | tf_op jit(solution)/shard_map/ppermute | solution.py:51
  64.5 2.8 %collective-permute-start.1 = (bf16[1,640,512]{2,1,0:T(8,128)(2,1)}, bf16[1,640,512]{2,1,0:T(8,128)(2,1)}, u32[]{:S(2)}, u32[]{:S(2)}) collective-permute-start(bf16[1,640,512]{2,1,0:T(8,128)(2,1)} %reshape_transpose_reshape.6), channel_id=1, source_target_pairs={{0,6},{2,0},{4,2},{6,4},{1,7},{3,1},{5,3},{7,5},{8,14},{10,8},{12,... | collective-permute-start | bytes 1966088 | tf_op jit(solution)/shard_map/ppermute | solution.py:51
  67.9 1.4 fusion.44
  69.3 1.3 fusion.39
  71.1 1.5 convolution_add_fusion.3
  72.5 22.0 %collective-permute-done.2 = bf16[1,640,512]{2,1,0:T(8,128)(2,1)} collective-permute-done((bf16[1,640,512]{2,1,0:T(8,128)(2,1)}, bf16[1,640,512]{2,1,0:T(8,128)(2,1)}, u32[]{:S(2)}, u32[]{:S(2)}) %collective-permute-start.2) | collective-permute-done | bytes 655392 | tf_op jit(solution)/shard_map/ppermute | solution.py:51
  94.5 1.5 fusion.19
  96.0 1.5 convolution_add_fusion.1
  97.5 1.5 fusion.17
  98.9 1.5 fusion.10
  100.4 1.5 multiply_convert_fusion
  101.9 3.8 %collective-permute-start.3 = (bf16[1,192,640]{2,1,0:T(8,128)(2,1)S(1)}, bf16[1,192,640]{2,1,0:T(8,128)(2,1)S(1)}, u32[]{:S(2)}, u32[]{:S(2)}) collective-permute-start(bf16[1,192,640]{2,1,0:T(8,128)(2,1)S(1)} %bitcast.85), channel_id=1, source_target_pairs={{0,2},{2,4},{4,6},{6,0},{1,3},{3,5},{5,7},{7,1},{8,10},{10,12},{12... | collective-permute-start | bytes 737288 | tf_op jit(solution)/shard_map/ppermute | solution.py:51
  105.8 3.7 %collective-permute-start.5 = (bf16[1,192,640]{2,1,0:T(8,128)(2,1)S(1)}, bf16[1,192,640]{2,1,0:T(8,128)(2,1)S(1)}, u32[]{:S(2)}, u32[]{:S(2)}) collective-permute-start(bf16[1,192,640]{2,1,0:T(8,128)(2,1)S(1)} %bitcast.86), channel_id=1, source_target_pairs={{0,4},{2,6},{4,0},{6,2},{1,5},{3,7},{5,1},{7,3},{8,12},{10,14},{12... | collective-permute-start | bytes 737288 | tf_op jit(solution)/shard_map/ppermute | solution.py:51
  109.5 2.5 %collective-permute-start.4 = (bf16[1,192,640]{2,1,0:T(8,128)(2,1)S(1)}, bf16[1,192,640]{2,1,0:T(8,128)(2,1)S(1)}, u32[]{:S(2)}, u32[]{:S(2)}) collective-permute-start(bf16[1,192,640]{2,1,0:T(8,128)(2,1)S(1)} %bitcast.87), channel_id=1, source_target_pairs={{0,6},{2,0},{4,2},{6,4},{1,7},{3,1},{5,3},{7,5},{8,14},{10,8},{12,... | collective-permute-start | bytes 737288 | tf_op jit(solution)/shard_map/ppermute | solution.py:51
  112.8 5.6 %collective-permute-done.5 = bf16[1,192,640]{2,1,0:T(8,128)(2,1)S(1)} collective-permute-done((bf16[1,192,640]{2,1,0:T(8,128)(2,1)S(1)}, bf16[1,192,640]{2,1,0:T(8,128)(2,1)S(1)}, u32[]{:S(2)}, u32[]{:S(2)}) %collective-permute-start.5) | collective-permute-done | bytes 245792 | tf_op jit(solution)/shard_map/ppermute | solution.py:51
  119.8 1.4 reshape_transpose_reshape.7
  121.2 6.9 %all-to-all-start.2 = ((bf16[128,20,128]{2,1,0:T(8,128)(2,1)}), bf16[128,20,128]{2,1,0:T(8,128)(2,1)S(1)}, u32[]{:S(2)}, u32[]{:S(2)}) async-start(bf16[128,20,128]{2,1,0:T(8,128)(2,1)} %reshape_transpose_reshape.7), calls=%async_computation.2 | async-start | bytes 1572864 | tf_op jit(solution)/shard_map/all_to_all | solution.py:139
  129.1 2.8 %convolution_convert_fusion.5 = bf16[32,16,128]{2,1,0:T(8,128)(2,1)} fusion(bf16[32,128,1,128]{3,1,2,0:T(8,128)(2,1)} %param.18, f32[32,16]{1,0:T(8,128)S(1)} %fusion.75, f32[32,16,128]{2,1,0:T(8,128)S(1)} %fusion.13), kind=kOutput, calls=%fused_computation.24 | convolution fusion | flops 17040000 | bytes 1443840 | tf_op jit(solution)/shard_map/rkgl,rlkd->rkgd/dot_general | solution.py:46
  132.0 22.2 %all-to-all-done.2 = bf16[128,20,128]{2,1,0:T(8,128)(2,1)S(1)} async-done(((bf16[128,20,128]{2,1,0:T(8,128)(2,1)}), bf16[128,20,128]{2,1,0:T(8,128)(2,1)S(1)}, u32[]{:S(2)}, u32[]{:S(2)}) %all-to-all-start.2) | async-done | bytes 655392 | tf_op jit(solution)/shard_map/all_to_all | solution.py:139
  (40 shorter events, 10.8 us)
Async XLA Ops:
  0.6 127.6 %copy-start = (bf16[32,128,1,128]{3,1,2,0:T(8,128)(2,1)S(1)}, bf16[32,128,1,128]{3,1,2,0:T(8,128)(2,1)}, u32[]{:S(2)}) copy-start(bf16[32,128,1,128]{3,1,2,0:T(8,128)(2,1)} %param.17) | copy-start | bytes 3145732
  5.6 48.8 %copy-start.1 = (bf16[1,192,2048]{2,1,0:T(8,128)(2,1)S(1)}, bf16[1,192,2048]{2,1,0:T(8,128)(2,1)}, u32[]{:S(2)}) copy-start(bf16[1,192,2048]{2,1,0:T(8,128)(2,1)} %param.15) | copy-start | bytes 2359300
  51.2 19.8 %collective-permute-start = (bf16[1,640,512]{2,1,0:T(8,128)(2,1)}, bf16[1,640,512]{2,1,0:T(8,128)(2,1)}, u32[]{:S(2)}, u32[]{:S(2)}) collective-permute-start(bf16[1,640,512]{2,1,0:T(8,128)(2,1)} %reshape_transpose_reshape.6), channel_id=1, source_target_pairs={{0,2},{2,4},{4,6},{6,0},{1,3},{3,5},{5,7},{7,1},{8,10},{10,12},{12... | collective-permute-start | bytes 1966088 | tf_op jit(solution)/shard_map/ppermute | solution.py:51
  55.9 56.1 %all-to-all-start.1 = ((bf16[4,1,192,512]{3,2,1,0:T(8,128)(2,1)}), bf16[4,1,192,512]{3,2,1,0:T(8,128)(2,1)S(1)}, u32[]{:S(2)}, u32[]{:S(2)}) async-start(bf16[4,1,192,512]{3,2,1,0:T(8,128)(2,1)} %copy.27), calls=%async_computation.1 | async-start | bytes 1572864 | tf_op jit(solution)/shard_map/all_to_all | solution.py:130
  59.6 34.9 %collective-permute-start.2 = (bf16[1,640,512]{2,1,0:T(8,128)(2,1)}, bf16[1,640,512]{2,1,0:T(8,128)(2,1)}, u32[]{:S(2)}, u32[]{:S(2)}) collective-permute-start(bf16[1,640,512]{2,1,0:T(8,128)(2,1)} %reshape_transpose_reshape.6), channel_id=1, source_target_pairs={{0,4},{2,6},{4,0},{6,2},{1,5},{3,7},{5,1},{7,3},{8,12},{10,14},{12... | collective-permute-start | bytes 1966088 | tf_op jit(solution)/shard_map/ppermute | solution.py:51
  64.5 34.4 %collective-permute-start.1 = (bf16[1,640,512]{2,1,0:T(8,128)(2,1)}, bf16[1,640,512]{2,1,0:T(8,128)(2,1)}, u32[]{:S(2)}, u32[]{:S(2)}) collective-permute-start(bf16[1,640,512]{2,1,0:T(8,128)(2,1)} %reshape_transpose_reshape.6), channel_id=1, source_target_pairs={{0,6},{2,0},{4,2},{6,4},{1,7},{3,1},{5,3},{7,5},{8,14},{10,8},{12,... | collective-permute-start | bytes 1966088 | tf_op jit(solution)/shard_map/ppermute | solution.py:51
  67.9 3.2 %copy-start.2 = (bf16[1,2048,192]{1,2,0:T(8,128)(2,1)S(1)}, bf16[1,2048,192]{1,2,0:T(8,128)(2,1)}, u32[]{:S(2)}) copy-start(bf16[1,2048,192]{1,2,0:T(8,128)(2,1)} %param.13) | copy-start | bytes 2359300
  70.6 25.4 %copy-start.3 = (bf16[1,2048,192]{1,2,0:T(8,128)(2,1)S(1)}, bf16[1,2048,192]{1,2,0:T(8,128)(2,1)}, u32[]{:S(2)}) copy-start(bf16[1,2048,192]{1,2,0:T(8,128)(2,1)} %param.14) | copy-start | bytes 2359300
  101.9 10.5 %collective-permute-start.3 = (bf16[1,192,640]{2,1,0:T(8,128)(2,1)S(1)}, bf16[1,192,640]{2,1,0:T(8,128)(2,1)S(1)}, u32[]{:S(2)}, u32[]{:S(2)}) collective-permute-start(bf16[1,192,640]{2,1,0:T(8,128)(2,1)S(1)} %bitcast.85), channel_id=1, source_target_pairs={{0,2},{2,4},{4,6},{6,0},{1,3},{3,5},{5,7},{7,1},{8,10},{10,12},{12... | collective-permute-start | bytes 737288 | tf_op jit(solution)/shard_map/ppermute | solution.py:51
  105.8 12.6 %collective-permute-start.5 = (bf16[1,192,640]{2,1,0:T(8,128)(2,1)S(1)}, bf16[1,192,640]{2,1,0:T(8,128)(2,1)S(1)}, u32[]{:S(2)}, u32[]{:S(2)}) collective-permute-start(bf16[1,192,640]{2,1,0:T(8,128)(2,1)S(1)} %bitcast.86), channel_id=1, source_target_pairs={{0,4},{2,6},{4,0},{6,2},{1,5},{3,7},{5,1},{7,3},{8,12},{10,14},{12... | collective-permute-start | bytes 737288 | tf_op jit(solution)/shard_map/ppermute | solution.py:51
  109.5 9.9 %collective-permute-start.4 = (bf16[1,192,640]{2,1,0:T(8,128)(2,1)S(1)}, bf16[1,192,640]{2,1,0:T(8,128)(2,1)S(1)}, u32[]{:S(2)}, u32[]{:S(2)}) collective-permute-start(bf16[1,192,640]{2,1,0:T(8,128)(2,1)S(1)} %bitcast.87), channel_id=1, source_target_pairs={{0,6},{2,0},{4,2},{6,4},{1,7},{3,1},{5,3},{7,5},{8,14},{10,8},{12,... | collective-permute-start | bytes 737288 | tf_op jit(solution)/shard_map/ppermute | solution.py:51
  119.8 8.4 %copy-start.5 = (s32[32]{0:T(128)S(1)}, s32[32]{0:T(128)}, u32[]{:S(2)}) copy-start(s32[32]{0:T(128)} %param.19) | copy-start | bytes 388
  119.8 8.5 %copy-start.4 = (bf16[32,16,128]{2,1,0:T(8,128)(2,1)S(1)}, bf16[32,16,128]{2,1,0:T(8,128)(2,1)}, u32[]{:S(2)}) copy-start(bf16[32,16,128]{2,1,0:T(8,128)(2,1)} %param.16) | copy-start | bytes 393220
  121.2 33.0 %all-to-all-start.2 = ((bf16[128,20,128]{2,1,0:T(8,128)(2,1)}), bf16[128,20,128]{2,1,0:T(8,128)(2,1)S(1)}, u32[]{:S(2)}, u32[]{:S(2)}) async-start(bf16[128,20,128]{2,1,0:T(8,128)(2,1)} %reshape_transpose_reshape.7), calls=%async_computation.2 | async-start | bytes 1572864 | tf_op jit(solution)/shard_map/all_to_all | solution.py:139

commit v8 on v4

--- a/solution.py
+++ b/solution.py
@@ -8,27 +8,20 @@
 
 
 def route_tables(expert_ids, weights, experts, capacity):
-    row_count, top_count = expert_ids.shape
-    pair_count = row_count * top_count
-    flat_ids = expert_ids.reshape(pair_count)
-    one_hot = (flat_ids[:, None] == jnp.arange(experts, dtype=jnp.int32)[None, :]).astype(
-        jnp.float32
-    )
-    ordinal = jnp.arange(pair_count, dtype=jnp.int32)
-    earlier = (ordinal[:, None] > ordinal[None, :]).astype(jnp.float32)
-    counts = jnp.dot(earlier, one_hot, preferred_element_type=jnp.float32)
-    slot_index = jnp.sum(counts * one_hot, axis=1).astype(jnp.int32)
-    target = flat_ids * capacity + slot_index
-    select = (jnp.arange(experts * capacity, dtype=jnp.int32)[:, None] == target[None, :]).astype(
-        jnp.float32
-    )
-    select = select.reshape(experts * capacity, row_count, top_count)
+    row_count = expert_ids.shape[0]
+    named = expert_ids[:, :, None] == jnp.arange(experts, dtype=jnp.int32)[None, None, :]
     share_norm = (weights / jnp.sum(weights, axis=1, keepdims=True)).astype(jnp.bfloat16)
     share_norm = lax.optimization_barrier(share_norm).astype(jnp.float32)
-    dispatch = jnp.sum(select, axis=2).astype(jnp.bfloat16)
-    combine = jnp.sum(select * share_norm[None, :, :], axis=2).astype(jnp.bfloat16)
-    return (dispatch, combine)
-
+    member = jnp.sum(named.astype(jnp.float32), axis=1)
+    share_of = jnp.sum(jnp.where(named, share_norm[:, :, None], 0.0), axis=1)
+    rows = jnp.arange(row_count, dtype=jnp.int32)
+    earlier = (rows[:, None] > rows[None, :]).astype(jnp.float32)
+    slot = jnp.dot(earlier, member, preferred_element_type=jnp.float32)
+    level = jnp.arange(capacity, dtype=jnp.float32)[None, :, None]
+    hit = (slot.T[:, None, :] == level) & (member.T[:, None, :] > 0)
+    dispatch = jnp.where(hit, 1.0, 0.0).reshape(experts * capacity, row_count)
+    combine = jnp.where(hit, share_of.T[:, None, :], 0.0).reshape(experts * capacity, row_count)
+    return (dispatch.astype(jnp.bfloat16), combine.astype(jnp.bfloat16))
 
 def attend(query, cache_keys, cache_values, lengths):
     row_count, head_count, head_size = query.shape

time: 147 us -> 147 us (level)
  no operation moved by 1% of the time
where the time goes in v8:
time: 147 us; the launch traced here: 146 us
  blocking collectives  55 us (37%)
  waiting for transfers between devices  35.8 us (24%)
  starting transfers between devices  28.2 us (19%)
  matrix products  13.3 us (9%)
  local copies, waits for them, and re-layouts  10.4 us (7%)
  other arithmetic  2.1 us (1%)
    all_to_all x1, blocking collectives, local(): lax.all_to_all(local_buffer, ('dp', 'sect'), split_axis=0, concat_axis=0,...  44.1 us
    all_to_all x1, waiting for transfers between devices, local(): lax.all_to_all(summed.reshape(own_experts, owners, CAP, last).transpose(1...  21.8 us
    ppermute x4, waiting for transfers between devices, shifted(): lax.ppermute(x, 'tensor', perm=[(i, (i + step) % count) for i in range(co...  14 us
    ppermute x4, starting transfers between devices, shifted(): lax.ppermute(x, 'tensor', perm=[(i, (i + step) % count) for i in range(co...  13.5 us
    all_gather x1, blocking collectives, local(): lax.all_gather(hidden.transpose(0, 2, 1), 'tensor', axis=0, tiled=False)  10.9 us
    all_to_all x1, starting transfers between devices, local(): lax.all_to_all(summed.reshape(own_experts, owners, CAP, last).transpose(1...  10.5 us
    all_to_all x1, starting transfers between devices, local(): lax.all_to_all(down_weight.reshape(own_experts, hidden_width, pieces, out...  4.19 us
    dot_general x4, matrix products, ring_projections(): jnp.einsum('end,edf->enf', piece, up_rows, preferred_element_type=jnp.flo...  3.62 us
  transfers between devices with their start and end apart: 6, of which 4 were waited for; matrix products, arithmetic and copies ran while one was open for 10% of the time, Pallas kernels for 0%

profile of v8, /device:TPU:1, one launch (start us, length us, event | category | flops | bytes accessed | tf_op | source)
XLA Modules:
  0.0 145.9 jit_solution(14431403877637570771)
XLA Ops:
  0.6 0.8 reduce_sum.49
  4.9 44.1 %all_to_all.15 = bf16[128,20,128]{2,1,0:T(8,128)(2,1)S(1)} all-to-all(bf16[128,20,128]{2,1,0:T(8,128)(2,1)S(1)} %reshape.189), channel_id=1, replica_groups=mesh['dp'=64,'tensor'=4,'sect'=2] {'dp','sect'}, dimensions={0} | all-to-all | bytes 1310720 | tf_op jit(solution)/shard_map/all_to_all | solution.py:96
  49.1 1.4 reshape_transpose_reshape.6
  50.4 4.4 %collective-permute-start.1 = (bf16[1,640,512]{2,1,0:T(8,128)(2,1)}, bf16[1,640,512]{2,1,0:T(8,128)(2,1)}, u32[]{:S(2)}, u32[]{:S(2)}) collective-permute-start(bf16[1,640,512]{2,1,0:T(8,128)(2,1)} %reshape_transpose_reshape.6), channel_id=1, source_target_pairs={{0,6},{2,0},{4,2},{6,4},{1,7},{3,1},{5,3},{7,5},{8,14},{10,8},{12,... | collective-permute-start | bytes 1966088 | tf_op jit(solution)/shard_map/ppermute | solution.py:44
  54.8 1.9 %collective-permute-start = (bf16[1,640,512]{2,1,0:T(8,128)(2,1)}, bf16[1,640,512]{2,1,0:T(8,128)(2,1)S(1)}, u32[]{:S(2)}, u32[]{:S(2)}) collective-permute-start(bf16[1,640,512]{2,1,0:T(8,128)(2,1)} %reshape_transpose_reshape.6), channel_id=1, source_target_pairs={{0,2},{2,4},{4,6},{6,0},{1,3},{3,5},{5,7},{7,1},{8,10},{10,12},{12... | collective-permute-start | bytes 1966088 | tf_op jit(solution)/shard_map/ppermute | solution.py:44
  56.8 2.3 %reshape.203 = bf16[1,192,4,512]{3,2,1,0:T(4,128)(2,1)S(1)} reshape(bf16[1,192,2048]{2,1,0:T(8,128)(2,1)} %param.15) | data formatting | bytes 1572864 | tf_op jit(solution)/shard_map/reshape | solution.py:109
  59.1 1.0 copy.29
  60.1 4.2 %all-to-all-start.1 = ((bf16[4,1,192,512]{3,2,1,0:T(8,128)(2,1)}), bf16[4,1,192,512]{3,2,1,0:T(8,128)(2,1)}, u32[]{:S(2)}, u32[]{:S(2)}) async-start(bf16[4,1,192,512]{3,2,1,0:T(8,128)(2,1)} %copy.29), calls=%async_computation.1 | async-start | bytes 1572864 | tf_op jit(solution)/shard_map/all_to_all | solution.py:108
  64.9 1.4 fusion.22
  66.7 2.7 %collective-permute-done.1 = bf16[1,640,512]{2,1,0:T(8,128)(2,1)} collective-permute-done((bf16[1,640,512]{2,1,0:T(8,128)(2,1)}, bf16[1,640,512]{2,1,0:T(8,128)(2,1)}, u32[]{:S(2)}, u32[]{:S(2)}) %collective-permute-start.1) | collective-permute-done | bytes 655392 | tf_op jit(solution)/shard_map/ppermute | solution.py:44
  69.4 1.0 slice.8
  70.4 5.3 %collective-permute-start.2 = (bf16[1,320,512]{2,1,0:T(8,128)(2,1)S(1)}, bf16[1,320,512]{2,1,0:T(8,128)(2,1)S(1)}, u32[]{:S(2)}, u32[]{:S(2)}) collective-permute-start(bf16[1,320,512]{2,1,0:T(8,128)(2,1)S(1)} %slice.8), channel_id=1, source_target_pairs={{0,6},{2,0},{4,2},{6,4},{1,7},{3,1},{5,3},{7,5},{8,14},{10,8},{12,... | collective-permute-start | bytes 983048 | tf_op jit(solution)/shard_map/ppermute | solution.py:44
  75.7 1.9 %collective-permute-start.3 = (bf16[1,320,512]{2,1,0:T(8,128)(2,1)S(1)}, bf16[1,320,512]{2,1,0:T(8,128)(2,1)S(1)}, u32[]{:S(2)}, u32[]{:S(2)}) collective-permute-start(bf16[1,320,512]{2,1,0:T(8,128)(2,1)S(1)} %slice.9), channel_id=1, source_target_pairs={{0,2},{2,4},{4,6},{6,0},{1,3},{3,5},{5,7},{7,1},{8,10},{10,12},{12... | collective-permute-start | bytes 983048 | tf_op jit(solution)/shard_map/ppermute | solution.py:44
  78.4 6.3 %collective-permute-done.2 = bf16[1,320,512]{2,1,0:T(8,128)(2,1)S(1)} collective-permute-done((bf16[1,320,512]{2,1,0:T(8,128)(2,1)S(1)}, bf16[1,320,512]{2,1,0:T(8,128)(2,1)S(1)}, u32[]{:S(2)}, u32[]{:S(2)}) %collective-permute-start.2) | collective-permute-done | bytes 327712 | tf_op jit(solution)/shard_map/ppermute | solution.py:44
  84.7 5.1 %collective-permute-done.3 = bf16[1,320,512]{2,1,0:T(8,128)(2,1)S(1)} collective-permute-done((bf16[1,320,512]{2,1,0:T(8,128)(2,1)S(1)}, bf16[1,320,512]{2,1,0:T(8,128)(2,1)S(1)}, u32[]{:S(2)}, u32[]{:S(2)}) %collective-permute-start.3) | collective-permute-done | bytes 327712 | tf_op jit(solution)/shard_map/ppermute | solution.py:44
  90.6 1.5 %fusion.3 = f32[640,192]{0,1:T(8,128)S(1)} fusion(f32[640,192]{0,1:T(8,128)S(1)} %fusion.18, f32[640,192]{0,1:T(8,128)S(1)} %convolution_add_fusion.3, bf16[1,640,512]{2,1,0:T(8,128)(2,1)} %collective-permute-done.1, bf16[1,2048,192]{1,2,0:T(8,128)(2,1)S(1)} %copy-done.1, s32[]{:T(128)S(6)} %select_n.69), kind=kOutput, calls=%fused_computation.8 | convolution fusion | flops 126074880 | bytes 2326532 | tf_op jit(solution)/shard_map/end,edf->enf/dot_general | solution.py:67
  92.0 1.5 %fusion.8 = bf16[1,192,640]{2,1,0:T(8,128)(2,1)S(1)} fusion(f32[640,192]{0,1:T(8,128)S(1)} %fusion.17, f32[640,192]{0,1:T(8,128)S(1)} %convolution_add_fusion.1, bf16[1,640,512]{2,1,0:T(8,128)(2,1)} %collective-permute-done.1, f32[640,192]{0,1:T(8,128)S(1)} %fusion.3, bf16[1,2048,192]{1,2,0:T(8,128)(2,1)S(1)} %copy-done.2, s32[]{:T(128)S(6)} %select_n.69), kind=kOutput, calls=%fused_computation.15 | convolution fusion | flops 126812160 | bytes 2572292 | tf_op jit(solution)/shard_map/end,edf->enf/dot_general | solution.py:68
  93.5 10.9 %all-gather = bf16[4,192,640]{2,1,0:T(8,128)(2,1)S(1)} all-gather(bf16[1,192,640]{2,1,0:T(8,128)(2,1)S(1)} %fusion.8), channel_id=2, replica_groups=mesh['dp'=64,'tensor'=4,'sect'=2] {'tensor'}, dimensions={0}, use_global_device_ids=true | all-gather | bytes 1228800 | tf_op jit(solution)/shard_map/all_gather | solution.py:115
  104.4 2.1 %convert_reduce_fusion = bf16[640,512]{1,0:T(8,128)(2,1)S(1)} fusion(bf16[4,192,640]{2,1,0:T(8,128)(2,1)S(1)} %all-gather, bf16[4,1,192,512]{3,2,1,0:T(8,128)(2,1)} %all-to-all-done.1), kind=kOutput, calls=%fused_computation.1 | convolution fusion | flops 505610240 | bytes 2424832 | tf_op jit(solution)/shard_map/gefn,gefc->genc/dot_general | solution.py:116
  106.5 1.4 reshape_transpose_reshape.7
  108.0 10.5 %all-to-all-start.2 = ((bf16[128,20,128]{2,1,0:T(8,128)(2,1)}), bf16[128,20,128]{2,1,0:T(8,128)(2,1)S(1)}, u32[]{:S(2)}, u32[]{:S(2)}) async-start(bf16[128,20,128]{2,1,0:T(8,128)(2,1)} %reshape_transpose_reshape.7), calls=%async_computation.2 | async-start | bytes 1572864 | tf_op jit(solution)/shard_map/all_to_all | solution.py:121
  119.8 2.8 %convolution_convert_fusion.1 = bf16[32,16,128]{2,1,0:T(8,128)(2,1)} fusion(bf16[32,128,1,128]{3,1,2,0:T(8,128)(2,1)} %param.18, f32[32,16]{1,0:T(8,128)S(1)} %fusion.55, f32[32,16,128]{2,1,0:T(8,128)S(1)} %fusion.7), kind=kOutput, calls=%fused_computation.16 | convolution fusion | flops 17040000 | bytes 1443840 | tf_op jit(solution)/shard_map/rkgl,rlkd->rkgd/dot_general | solution.py:39
  122.7 21.8 %all-to-all-done.2 = bf16[128,20,128]{2,1,0:T(8,128)(2,1)S(1)} async-done(((bf16[128,20,128]{2,1,0:T(8,128)(2,1)}), bf16[128,20,128]{2,1,0:T(8,128)(2,1)S(1)}, u32[]{:S(2)}, u32[]{:S(2)}) %all-to-all-start.2) | async-done | bytes 655392 | tf_op jit(solution)/shard_map/all_to_all | solution.py:121
  145.0 0.9 convolution_convert_fusion.2
  (43 shorter events, 7.7 us)
Async XLA Ops:
  0.6 118.3 %copy-start = (bf16[32,128,1,128]{3,1,2,0:T(8,128)(2,1)S(1)}, bf16[32,128,1,128]{3,1,2,0:T(8,128)(2,1)}, u32[]{:S(2)}) copy-start(bf16[32,128,1,128]{3,1,2,0:T(8,128)(2,1)} %param.17) | copy-start | bytes 3145732
  3.0 1.0 copy-start.4
  50.4 18.9 %collective-permute-start.1 = (bf16[1,640,512]{2,1,0:T(8,128)(2,1)}, bf16[1,640,512]{2,1,0:T(8,128)(2,1)}, u32[]{:S(2)}, u32[]{:S(2)}) collective-permute-start(bf16[1,640,512]{2,1,0:T(8,128)(2,1)} %reshape_transpose_reshape.6), channel_id=1, source_target_pairs={{0,6},{2,0},{4,2},{6,4},{1,7},{3,1},{5,3},{7,5},{8,14},{10,8},{12,... | collective-permute-start | bytes 1966088 | tf_op jit(solution)/shard_map/ppermute | solution.py:44
  54.8 20.9 %collective-permute-start = (bf16[1,640,512]{2,1,0:T(8,128)(2,1)}, bf16[1,640,512]{2,1,0:T(8,128)(2,1)S(1)}, u32[]{:S(2)}, u32[]{:S(2)}) collective-permute-start(bf16[1,640,512]{2,1,0:T(8,128)(2,1)} %reshape_transpose_reshape.6), channel_id=1, source_target_pairs={{0,2},{2,4},{4,6},{6,0},{1,3},{3,5},{5,7},{7,1},{8,10},{10,12},{12... | collective-permute-start | bytes 1966088 | tf_op jit(solution)/shard_map/ppermute | solution.py:44
  60.1 44.3 %all-to-all-start.1 = ((bf16[4,1,192,512]{3,2,1,0:T(8,128)(2,1)}), bf16[4,1,192,512]{3,2,1,0:T(8,128)(2,1)}, u32[]{:S(2)}, u32[]{:S(2)}) async-start(bf16[4,1,192,512]{3,2,1,0:T(8,128)(2,1)} %copy.29), calls=%async_computation.1 | async-start | bytes 1572864 | tf_op jit(solution)/shard_map/all_to_all | solution.py:108
  64.9 1.4 copy-start.1
  66.3 11.4 %copy-start.2 = (bf16[1,2048,192]{1,2,0:T(8,128)(2,1)S(1)}, bf16[1,2048,192]{1,2,0:T(8,128)(2,1)}, u32[]{:S(2)}) copy-start(bf16[1,2048,192]{1,2,0:T(8,128)(2,1)} %param.14) | copy-start | bytes 2359300
  70.4 14.3 %collective-permute-start.2 = (bf16[1,320,512]{2,1,0:T(8,128)(2,1)S(1)}, bf16[1,320,512]{2,1,0:T(8,128)(2,1)S(1)}, u32[]{:S(2)}, u32[]{:S(2)}) collective-permute-start(bf16[1,320,512]{2,1,0:T(8,128)(2,1)S(1)} %slice.8), channel_id=1, source_target_pairs={{0,6},{2,0},{4,2},{6,4},{1,7},{3,1},{5,3},{7,5},{8,14},{10,8},{12,... | collective-permute-start | bytes 983048 | tf_op jit(solution)/shard_map/ppermute | solution.py:44
  75.7 14.1 %collective-permute-start.3 = (bf16[1,320,512]{2,1,0:T(8,128)(2,1)S(1)}, bf16[1,320,512]{2,1,0:T(8,128)(2,1)S(1)}, u32[]{:S(2)}, u32[]{:S(2)}) collective-permute-start(bf16[1,320,512]{2,1,0:T(8,128)(2,1)S(1)} %slice.9), channel_id=1, source_target_pairs={{0,2},{2,4},{4,6},{6,0},{1,3},{3,5},{5,7},{7,1},{8,10},{10,12},{12... | collective-permute-start | bytes 983048 | tf_op jit(solution)/shard_map/ppermute | solution.py:44
  108.0 10.9 %copy-start.5 = (s32[32]{0:T(128)S(1)}, s32[32]{0:T(128)}, u32[]{:S(2)}) copy-start(s32[32]{0:T(128)} %param.19) | copy-start | bytes 388
  108.0 11.0 %copy-start.3 = (bf16[32,16,128]{2,1,0:T(8,128)(2,1)S(1)}, bf16[32,16,128]{2,1,0:T(8,128)(2,1)}, u32[]{:S(2)}) copy-start(bf16[32,16,128]{2,1,0:T(8,128)(2,1)} %param.16) | copy-start | bytes 393220
  108.0 36.5 %all-to-all-start.2 = ((bf16[128,20,128]{2,1,0:T(8,128)(2,1)}), bf16[128,20,128]{2,1,0:T(8,128)(2,1)S(1)}, u32[]{:S(2)}, u32[]{:S(2)}) async-start(bf16[128,20,128]{2,1,0:T(8,128)(2,1)} %reshape_transpose_reshape.7), calls=%async_computation.2 | async-start | bytes 1572864 | tf_op jit(solution)/shard_map/all_to_all | solution.py:121

commit v9 on v8

--- a/solution.py
+++ b/solution.py
@@ -7,21 +7,27 @@
 CAP = 5
 
 
-def route_tables(expert_ids, weights, experts, capacity):
+def route_slots(expert_ids, experts, capacity):
     row_count = expert_ids.shape[0]
     named = expert_ids[:, :, None] == jnp.arange(experts, dtype=jnp.int32)[None, None, :]
-    share_norm = (weights / jnp.sum(weights, axis=1, keepdims=True)).astype(jnp.bfloat16)
-    share_norm = lax.optimization_barrier(share_norm).astype(jnp.float32)
     member = jnp.sum(named.astype(jnp.float32), axis=1)
-    share_of = jnp.sum(jnp.where(named, share_norm[:, :, None], 0.0), axis=1)
     rows = jnp.arange(row_count, dtype=jnp.int32)
     earlier = (rows[:, None] > rows[None, :]).astype(jnp.float32)
     slot = jnp.dot(earlier, member, preferred_element_type=jnp.float32)
     level = jnp.arange(capacity, dtype=jnp.float32)[None, :, None]
     hit = (slot.T[:, None, :] == level) & (member.T[:, None, :] > 0)
     dispatch = jnp.where(hit, 1.0, 0.0).reshape(experts * capacity, row_count)
+    return dispatch.astype(jnp.bfloat16), hit
+
+
+def route_combine(expert_ids, weights, hit, experts, capacity):
+    row_count = expert_ids.shape[0]
+    named = expert_ids[:, :, None] == jnp.arange(experts, dtype=jnp.int32)[None, None, :]
+    share_norm = (weights / jnp.sum(weights, axis=1, keepdims=True)).astype(jnp.bfloat16)
+    share_norm = lax.optimization_barrier(share_norm).astype(jnp.float32)
+    share_of = jnp.sum(jnp.where(named, share_norm[:, :, None], 0.0), axis=1)
     combine = jnp.where(hit, share_of.T[:, None, :], 0.0).reshape(experts * capacity, row_count)
-    return (dispatch.astype(jnp.bfloat16), combine.astype(jnp.bfloat16))
+    return combine.astype(jnp.bfloat16)
 
 def attend(query, cache_keys, cache_values, lengths):
     row_count, head_count, head_size = query.shape
@@ -84,7 +90,7 @@
     lengths,
 ):
     owners = lax.axis_size("dp") * lax.axis_size("sect")
-    dispatch, combine = route_tables(route_experts, route_weights, EXPERTS, CAP)
+    dispatch, hit = route_slots(route_experts, EXPERTS, CAP)
     slot_total = EXPERTS * CAP
     per_owner = slot_total // owners
     local_buffer = jnp.dot(dispatch, tokens, preferred_element_type=jnp.float32).astype(
@@ -94,6 +100,10 @@
     lanes = 128
     local_buffer = local_buffer.reshape(owners, per_owner * width // lanes, lanes)
     arrived = lax.all_to_all(local_buffer, ("dp", "sect"), split_axis=0, concat_axis=0, tiled=True)
+    arrived, late_ids, late_weights, late_hit = lax.optimization_barrier(
+        (arrived, route_experts, route_weights, hit)
+    )
+    combine = route_combine(late_ids, late_weights, late_hit, EXPERTS, CAP)
     own_experts = gate_weight.shape[0]
     pieces = lax.axis_size("tensor")
     inputs = (

time: 147 us -> 146 us (level)
  blocking collectives: 55 us -> 10.9 us
  waiting for transfers between devices: 35.8 us -> 61.3 us
  starting transfers between devices: 28.2 us -> 46.7 us
    all_to_all x1 -> x0, blocking collectives: 44.1 us -> none  [local(): lax.all_to_all(local_buffer, ('dp', 'sect'), split_axis=0, concat_axis=0,...]
    all_to_all x0 -> x1, waiting for transfers between devices: none -> 25.8 us  [local(): lax.all_to_all(local_buffer, ('dp', 'sect'), split_axis=0, concat_axis=0,...]
    all_to_all x0 -> x1, starting transfers between devices: none -> 18.4 us  [local(): lax.all_to_all(local_buffer, ('dp', 'sect'), split_axis=0, concat_axis=0,...]
  transfers between devices with their start and end apart: 6 -> 7, of which waited for: 4 -> 5; matrix products, arithmetic and copies ran while one was open for 10% -> 11% of each run, Pallas kernels for 0% -> 0%
where the time goes in v9:
time: 146 us; the launch traced here: 145 us
  waiting for transfers between devices  61.3 us (42%)
  starting transfers between devices  46.7 us (32%)
  matrix products  13.3 us (9%)
  local copies, waits for them, and re-layouts  11.5 us (8%)
  blocking collectives  10.9 us (7%)
    all_to_all x1, waiting for transfers between devices, local(): lax.all_to_all(local_buffer, ('dp', 'sect'), split_axis=0, concat_axis=0,...  25.8 us
    all_to_all x1, waiting for transfers between devices, local(): lax.all_to_all(summed.reshape(own_experts, owners, CAP, last).transpose(1...  21.5 us
    all_to_all x1, starting transfers between devices, local(): lax.all_to_all(local_buffer, ('dp', 'sect'), split_axis=0, concat_axis=0,...  18.4 us
    ppermute x4, waiting for transfers between devices, shifted(): lax.ppermute(x, 'tensor', perm=[(i, (i + step) % count) for i in range(co...  14 us
    ppermute x4, starting transfers between devices, shifted(): lax.ppermute(x, 'tensor', perm=[(i, (i + step) % count) for i in range(co...  13.5 us
    all_gather x1, blocking collectives, local(): lax.all_gather(hidden.transpose(0, 2, 1), 'tensor', axis=0, tiled=False)  10.9 us
    all_to_all x1, starting transfers between devices, local(): lax.all_to_all(summed.reshape(own_experts, owners, CAP, last).transpose(1...  10.5 us
    all_to_all x1, starting transfers between devices, local(): lax.all_to_all(down_weight.reshape(own_experts, hidden_width, pieces, out...  4.19 us
  transfers between devices with their start and end apart: 7, of which 5 were waited for; matrix products, arithmetic and copies ran while one was open for 11% of the time, Pallas kernels for 0%

profile of v9, /device:TPU:1, one launch (start us, length us, event | category | flops | bytes accessed | tf_op | source)
XLA Modules:
  0.0 145.4 jit_solution(15316986792925892543)
XLA Ops:
  2.9 1.4 reshape.151
  4.3 18.4 %all-to-all-start = ((bf16[128,20,128]{2,1,0:T(8,128)(2,1)}), bf16[128,20,128]{2,1,0:T(8,128)(2,1)S(1)}, u32[]{:S(2)}, u32[]{:S(2)}) async-start(bf16[128,20,128]{2,1,0:T(8,128)(2,1)} %reshape.151), calls=%async_computation | async-start | bytes 1572864 | tf_op jit(solution)/shard_map/all_to_all | solution.py:102
  22.8 25.8 %all-to-all-done = bf16[128,20,128]{2,1,0:T(8,128)(2,1)S(1)} async-done(((bf16[128,20,128]{2,1,0:T(8,128)(2,1)}), bf16[128,20,128]{2,1,0:T(8,128)(2,1)S(1)}, u32[]{:S(2)}, u32[]{:S(2)}) %all-to-all-start) | async-done | bytes 655392 | tf_op jit(solution)/shard_map/all_to_all | solution.py:102
  48.6 1.4 reshape_transpose_reshape.6
  50.0 4.4 %collective-permute-start.1 = (bf16[1,640,512]{2,1,0:T(8,128)(2,1)}, bf16[1,640,512]{2,1,0:T(8,128)(2,1)}, u32[]{:S(2)}, u32[]{:S(2)}) collective-permute-start(bf16[1,640,512]{2,1,0:T(8,128)(2,1)} %reshape_transpose_reshape.6), channel_id=1, source_target_pairs={{0,6},{2,0},{4,2},{6,4},{1,7},{3,1},{5,3},{7,5},{8,14},{10,8},{12,... | collective-permute-start | bytes 1966088 | tf_op jit(solution)/shard_map/ppermute | solution.py:50
  54.4 1.9 %collective-permute-start = (bf16[1,640,512]{2,1,0:T(8,128)(2,1)}, bf16[1,640,512]{2,1,0:T(8,128)(2,1)S(1)}, u32[]{:S(2)}, u32[]{:S(2)}) collective-permute-start(bf16[1,640,512]{2,1,0:T(8,128)(2,1)} %reshape_transpose_reshape.6), channel_id=1, source_target_pairs={{0,2},{2,4},{4,6},{6,0},{1,3},{3,5},{5,7},{7,1},{8,10},{10,12},{12... | collective-permute-start | bytes 1966088 | tf_op jit(solution)/shard_map/ppermute | solution.py:50
  56.3 2.3 %reshape.165 = bf16[1,192,4,512]{3,2,1,0:T(4,128)(2,1)S(1)} reshape(bf16[1,192,2048]{2,1,0:T(8,128)(2,1)} %param.15) | data formatting | bytes 1572864 | tf_op jit(solution)/shard_map/reshape | solution.py:119
  58.6 1.0 copy.33
  59.6 4.2 %all-to-all-start.1 = ((bf16[4,1,192,512]{3,2,1,0:T(8,128)(2,1)}), bf16[4,1,192,512]{3,2,1,0:T(8,128)(2,1)}, u32[]{:S(2)}, u32[]{:S(2)}) async-start(bf16[4,1,192,512]{3,2,1,0:T(8,128)(2,1)} %copy.33), calls=%async_computation.1 | async-start | bytes 1572864 | tf_op jit(solution)/shard_map/all_to_all | solution.py:118
  64.4 1.4 fusion.22
  66.2 2.7 %collective-permute-done.1 = bf16[1,640,512]{2,1,0:T(8,128)(2,1)} collective-permute-done((bf16[1,640,512]{2,1,0:T(8,128)(2,1)}, bf16[1,640,512]{2,1,0:T(8,128)(2,1)}, u32[]{:S(2)}, u32[]{:S(2)}) %collective-permute-start.1) | collective-permute-done | bytes 655392 | tf_op jit(solution)/shard_map/ppermute | solution.py:50
  68.9 1.0 slice.8
  69.9 5.3 %collective-permute-start.2 = (bf16[1,320,512]{2,1,0:T(8,128)(2,1)S(1)}, bf16[1,320,512]{2,1,0:T(8,128)(2,1)S(1)}, u32[]{:S(2)}, u32[]{:S(2)}) collective-permute-start(bf16[1,320,512]{2,1,0:T(8,128)(2,1)S(1)} %slice.8), channel_id=1, source_target_pairs={{0,6},{2,0},{4,2},{6,4},{1,7},{3,1},{5,3},{7,5},{8,14},{10,8},{12,... | collective-permute-start | bytes 983048 | tf_op jit(solution)/shard_map/ppermute | solution.py:50
  75.3 1.9 %collective-permute-start.3 = (bf16[1,320,512]{2,1,0:T(8,128)(2,1)S(1)}, bf16[1,320,512]{2,1,0:T(8,128)(2,1)S(1)}, u32[]{:S(2)}, u32[]{:S(2)}) collective-permute-start(bf16[1,320,512]{2,1,0:T(8,128)(2,1)S(1)} %slice.9), channel_id=1, source_target_pairs={{0,2},{2,4},{4,6},{6,0},{1,3},{3,5},{5,7},{7,1},{8,10},{10,12},{12... | collective-permute-start | bytes 983048 | tf_op jit(solution)/shard_map/ppermute | solution.py:50
  78.0 6.3 %collective-permute-done.2 = bf16[1,320,512]{2,1,0:T(8,128)(2,1)S(1)} collective-permute-done((bf16[1,320,512]{2,1,0:T(8,128)(2,1)S(1)}, bf16[1,320,512]{2,1,0:T(8,128)(2,1)S(1)}, u32[]{:S(2)}, u32[]{:S(2)}) %collective-permute-start.2) | collective-permute-done | bytes 327712 | tf_op jit(solution)/shard_map/ppermute | solution.py:50
  84.2 5.1 %collective-permute-done.3 = bf16[1,320,512]{2,1,0:T(8,128)(2,1)S(1)} collective-permute-done((bf16[1,320,512]{2,1,0:T(8,128)(2,1)S(1)}, bf16[1,320,512]{2,1,0:T(8,128)(2,1)S(1)}, u32[]{:S(2)}, u32[]{:S(2)}) %collective-permute-start.3) | collective-permute-done | bytes 327712 | tf_op jit(solution)/shard_map/ppermute | solution.py:50
  90.1 1.5 %fusion.3 = f32[640,192]{0,1:T(8,128)S(1)} fusion(f32[640,192]{0,1:T(8,128)S(1)} %fusion.18, f32[640,192]{0,1:T(8,128)S(1)} %convolution_add_fusion.3, bf16[1,640,512]{2,1,0:T(8,128)(2,1)} %collective-permute-done.1, bf16[1,2048,192]{1,2,0:T(8,128)(2,1)S(1)} %copy-done.1, s32[]{:T(128)S(6)} %select_n.61), kind=kOutput, calls=%fused_computation.8 | convolution fusion | flops 126074880 | bytes 2326532 | tf_op jit(solution)/shard_map/end,edf->enf/dot_general | solution.py:73
  91.6 1.5 %fusion.8 = bf16[1,192,640]{2,1,0:T(8,128)(2,1)S(1)} fusion(f32[640,192]{0,1:T(8,128)S(1)} %fusion.17, f32[640,192]{0,1:T(8,128)S(1)} %convolution_add_fusion.1, bf16[1,640,512]{2,1,0:T(8,128)(2,1)} %collective-permute-done.1, f32[640,192]{0,1:T(8,128)S(1)} %fusion.3, bf16[1,2048,192]{1,2,0:T(8,128)(2,1)S(1)} %copy-done.2, s32[]{:T(128)S(6)} %select_n.61), kind=kOutput, calls=%fused_computation.15 | convolution fusion | flops 126812160 | bytes 2572292 | tf_op jit(solution)/shard_map/end,edf->enf/dot_general | solution.py:74
  93.1 10.9 %all-gather = bf16[4,192,640]{2,1,0:T(8,128)(2,1)S(1)} all-gather(bf16[1,192,640]{2,1,0:T(8,128)(2,1)S(1)} %fusion.8), channel_id=2, replica_groups=mesh['dp'=64,'tensor'=4,'sect'=2] {'tensor'}, dimensions={0}, use_global_device_ids=true | all-gather | bytes 1228800 | tf_op jit(solution)/shard_map/all_gather | solution.py:125
  103.9 2.1 %convert_reduce_fusion = bf16[640,512]{1,0:T(8,128)(2,1)S(1)} fusion(bf16[4,192,640]{2,1,0:T(8,128)(2,1)S(1)} %all-gather, bf16[4,1,192,512]{3,2,1,0:T(8,128)(2,1)} %all-to-all-done.1), kind=kOutput, calls=%fused_computation.1 | convolution fusion | flops 505610240 | bytes 2424832 | tf_op jit(solution)/shard_map/gefn,gefc->genc/dot_general | solution.py:126
  106.1 1.4 reshape_transpose_reshape.7
  107.5 10.5 %all-to-all-start.2 = ((bf16[128,20,128]{2,1,0:T(8,128)(2,1)}), bf16[128,20,128]{2,1,0:T(8,128)(2,1)S(1)}, u32[]{:S(2)}, u32[]{:S(2)}) async-start(bf16[128,20,128]{2,1,0:T(8,128)(2,1)} %reshape_transpose_reshape.7), calls=%async_computation.2 | async-start | bytes 1572864 | tf_op jit(solution)/shard_map/all_to_all | solution.py:131
  119.0 2.8 %convolution_convert_fusion.1 = bf16[32,16,128]{2,1,0:T(8,128)(2,1)} fusion(bf16[32,128,1,128]{3,1,2,0:T(8,128)(2,1)} %param.18, f32[32,16]{1,0:T(8,128)S(1)} %fusion.55, f32[32,16,128]{2,1,0:T(8,128)S(1)} %fusion.7), kind=kOutput, calls=%fused_computation.16 | convolution fusion | flops 17040000 | bytes 1443840 | tf_op jit(solution)/shard_map/rkgl,rlkd->rkgd/dot_general | solution.py:45
  122.5 21.5 %all-to-all-done.2 = bf16[128,20,128]{2,1,0:T(8,128)(2,1)S(1)} async-done(((bf16[128,20,128]{2,1,0:T(8,128)(2,1)}), bf16[128,20,128]{2,1,0:T(8,128)(2,1)S(1)}, u32[]{:S(2)}, u32[]{:S(2)}) %all-to-all-start.2) | async-done | bytes 655392 | tf_op jit(solution)/shard_map/all_to_all | solution.py:131
  (51 shorter events, 7.7 us)
Async XLA Ops:
  0.6 117.5 %copy-start = (bf16[32,128,1,128]{3,1,2,0:T(8,128)(2,1)S(1)}, bf16[32,128,1,128]{3,1,2,0:T(8,128)(2,1)}, u32[]{:S(2)}) copy-start(bf16[32,128,1,128]{3,1,2,0:T(8,128)(2,1)} %param.17) | copy-start | bytes 3145732
  1.5 1.0 copy-start.4
  4.3 44.4 %all-to-all-start = ((bf16[128,20,128]{2,1,0:T(8,128)(2,1)}), bf16[128,20,128]{2,1,0:T(8,128)(2,1)S(1)}, u32[]{:S(2)}, u32[]{:S(2)}) async-start(bf16[128,20,128]{2,1,0:T(8,128)(2,1)} %reshape.151), calls=%async_computation | async-start | bytes 1572864 | tf_op jit(solution)/shard_map/all_to_all | solution.py:102
  50.0 18.9 %collective-permute-start.1 = (bf16[1,640,512]{2,1,0:T(8,128)(2,1)}, bf16[1,640,512]{2,1,0:T(8,128)(2,1)}, u32[]{:S(2)}, u32[]{:S(2)}) collective-permute-start(bf16[1,640,512]{2,1,0:T(8,128)(2,1)} %reshape_transpose_reshape.6), channel_id=1, source_target_pairs={{0,6},{2,0},{4,2},{6,4},{1,7},{3,1},{5,3},{7,5},{8,14},{10,8},{12,... | collective-permute-start | bytes 1966088 | tf_op jit(solution)/shard_map/ppermute | solution.py:50
  54.4 20.9 %collective-permute-start = (bf16[1,640,512]{2,1,0:T(8,128)(2,1)}, bf16[1,640,512]{2,1,0:T(8,128)(2,1)S(1)}, u32[]{:S(2)}, u32[]{:S(2)}) collective-permute-start(bf16[1,640,512]{2,1,0:T(8,128)(2,1)} %reshape_transpose_reshape.6), channel_id=1, source_target_pairs={{0,2},{2,4},{4,6},{6,0},{1,3},{3,5},{5,7},{7,1},{8,10},{10,12},{12... | collective-permute-start | bytes 1966088 | tf_op jit(solution)/shard_map/ppermute | solution.py:50
  59.6 44.3 %all-to-all-start.1 = ((bf16[4,1,192,512]{3,2,1,0:T(8,128)(2,1)}), bf16[4,1,192,512]{3,2,1,0:T(8,128)(2,1)}, u32[]{:S(2)}, u32[]{:S(2)}) async-start(bf16[4,1,192,512]{3,2,1,0:T(8,128)(2,1)} %copy.33), calls=%async_computation.1 | async-start | bytes 1572864 | tf_op jit(solution)/shard_map/all_to_all | solution.py:118
  64.4 1.4 copy-start.1
  65.8 11.4 %copy-start.2 = (bf16[1,2048,192]{1,2,0:T(8,128)(2,1)S(1)}, bf16[1,2048,192]{1,2,0:T(8,128)(2,1)}, u32[]{:S(2)}) copy-start(bf16[1,2048,192]{1,2,0:T(8,128)(2,1)} %param.14) | copy-start | bytes 2359300
  69.9 14.3 %collective-permute-start.2 = (bf16[1,320,512]{2,1,0:T(8,128)(2,1)S(1)}, bf16[1,320,512]{2,1,0:T(8,128)(2,1)S(1)}, u32[]{:S(2)}, u32[]{:S(2)}) collective-permute-start(bf16[1,320,512]{2,1,0:T(8,128)(2,1)S(1)} %slice.8), channel_id=1, source_target_pairs={{0,6},{2,0},{4,2},{6,4},{1,7},{3,1},{5,3},{7,5},{8,14},{10,8},{12,... | collective-permute-start | bytes 983048 | tf_op jit(solution)/shard_map/ppermute | solution.py:50
  75.3 14.1 %collective-permute-start.3 = (bf16[1,320,512]{2,1,0:T(8,128)(2,1)S(1)}, bf16[1,320,512]{2,1,0:T(8,128)(2,1)S(1)}, u32[]{:S(2)}, u32[]{:S(2)}) collective-permute-start(bf16[1,320,512]{2,1,0:T(8,128)(2,1)S(1)} %slice.9), channel_id=1, source_target_pairs={{0,2},{2,4},{4,6},{6,0},{1,3},{3,5},{5,7},{7,1},{8,10},{10,12},{12... | collective-permute-start | bytes 983048 | tf_op jit(solution)/shard_map/ppermute | solution.py:50
  107.5 10.5 %copy-start.7 = (s32[32]{0:T(128)S(1)}, s32[32]{0:T(128)}, u32[]{:S(2)}) copy-start(s32[32]{0:T(128)} %param.19) | copy-start | bytes 388
  107.5 10.6 %copy-start.3 = (bf16[32,16,128]{2,1,0:T(8,128)(2,1)S(1)}, bf16[32,16,128]{2,1,0:T(8,128)(2,1)}, u32[]{:S(2)}) copy-start(bf16[32,16,128]{2,1,0:T(8,128)(2,1)} %param.16) | copy-start | bytes 393220
  107.5 36.6 %all-to-all-start.2 = ((bf16[128,20,128]{2,1,0:T(8,128)(2,1)}), bf16[128,20,128]{2,1,0:T(8,128)(2,1)S(1)}, u32[]{:S(2)}, u32[]{:S(2)}) async-start(bf16[128,20,128]{2,1,0:T(8,128)(2,1)} %reshape_transpose_reshape.7), calls=%async_computation.2 | async-start | bytes 1572864 | tf_op jit(solution)/shard_map/all_to_all | solution.py:131
  118.7 3.1 %copy-start.6 = (f32[32,8]{0,1:T(8,128)S(1)}, f32[32,8]{0,1:T(8,128)}, u32[]{:S(2)}) copy-start(f32[32,8]{0,1:T(8,128)} %param.12) | copy-start | bytes 3076
  118.7 3.2 %copy-start.5 = (s32[32,8]{0,1:T(8,128)S(1)}, s32[32,8]{0,1:T(8,128)}, u32[]{:S(2)}) copy-start(s32[32,8]{0,1:T(8,128)} %param.11) | copy-start | bytes 3076

commit v10 on v9

--- a/solution.py
+++ b/solution.py
@@ -77,6 +77,48 @@
     return gate, up
 
 
+def split_down(down_weight, count):
+    width = down_weight.shape[2] // count
+    if count != 4:
+        return lax.all_to_all(
+            down_weight.reshape(down_weight.shape[0], down_weight.shape[1], count, width)
+            .transpose(2, 0, 1, 3),
+            "tensor",
+            split_axis=0,
+            concat_axis=0,
+            tiled=True,
+        )
+    me = lax.axis_index("tensor")
+
+    def columns(offset):
+        start = ((me + offset) % count) * width
+        return lax.dynamic_slice_in_dim(down_weight, start, width, axis=2)
+
+    return (
+        columns(0),
+        shifted(columns(1), 1, count),
+        shifted(columns(count - 1), -1, count),
+        shifted(columns(2), 2, count),
+    )
+
+
+def down_projection(hidden_t, down_pieces, count):
+    hidden_all = lax.all_gather(hidden_t, "tensor", axis=0, tiled=False)
+    if count != 4:
+        group_sums = jnp.einsum(
+            "gefn,gefc->genc", hidden_all, down_pieces, preferred_element_type=jnp.float32
+        ).astype(jnp.bfloat16)
+        return jnp.sum(group_sums.astype(jnp.float32), axis=0).astype(jnp.bfloat16)
+    me = lax.axis_index("tensor")
+    total = None
+    for offset, weight in zip((0, count - 1, 1, 2), down_pieces):
+        piece = lax.dynamic_index_in_dim(hidden_all, (me + offset) % count, axis=0, keepdims=False)
+        group = jnp.einsum("efn,efc->enc", piece, weight, preferred_element_type=jnp.float32)
+        group = group.astype(jnp.bfloat16).astype(jnp.float32)
+        total = group if total is None else total + group
+    return total.astype(jnp.bfloat16)
+
+
 def local(
     tokens,
     route_experts,
@@ -99,9 +141,10 @@
     width = local_buffer.shape[1]
     lanes = 128
     local_buffer = local_buffer.reshape(owners, per_owner * width // lanes, lanes)
+    down_pieces = split_down(down_weight, lax.axis_size("tensor"))
     arrived = lax.all_to_all(local_buffer, ("dp", "sect"), split_axis=0, concat_axis=0, tiled=True)
-    arrived, late_ids, late_weights, late_hit = lax.optimization_barrier(
-        (arrived, route_experts, route_weights, hit)
+    arrived, late_ids, late_weights, late_hit, down_pieces = lax.optimization_barrier(
+        (arrived, route_experts, route_weights, hit, down_pieces)
     )
     combine = route_combine(late_ids, late_weights, late_hit, EXPERTS, CAP)
     own_experts = gate_weight.shape[0]
@@ -114,19 +157,7 @@
     hidden_width = gate_weight.shape[2]
     gate_part, up_part = ring_projections(inputs, gate_weight, up_weight, pieces)
     hidden = (jax.nn.silu(gate_part) * up_part).astype(jnp.bfloat16)
-    out_width = down_weight.shape[2] // pieces
-    down_mine = lax.all_to_all(
-        down_weight.reshape(own_experts, hidden_width, pieces, out_width).transpose(2, 0, 1, 3),
-        "tensor",
-        split_axis=0,
-        concat_axis=0,
-        tiled=True,
-    )
-    hidden_all = lax.all_gather(hidden.transpose(0, 2, 1), "tensor", axis=0, tiled=False)
-    group_sums = jnp.einsum(
-        "gefn,gefc->genc", hidden_all, down_mine, preferred_element_type=jnp.float32
-    ).astype(jnp.bfloat16)
-    summed = jnp.sum(group_sums.astype(jnp.float32), axis=0).astype(jnp.bfloat16)
+    summed = down_projection(hidden.transpose(0, 2, 1), down_pieces, pieces)
     last = summed.shape[2]
     returned = lax.all_to_all(
         summed.reshape(own_experts, owners, CAP, last)

time: 146 us -> 144 us (0.986)
  starting transfers between devices: 46.7 us -> 52.1 us
  waiting for transfers between devices: 61.3 us -> 58.3 us
  matrix products: 13.3 us -> 10.4 us
  local copies, waits for them, and re-layouts: 11.5 us -> 9.33 us
    all_to_all x1, waiting for transfers between devices: 25.8 us -> 10.9 us  [local(): lax.all_to_all(local_buffer, ('dp', 'sect'), split_axis=0, concat_axis=0,...]
    ppermute x4 -> x7, waiting for transfers between devices: 14 us -> 24.6 us  [shifted(): lax.ppermute(x, 'tensor', perm=[(i, (i + step) % count) for i in range(co...]
    ppermute x4 -> x7, starting transfers between devices: 13.5 us -> 23.6 us  [shifted(): lax.ppermute(x, 'tensor', perm=[(i, (i + step) % count) for i in range(co...]
    all_to_all x1 -> x0, starting transfers between devices: 4.19 us -> none  [local(): lax.all_to_all(down_weight.reshape(own_experts, hidden_width, pieces, out...]
    reshape x2 -> x1, local copies, waits for them, and re-layouts: 2.82 us -> 0.52 us  [the longest x1 2.29 us: local(): down_weight.reshape(own_experts, hidden_width, pieces, out_width)]
  transfers between devices with their start and end apart: 7 -> 9, of which waited for: 5 -> 7; matrix products, arithmetic and copies ran while one was open for 11% -> 5% of each run, Pallas kernels for 0% -> 0%
where the time goes in v10:
time: 144 us; the launch traced here: 143 us
  waiting for transfers between devices  58.3 us (40%)
  starting transfers between devices  52.1 us (36%)
  blocking collectives  11.3 us (8%)
  matrix products  10.4 us (7%)
  local copies, waits for them, and re-layouts  9.33 us (6%)
    ppermute x7, waiting for transfers between devices, shifted(): lax.ppermute(x, 'tensor', perm=[(i, (i + step) % count) for i in range(co...  24.6 us
    ppermute x7, starting transfers between devices, shifted(): lax.ppermute(x, 'tensor', perm=[(i, (i + step) % count) for i in range(co...  23.6 us
    all_to_all x1, waiting for transfers between devices, local(): lax.all_to_all(summed.reshape(own_experts, owners, CAP, last).transpose(1...  22.7 us
    all_to_all x1, starting transfers between devices, local(): lax.all_to_all(local_buffer, ('dp', 'sect'), split_axis=0, concat_axis=0,...  18.4 us
    all_gather x1, blocking collectives, down_projection(): hidden_all = lax.all_gather(hidden_t, 'tensor', axis=0, tiled=False)  11.3 us
    all_to_all x1, waiting for transfers between devices, local(): lax.all_to_all(local_buffer, ('dp', 'sect'), split_axis=0, concat_axis=0,...  10.9 us
    all_to_all x1, starting transfers between devices, local(): lax.all_to_all(summed.reshape(own_experts, owners, CAP, last).transpose(1...  10.1 us
  transfers between devices with their start and end apart: 9, of which 7 were waited for; matrix products, arithmetic and copies ran while one was open for 5% of the time, Pallas kernels for 0%

profile of v10, /device:TPU:1, one launch (start us, length us, event | category | flops | bytes accessed | tf_op | source)
XLA Modules:
  0.0 143.4 jit_solution(9265957689440882720)
XLA Ops:
  2.9 1.4 reshape.183
  4.3 18.4 %all-to-all-start = ((bf16[128,20,128]{2,1,0:T(8,128)(2,1)}), bf16[128,20,128]{2,1,0:T(8,128)(2,1)S(1)}, u32[]{:S(2)}, u32[]{:S(2)}) async-start(bf16[128,20,128]{2,1,0:T(8,128)(2,1)} %reshape.183), calls=%async_computation | async-start | bytes 1572864 | tf_op jit(solution)/shard_map/all_to_all | solution.py:145
  22.9 3.1 %collective-permute-start = (bf16[1,192,512]{2,1,0:T(8,128)(2,1)S(1)}, bf16[1,192,512]{2,1,0:T(8,128)(2,1)S(1)}, u32[]{:S(2)}, u32[]{:S(2)}) collective-permute-start(bf16[1,192,512]{2,1,0:T(8,128)(2,1)S(1)} %get-tuple-element.19), channel_id=1, source_target_pairs={{0,2},{2,4},{4,6},{6,0},{1,3},{3,5},{5,7},{7,1},{8,10},{10,12},{12... | collective-permute-start | bytes 589832 | tf_op jit(solution)/shard_map/ppermute | solution.py:50
  26.0 3.4 %collective-permute-start.1 = (bf16[1,192,512]{2,1,0:T(8,128)(2,1)S(1)}, bf16[1,192,512]{2,1,0:T(8,128)(2,1)S(1)}, u32[]{:S(2)}, u32[]{:S(2)}) collective-permute-start(bf16[1,192,512]{2,1,0:T(8,128)(2,1)S(1)} %get-tuple-element.21), channel_id=1, source_target_pairs={{0,6},{2,0},{4,2},{6,4},{1,7},{3,1},{5,3},{7,5},{8,14},{10,8},{12,... | collective-permute-start | bytes 589832 | tf_op jit(solution)/shard_map/ppermute | solution.py:50
  29.4 3.4 %collective-permute-start.2 = (bf16[1,192,512]{2,1,0:T(8,128)(2,1)S(1)}, bf16[1,192,512]{2,1,0:T(8,128)(2,1)S(1)}, u32[]{:S(2)}, u32[]{:S(2)}) collective-permute-start(bf16[1,192,512]{2,1,0:T(8,128)(2,1)S(1)} %get-tuple-element.18), channel_id=1, source_target_pairs={{0,4},{2,6},{4,0},{6,2},{1,5},{3,7},{5,1},{7,3},{8,12},{10,14},{12... | collective-permute-start | bytes 589832 | tf_op jit(solution)/shard_map/ppermute | solution.py:50
  33.1 4.6 %collective-permute-done.2 = bf16[1,192,512]{2,1,0:T(8,128)(2,1)S(1)} collective-permute-done((bf16[1,192,512]{2,1,0:T(8,128)(2,1)S(1)}, bf16[1,192,512]{2,1,0:T(8,128)(2,1)S(1)}, u32[]{:S(2)}, u32[]{:S(2)}) %collective-permute-start.2) | collective-permute-done | bytes 196640 | tf_op jit(solution)/shard_map/ppermute | solution.py:50
  37.7 10.9 %all-to-all-done = bf16[128,20,128]{2,1,0:T(8,128)(2,1)S(1)} async-done(((bf16[128,20,128]{2,1,0:T(8,128)(2,1)}), bf16[128,20,128]{2,1,0:T(8,128)(2,1)S(1)}, u32[]{:S(2)}, u32[]{:S(2)}) %all-to-all-start) | async-done | bytes 655392 | tf_op jit(solution)/shard_map/all_to_all | solution.py:145
  48.6 1.4 reshape_transpose_reshape.6
  50.0 4.4 %collective-permute-start.4 = (bf16[1,640,512]{2,1,0:T(8,128)(2,1)}, bf16[1,640,512]{2,1,0:T(8,128)(2,1)}, u32[]{:S(2)}, u32[]{:S(2)}) collective-permute-start(bf16[1,640,512]{2,1,0:T(8,128)(2,1)} %reshape_transpose_reshape.6), channel_id=1, source_target_pairs={{0,6},{2,0},{4,2},{6,4},{1,7},{3,1},{5,3},{7,5},{8,14},{10,8},{12,... | collective-permute-start | bytes 1966088 | tf_op jit(solution)/shard_map/ppermute | solution.py:50
  54.4 1.9 %collective-permute-start.3 = (bf16[1,640,512]{2,1,0:T(8,128)(2,1)}, bf16[1,640,512]{2,1,0:T(8,128)(2,1)S(1)}, u32[]{:S(2)}, u32[]{:S(2)}) collective-permute-start(bf16[1,640,512]{2,1,0:T(8,128)(2,1)} %reshape_transpose_reshape.6), channel_id=1, source_target_pairs={{0,2},{2,4},{4,6},{6,0},{1,3},{3,5},{5,7},{7,1},{8,10},{10,12},{12... | collective-permute-start | bytes 1966088 | tf_op jit(solution)/shard_map/ppermute | solution.py:50
  56.9 12.0 %collective-permute-done.4 = bf16[1,640,512]{2,1,0:T(8,128)(2,1)} collective-permute-done((bf16[1,640,512]{2,1,0:T(8,128)(2,1)}, bf16[1,640,512]{2,1,0:T(8,128)(2,1)}, u32[]{:S(2)}, u32[]{:S(2)}) %collective-permute-start.4) | collective-permute-done | bytes 655392 | tf_op jit(solution)/shard_map/ppermute | solution.py:50
  68.9 1.0 slice.8
  69.9 5.3 %collective-permute-start.5 = (bf16[1,320,512]{2,1,0:T(8,128)(2,1)S(1)}, bf16[1,320,512]{2,1,0:T(8,128)(2,1)S(1)}, u32[]{:S(2)}, u32[]{:S(2)}) collective-permute-start(bf16[1,320,512]{2,1,0:T(8,128)(2,1)S(1)} %slice.8), channel_id=1, source_target_pairs={{0,6},{2,0},{4,2},{6,4},{1,7},{3,1},{5,3},{7,5},{8,14},{10,8},{12,... | collective-permute-start | bytes 983048 | tf_op jit(solution)/shard_map/ppermute | solution.py:50
  75.3 2.1 %collective-permute-start.6 = (bf16[1,320,512]{2,1,0:T(8,128)(2,1)S(1)}, bf16[1,320,512]{2,1,0:T(8,128)(2,1)S(1)}, u32[]{:S(2)}, u32[]{:S(2)}) collective-permute-start(bf16[1,320,512]{2,1,0:T(8,128)(2,1)S(1)} %slice.9), channel_id=1, source_target_pairs={{0,2},{2,4},{4,6},{6,0},{1,3},{3,5},{5,7},{7,1},{8,10},{10,12},{12... | collective-permute-start | bytes 983048 | tf_op jit(solution)/shard_map/ppermute | solution.py:50
  78.9 2.6 %collective-permute-done.5 = bf16[1,320,512]{2,1,0:T(8,128)(2,1)S(1)} collective-permute-done((bf16[1,320,512]{2,1,0:T(8,128)(2,1)S(1)}, bf16[1,320,512]{2,1,0:T(8,128)(2,1)S(1)}, u32[]{:S(2)}, u32[]{:S(2)}) %collective-permute-start.5) | collective-permute-done | bytes 327712 | tf_op jit(solution)/shard_map/ppermute | solution.py:50
  81.6 5.2 %collective-permute-done.6 = bf16[1,320,512]{2,1,0:T(8,128)(2,1)S(1)} collective-permute-done((bf16[1,320,512]{2,1,0:T(8,128)(2,1)S(1)}, bf16[1,320,512]{2,1,0:T(8,128)(2,1)S(1)}, u32[]{:S(2)}, u32[]{:S(2)}) %collective-permute-start.6) | collective-permute-done | bytes 327712 | tf_op jit(solution)/shard_map/ppermute | solution.py:50
  87.5 1.5 %fusion.11 = f32[640,192]{0,1:T(8,128)S(1)} fusion(f32[640,192]{0,1:T(8,128)S(1)} %fusion.27, f32[640,192]{0,1:T(8,128)S(1)} %convolution_add_fusion.3, bf16[1,640,512]{2,1,0:T(8,128)(2,1)} %collective-permute-done.4, bf16[1,2048,192]{1,2,0:T(8,128)(2,1)S(1)} %copy-done.2, s32[]{:T(128)S(6)} %select_n.90), kind=kOutput, calls=%fused_computation.19 | convolution fusion | flops 126074880 | bytes 2326532 | tf_op jit(solution)/shard_map/end,edf->enf/dot_general | solution.py:73
  89.0 1.5 %fusion.16 = bf16[1,192,640]{2,1,0:T(8,128)(2,1)S(1)} fusion(f32[640,192]{0,1:T(8,128)S(1)} %fusion.26, f32[640,192]{0,1:T(8,128)S(1)} %convolution_add_fusion.1, bf16[1,640,512]{2,1,0:T(8,128)(2,1)} %collective-permute-done.4, f32[640,192]{0,1:T(8,128)S(1)} %fusion.11, bf16[1,2048,192]{1,2,0:T(8,128)(2,1)S(1)} %copy-done.7, s32[]{:T(128)S(6)} %select_n.90), kind=kOutput, calls=%fused_computation.26 | convolution fusion | flops 126812160 | bytes 2572292 | tf_op jit(solution)/shard_map/end,edf->enf/dot_general | solution.py:74
  90.6 11.3 %all-gather = bf16[4,192,640]{2,1,0:T(8,128)(2,1)S(1)} all-gather(bf16[1,192,640]{2,1,0:T(8,128)(2,1)S(1)} %fusion.16), channel_id=2, replica_groups=mesh['dp'=64,'tensor'=4,'sect'=2] {'tensor'}, dimensions={0}, use_global_device_ids=true | all-gather | bytes 1228800 | tf_op jit(solution)/shard_map/all_gather | solution.py:106
  104.5 1.4 reshape_transpose_reshape.7
  105.9 10.1 %all-to-all-start.1 = ((bf16[128,20,128]{2,1,0:T(8,128)(2,1)}), bf16[128,20,128]{2,1,0:T(8,128)(2,1)S(1)}, u32[]{:S(2)}, u32[]{:S(2)}) async-start(bf16[128,20,128]{2,1,0:T(8,128)(2,1)} %reshape_transpose_reshape.7), calls=%async_computation.1 | async-start | bytes 1572864 | tf_op jit(solution)/shard_map/all_to_all | solution.py:162
  116.9 1.6 %convolution_convert_fusion.5 = bf16[32,16,128]{2,1,0:T(8,128)(2,1)} fusion(bf16[32,128,1,128]{3,1,2,0:T(8,128)(2,1)S(1)} %copy-done.15, f32[32,16]{1,0:T(8,128)S(1)} %fusion.78, f32[32,16,128]{2,1,0:T(8,128)S(1)} %fusion.15), kind=kOutput, calls=%fused_computation.27 | convolution fusion | flops 17040000 | bytes 1443840 | tf_op jit(solution)/shard_map/rkgl,rlkd->rkgd/dot_general | solution.py:45
  119.2 22.7 %all-to-all-done.1 = bf16[128,20,128]{2,1,0:T(8,128)(2,1)S(1)} async-done(((bf16[128,20,128]{2,1,0:T(8,128)(2,1)}), bf16[128,20,128]{2,1,0:T(8,128)(2,1)S(1)}, u32[]{:S(2)}, u32[]{:S(2)}) %all-to-all-start.1) | async-done | bytes 655392 | tf_op jit(solution)/shard_map/all_to_all | solution.py:162
  142.5 0.9 convolution_convert_fusion.6
  (73 shorter events, 10.1 us)
Async XLA Ops:
  0.6 115.4 %copy-start = (bf16[32,128,1,128]{3,1,2,0:T(8,128)(2,1)S(1)}, bf16[32,128,1,128]{3,1,2,0:T(8,128)(2,1)}, u32[]{:S(2)}) copy-start(bf16[32,128,1,128]{3,1,2,0:T(8,128)(2,1)} %param.17) | copy-start | bytes 3145732
  0.6 1.8 %copy-start.11 = (bf16[32,512]{1,0:T(8,128)(2,1)S(1)}, bf16[32,512]{1,0:T(8,128)(2,1)}, u32[]{:S(2)}) copy-start(bf16[32,512]{1,0:T(8,128)(2,1)} %param.10) | copy-start | bytes 98308
  2.9 19.9 %copy-start.1 = (bf16[1,192,2048]{2,1,0:T(8,128)(2,1)S(1)}, bf16[1,192,2048]{2,1,0:T(8,128)(2,1)}, u32[]{:S(2)}) copy-start(bf16[1,192,2048]{2,1,0:T(8,128)(2,1)} %param.15) | copy-start | bytes 2359300
  4.3 44.3 %all-to-all-start = ((bf16[128,20,128]{2,1,0:T(8,128)(2,1)}), bf16[128,20,128]{2,1,0:T(8,128)(2,1)S(1)}, u32[]{:S(2)}, u32[]{:S(2)}) async-start(bf16[128,20,128]{2,1,0:T(8,128)(2,1)} %reshape.183), calls=%async_computation | async-start | bytes 1572864 | tf_op jit(solution)/shard_map/all_to_all | solution.py:145
  22.9 10.1 %collective-permute-start = (bf16[1,192,512]{2,1,0:T(8,128)(2,1)S(1)}, bf16[1,192,512]{2,1,0:T(8,128)(2,1)S(1)}, u32[]{:S(2)}, u32[]{:S(2)}) collective-permute-start(bf16[1,192,512]{2,1,0:T(8,128)(2,1)S(1)} %get-tuple-element.19), channel_id=1, source_target_pairs={{0,2},{2,4},{4,6},{6,0},{1,3},{3,5},{5,7},{7,1},{8,10},{10,12},{12... | collective-permute-start | bytes 589832 | tf_op jit(solution)/shard_map/ppermute | solution.py:50
  26.0 7.1 %collective-permute-start.1 = (bf16[1,192,512]{2,1,0:T(8,128)(2,1)S(1)}, bf16[1,192,512]{2,1,0:T(8,128)(2,1)S(1)}, u32[]{:S(2)}, u32[]{:S(2)}) collective-permute-start(bf16[1,192,512]{2,1,0:T(8,128)(2,1)S(1)} %get-tuple-element.21), channel_id=1, source_target_pairs={{0,6},{2,0},{4,2},{6,4},{1,7},{3,1},{5,3},{7,5},{8,14},{10,8},{12,... | collective-permute-start | bytes 589832 | tf_op jit(solution)/shard_map/ppermute | solution.py:50
  29.4 8.3 %collective-permute-start.2 = (bf16[1,192,512]{2,1,0:T(8,128)(2,1)S(1)}, bf16[1,192,512]{2,1,0:T(8,128)(2,1)S(1)}, u32[]{:S(2)}, u32[]{:S(2)}) collective-permute-start(bf16[1,192,512]{2,1,0:T(8,128)(2,1)S(1)} %get-tuple-element.18), channel_id=1, source_target_pairs={{0,4},{2,6},{4,0},{6,2},{1,5},{3,7},{5,1},{7,3},{8,12},{10,14},{12... | collective-permute-start | bytes 589832 | tf_op jit(solution)/shard_map/ppermute | solution.py:50
  33.0 17.0 %copy-start.3 = (bf16[1,192,512]{2,1,0:T(8,128)(2,1)}, bf16[1,192,512]{2,1,0:T(8,128)(2,1)S(1)}, u32[]{:S(2)}) copy-start(bf16[1,192,512]{2,1,0:T(8,128)(2,1)S(1)} %collective-permute-done) | copy-start | bytes 589828
  33.1 16.9 %copy-start.5 = (bf16[1,192,512]{2,1,0:T(8,128)(2,1)}, bf16[1,192,512]{2,1,0:T(8,128)(2,1)S(1)}, u32[]{:S(2)}) copy-start(bf16[1,192,512]{2,1,0:T(8,128)(2,1)S(1)} %collective-permute-done.1) | copy-start | bytes 589828
  37.7 18.6 %copy-start.8 = (bf16[1,192,512]{2,1,0:T(8,128)(2,1)}, bf16[1,192,512]{2,1,0:T(8,128)(2,1)S(1)}, u32[]{:S(2)}) copy-start(bf16[1,192,512]{2,1,0:T(8,128)(2,1)S(1)} %collective-permute-done.2) | copy-start | bytes 589828
  50.0 18.9 %collective-permute-start.4 = (bf16[1,640,512]{2,1,0:T(8,128)(2,1)}, bf16[1,640,512]{2,1,0:T(8,128)(2,1)}, u32[]{:S(2)}, u32[]{:S(2)}) collective-permute-start(bf16[1,640,512]{2,1,0:T(8,128)(2,1)} %reshape_transpose_reshape.6), channel_id=1, source_target_pairs={{0,6},{2,0},{4,2},{6,4},{1,7},{3,1},{5,3},{7,5},{8,14},{10,8},{12,... | collective-permute-start | bytes 1966088 | tf_op jit(solution)/shard_map/ppermute | solution.py:50
  54.4 20.9 %collective-permute-start.3 = (bf16[1,640,512]{2,1,0:T(8,128)(2,1)}, bf16[1,640,512]{2,1,0:T(8,128)(2,1)S(1)}, u32[]{:S(2)}, u32[]{:S(2)}) collective-permute-start(bf16[1,640,512]{2,1,0:T(8,128)(2,1)} %reshape_transpose_reshape.6), channel_id=1, source_target_pairs={{0,2},{2,4},{4,6},{6,0},{1,3},{3,5},{5,7},{7,1},{8,10},{10,12},{12... | collective-permute-start | bytes 1966088 | tf_op jit(solution)/shard_map/ppermute | solution.py:50
  56.9 20.5 %copy-start.2 = (bf16[1,2048,192]{1,2,0:T(8,128)(2,1)S(1)}, bf16[1,2048,192]{1,2,0:T(8,128)(2,1)}, u32[]{:S(2)}) copy-start(bf16[1,2048,192]{1,2,0:T(8,128)(2,1)} %param.13) | copy-start | bytes 2359300
  69.9 11.6 %collective-permute-start.5 = (bf16[1,320,512]{2,1,0:T(8,128)(2,1)S(1)}, bf16[1,320,512]{2,1,0:T(8,128)(2,1)S(1)}, u32[]{:S(2)}, u32[]{:S(2)}) collective-permute-start(bf16[1,320,512]{2,1,0:T(8,128)(2,1)S(1)} %slice.8), channel_id=1, source_target_pairs={{0,6},{2,0},{4,2},{6,4},{1,7},{3,1},{5,3},{7,5},{8,14},{10,8},{12,... | collective-permute-start | bytes 983048 | tf_op jit(solution)/shard_map/ppermute | solution.py:50
  75.3 2.9 %copy-start.7 = (bf16[1,2048,192]{1,2,0:T(8,128)(2,1)S(1)}, bf16[1,2048,192]{1,2,0:T(8,128)(2,1)}, u32[]{:S(2)}) copy-start(bf16[1,2048,192]{1,2,0:T(8,128)(2,1)} %param.14) | copy-start | bytes 2359300
  75.3 11.5 %collective-permute-start.6 = (bf16[1,320,512]{2,1,0:T(8,128)(2,1)S(1)}, bf16[1,320,512]{2,1,0:T(8,128)(2,1)S(1)}, u32[]{:S(2)}, u32[]{:S(2)}) collective-permute-start(bf16[1,320,512]{2,1,0:T(8,128)(2,1)S(1)} %slice.9), channel_id=1, source_target_pairs={{0,2},{2,4},{4,6},{6,0},{1,3},{3,5},{5,7},{7,1},{8,10},{10,12},{12... | collective-permute-start | bytes 983048 | tf_op jit(solution)/shard_map/ppermute | solution.py:50
  90.5 11.7 %copy-start.4 = (bf16[1,192,512]{2,1,0:T(8,128)(2,1)S(1)}, bf16[1,192,512]{2,1,0:T(8,128)(2,1)}, u32[]{:S(2)}) copy-start(bf16[1,192,512]{2,1,0:T(8,128)(2,1)} %copy-done.3) | copy-start | bytes 589828
  102.2 0.9 copy-start.6
  104.4 11.5 %copy-start.14 = (s32[32]{0:T(128)S(1)}, s32[32]{0:T(128)}, u32[]{:S(2)}) copy-start(s32[32]{0:T(128)} %param.19) | copy-start | bytes 388
  104.4 11.6 %copy-start.10 = (bf16[32,16,128]{2,1,0:T(8,128)(2,1)S(1)}, bf16[32,16,128]{2,1,0:T(8,128)(2,1)}, u32[]{:S(2)}) copy-start(bf16[32,16,128]{2,1,0:T(8,128)(2,1)} %param.16) | copy-start | bytes 393220
  105.9 11.1 %copy-start.15 = (bf16[32,128,1,128]{3,1,2,0:T(8,128)(2,1)S(1)}, bf16[32,128,1,128]{3,1,2,0:T(8,128)(2,1)}, u32[]{:S(2)}) copy-start(bf16[32,128,1,128]{3,1,2,0:T(8,128)(2,1)} %param.18) | copy-start | bytes 3145732
  105.9 36.1 %all-to-all-start.1 = ((bf16[128,20,128]{2,1,0:T(8,128)(2,1)}), bf16[128,20,128]{2,1,0:T(8,128)(2,1)S(1)}, u32[]{:S(2)}, u32[]{:S(2)}) async-start(bf16[128,20,128]{2,1,0:T(8,128)(2,1)} %reshape_transpose_reshape.7), calls=%async_computation.1 | async-start | bytes 1572864 | tf_op jit(solution)/shard_map/all_to_all | solution.py:162
  116.7 1.9 %copy-start.13 = (f32[32,8]{0,1:T(8,128)S(1)}, f32[32,8]{0,1:T(8,128)}, u32[]{:S(2)}) copy-start(f32[32,8]{0,1:T(8,128)} %param.12) | copy-start | bytes 3076
  116.7 2.0 %copy-start.12 = (s32[32,8]{0,1:T(8,128)S(1)}, s32[32,8]{0,1:T(8,128)}, u32[]{:S(2)}) copy-start(s32[32,8]{0,1:T(8,128)} %param.11) | copy-start | bytes 3076
  (1 other events, 0.9 us)

commit v11 on v10

--- a/solution.py
+++ b/solution.py
@@ -58,12 +58,13 @@
         up = jnp.einsum("end,edf->enf", gathered, up_weight, preferred_element_type=jnp.float32)
         return gate, up
     me = lax.axis_index("tensor")
-    from_left = shifted(inputs, 1, count)
-    from_right = shifted(inputs, -1, count)
     half = inputs.shape[1] // 2
-    far = jnp.concatenate(
-        [shifted(from_right[:, :half], -1, count), shifted(from_left[:, half:], 1, count)], axis=1
-    )
+    top, bottom = inputs[:, :half], inputs[:, half:]
+    right_top = shifted(top, -1, count)
+    left_bottom = shifted(bottom, 1, count)
+    from_left = jnp.concatenate([shifted(top, 1, count), left_bottom], axis=1)
+    from_right = jnp.concatenate([right_top, shifted(bottom, -1, count)], axis=1)
+    far = jnp.concatenate([shifted(right_top, -1, count), shifted(left_bottom, 1, count)], axis=1)
     gate = None
     up = None
     for piece, offset in ((inputs, 0), (from_left, count - 1), (from_right, 1), (far, 2)):

time: 144 us -> 140 us (0.972)
  waiting for transfers between devices: 58.3 us -> 47.8 us
  starting transfers between devices: 52.1 us -> 58.4 us
  local copies, waits for them, and re-layouts: 9.33 us -> 7.55 us
    ppermute x7 -> x9, waiting for transfers between devices: 24.6 us -> 14.1 us  [shifted(): lax.ppermute(x, 'tensor', perm=[(i, (i + step) % count) for i in range(co...]
    ppermute x7 -> x9, starting transfers between devices: 23.6 us -> 29.4 us  [shifted(): lax.ppermute(x, 'tensor', perm=[(i, (i + step) % count) for i in range(co...]
  transfers between devices with their start and end apart: 9 -> 11, of which waited for: 7 -> 8; matrix products, arithmetic and copies ran while one was open for 5% -> 7% of each run, Pallas kernels for 0% -> 0%
where the time goes in v11:
time: 140 us; the launch traced here: 139 us
  starting transfers between devices  58.4 us (42%)
  waiting for transfers between devices  47.8 us (34%)
  blocking collectives  11.9 us (8%)
  matrix products  11.4 us (8%)
  local copies, waits for them, and re-layouts  7.55 us (5%)
    ppermute x9, starting transfers between devices, shifted(): lax.ppermute(x, 'tensor', perm=[(i, (i + step) % count) for i in range(co...  29.4 us
    all_to_all x1, waiting for transfers between devices, local(): lax.all_to_all(summed.reshape(own_experts, owners, CAP, last).transpose(1...  22.7 us
    all_to_all x1, starting transfers between devices, local(): lax.all_to_all(local_buffer, ('dp', 'sect'), split_axis=0, concat_axis=0,...  18.4 us
    ppermute x9, waiting for transfers between devices, shifted(): lax.ppermute(x, 'tensor', perm=[(i, (i + step) % count) for i in range(co...  14.1 us
    all_gather x1, blocking collectives, down_projection(): hidden_all = lax.all_gather(hidden_t, 'tensor', axis=0, tiled=False)  11.9 us
    all_to_all x1, waiting for transfers between devices, local(): lax.all_to_all(local_buffer, ('dp', 'sect'), split_axis=0, concat_axis=0,...  10.9 us
    all_to_all x1, starting transfers between devices, local(): lax.all_to_all(summed.reshape(own_experts, owners, CAP, last).transpose(1...  10.6 us
    dot_general x4, matrix products, ring_projections(): jnp.einsum('end,edf->enf', piece, up_rows, preferred_element_type=jnp.flo...  3.57 us
  transfers between devices with their start and end apart: 11, of which 8 were waited for; matrix products, arithmetic and copies ran while one was open for 7% of the time, Pallas kernels for 0%

profile of v11, /device:TPU:1, one launch (start us, length us, event | category | flops | bytes accessed | tf_op | source)
XLA Modules:
  0.0 139.0 jit_solution(402091287416267894)
XLA Ops:
  2.9 1.4 %reshape.183 = bf16[128,20,128]{2,1,0:T(8,128)(2,1)} reshape(bf16[640,512]{1,0:T(8,128)(2,1)S(1)} %convolution_convert_fusion) | data formatting | bytes 1310720 | tf_op jit(solution)/shard_map/reshape | solution.py:144
  4.3 18.4 %all-to-all-start = ((bf16[128,20,128]{2,1,0:T(8,128)(2,1)}), bf16[128,20,128]{2,1,0:T(8,128)(2,1)S(1)}, u32[]{:S(2)}, u32[]{:S(2)}) async-start(bf16[128,20,128]{2,1,0:T(8,128)(2,1)} %reshape.183), calls=%async_computation | async-start | bytes 1572864 | tf_op jit(solution)/shard_map/all_to_all | solution.py:146
  22.9 3.1 %collective-permute-start = (bf16[1,192,512]{2,1,0:T(8,128)(2,1)S(1)}, bf16[1,192,512]{2,1,0:T(8,128)(2,1)S(1)}, u32[]{:S(2)}, u32[]{:S(2)}) collective-permute-start(bf16[1,192,512]{2,1,0:T(8,128)(2,1)S(1)} %get-tuple-element.19), channel_id=1, source_target_pairs={{0,2},{2,4},{4,6},{6,0},{1,3},{3,5},{5,7},{7,1},{8,10},{10,12},{12... | collective-permute-start | bytes 589832 | tf_op jit(solution)/shard_map/ppermute | solution.py:50
  26.0 3.4 %collective-permute-start.1 = (bf16[1,192,512]{2,1,0:T(8,128)(2,1)S(1)}, bf16[1,192,512]{2,1,0:T(8,128)(2,1)S(1)}, u32[]{:S(2)}, u32[]{:S(2)}) collective-permute-start(bf16[1,192,512]{2,1,0:T(8,128)(2,1)S(1)} %get-tuple-element.21), channel_id=1, source_target_pairs={{0,6},{2,0},{4,2},{6,4},{1,7},{3,1},{5,3},{7,5},{8,14},{10,8},{12,... | collective-permute-start | bytes 589832 | tf_op jit(solution)/shard_map/ppermute | solution.py:50
  29.4 3.4 %collective-permute-start.2 = (bf16[1,192,512]{2,1,0:T(8,128)(2,1)S(1)}, bf16[1,192,512]{2,1,0:T(8,128)(2,1)S(1)}, u32[]{:S(2)}, u32[]{:S(2)}) collective-permute-start(bf16[1,192,512]{2,1,0:T(8,128)(2,1)S(1)} %get-tuple-element.18), channel_id=1, source_target_pairs={{0,4},{2,6},{4,0},{6,2},{1,5},{3,7},{5,1},{7,3},{8,12},{10,14},{12... | collective-permute-start | bytes 589832 | tf_op jit(solution)/shard_map/ppermute | solution.py:50
  33.1 4.6 %collective-permute-done.2 = bf16[1,192,512]{2,1,0:T(8,128)(2,1)S(1)} collective-permute-done((bf16[1,192,512]{2,1,0:T(8,128)(2,1)S(1)}, bf16[1,192,512]{2,1,0:T(8,128)(2,1)S(1)}, u32[]{:S(2)}, u32[]{:S(2)}) %collective-permute-start.2) | collective-permute-done | bytes 196640 | tf_op jit(solution)/shard_map/ppermute | solution.py:50
  37.8 10.9 %all-to-all-done = bf16[128,20,128]{2,1,0:T(8,128)(2,1)S(1)} async-done(((bf16[128,20,128]{2,1,0:T(8,128)(2,1)}), bf16[128,20,128]{2,1,0:T(8,128)(2,1)S(1)}, u32[]{:S(2)}, u32[]{:S(2)}) %all-to-all-start) | async-done | bytes 655392 | tf_op jit(solution)/shard_map/all_to_all | solution.py:146
  49.3 3.1 %collective-permute-start.4 = (bf16[1,320,512]{2,1,0:T(8,128)(2,1)S(1)}, bf16[1,320,512]{2,1,0:T(8,128)(2,1)}, u32[]{:S(2)}, u32[]{:S(2)}) collective-permute-start(bf16[1,320,512]{2,1,0:T(8,128)(2,1)S(1)} %get-tuple-element.23), channel_id=1, source_target_pairs={{0,2},{2,4},{4,6},{6,0},{1,3},{3,5},{5,7},{7,1},{8,10},{10,12},{12... | collective-permute-start | bytes 983048 | tf_op jit(solution)/shard_map/ppermute | solution.py:50
  52.4 3.1 %collective-permute-start.3 = (bf16[1,320,512]{2,1,0:T(8,128)(2,1)S(1)}, bf16[1,320,512]{2,1,0:T(8,128)(2,1)}, u32[]{:S(2)}, u32[]{:S(2)}) collective-permute-start(bf16[1,320,512]{2,1,0:T(8,128)(2,1)S(1)} %get-tuple-element.22), channel_id=1, source_target_pairs={{0,2},{2,4},{4,6},{6,0},{1,3},{3,5},{5,7},{7,1},{8,10},{10,12},{12... | collective-permute-start | bytes 983048 | tf_op jit(solution)/shard_map/ppermute | solution.py:50
  56.1 3.5 %collective-permute-start.6 = (bf16[1,320,512]{2,1,0:T(8,128)(2,1)S(1)}, bf16[1,320,512]{2,1,0:T(8,128)(2,1)S(1)}, u32[]{:S(2)}, u32[]{:S(2)}) collective-permute-start(bf16[1,320,512]{2,1,0:T(8,128)(2,1)S(1)} %get-tuple-element.23), channel_id=1, source_target_pairs={{0,6},{2,0},{4,2},{6,4},{1,7},{3,1},{5,3},{7,5},{8,14},{10,8},{12,... | collective-permute-start | bytes 983048 | tf_op jit(solution)/shard_map/ppermute | solution.py:50
  59.6 2.2 %collective-permute-start.5 = (bf16[1,320,512]{2,1,0:T(8,128)(2,1)S(1)}, bf16[1,320,512]{2,1,0:T(8,128)(2,1)S(1)}, u32[]{:S(2)}, u32[]{:S(2)}) collective-permute-start(bf16[1,320,512]{2,1,0:T(8,128)(2,1)S(1)} %get-tuple-element.22), channel_id=1, source_target_pairs={{0,6},{2,0},{4,2},{6,4},{1,7},{3,1},{5,3},{7,5},{8,14},{10,8},{12,... | collective-permute-start | bytes 983048 | tf_op jit(solution)/shard_map/ppermute | solution.py:50
  61.9 3.0 %collective-permute-start.8 = (bf16[1,320,512]{2,1,0:T(8,128)(2,1)}, bf16[1,320,512]{2,1,0:T(8,128)(2,1)S(1)}, u32[]{:S(2)}, u32[]{:S(2)}) collective-permute-start(bf16[1,320,512]{2,1,0:T(8,128)(2,1)} %collective-permute-done.4), channel_id=1, source_target_pairs={{0,2},{2,4},{4,6},{6,0},{1,3},{3,5},{5,7},{7,1},{8,10},{10,12},{12... | collective-permute-start | bytes 983048 | tf_op jit(solution)/shard_map/ppermute | solution.py:50
  64.9 4.0 %collective-permute-done.3 = bf16[1,320,512]{2,1,0:T(8,128)(2,1)} collective-permute-done((bf16[1,320,512]{2,1,0:T(8,128)(2,1)S(1)}, bf16[1,320,512]{2,1,0:T(8,128)(2,1)}, u32[]{:S(2)}, u32[]{:S(2)}) %collective-permute-start.3) | collective-permute-done | bytes 327712 | tf_op jit(solution)/shard_map/ppermute | solution.py:50
  68.9 1.5 %fusion.18 = f32[640,192]{0,1:T(8,128)S(1)} fusion(bf16[1,320,512]{2,1,0:T(8,128)(2,1)} %collective-permute-done.4, bf16[1,320,512]{2,1,0:T(8,128)(2,1)} %collective-permute-done.3, bf16[1,2048,192]{1,2,0:T(8,128)(2,1)} %param.14, s32[]{:T(128)S(6)} %select_n.92), kind=kOutput, calls=%fused_computation.37 | convolution fusion | flops 127139840 | bytes 1343492 | tf_op jit(solution)/shard_map/end,edf->enf/dot_general | solution.py:75
  70.4 1.3 convolution_add_fusion.2
  71.8 1.5 %fusion.19 = f32[640,192]{0,1:T(8,128)S(1)} fusion(bf16[1,320,512]{2,1,0:T(8,128)(2,1)} %collective-permute-done.4, bf16[1,320,512]{2,1,0:T(8,128)(2,1)} %collective-permute-done.3, bf16[1,2048,192]{1,2,0:T(8,128)(2,1)S(1)} %copy-done.2, s32[]{:T(128)S(6)} %select_n.92), kind=kOutput, calls=%fused_computation.38 | convolution fusion | flops 127139840 | bytes 1343492 | tf_op jit(solution)/shard_map/end,edf->enf/dot_general | solution.py:74
  74.0 4.6 %collective-permute-start.7 = (bf16[1,320,512]{2,1,0:T(8,128)(2,1)S(1)}, bf16[1,320,512]{2,1,0:T(8,128)(2,1)S(1)}, u32[]{:S(2)}, u32[]{:S(2)}) collective-permute-start(bf16[1,320,512]{2,1,0:T(8,128)(2,1)S(1)} %collective-permute-done.5), channel_id=1, source_target_pairs={{0,6},{2,0},{4,2},{6,4},{1,7},{3,1},{5,3},{7,5},{8,14},{10,8},{12,... | collective-permute-start | bytes 983048 | tf_op jit(solution)/shard_map/ppermute | solution.py:50
  79.8 4.5 %collective-permute-done.7 = bf16[1,320,512]{2,1,0:T(8,128)(2,1)S(1)} collective-permute-done((bf16[1,320,512]{2,1,0:T(8,128)(2,1)S(1)}, bf16[1,320,512]{2,1,0:T(8,128)(2,1)S(1)}, u32[]{:S(2)}, u32[]{:S(2)}) %collective-permute-start.7) | collective-permute-done | bytes 327712 | tf_op jit(solution)/shard_map/ppermute | solution.py:50
  85.1 11.9 %all-gather = bf16[4,192,640]{2,1,0:T(8,128)(2,1)S(1)} all-gather(bf16[1,192,640]{2,1,0:T(8,128)(2,1)S(1)} %fusion.14), channel_id=2, replica_groups=mesh['dp'=64,'tensor'=4,'sect'=2] {'tensor'}, dimensions={0}, use_global_device_ids=true | all-gather | bytes 1228800 | tf_op jit(solution)/shard_map/all_gather | solution.py:107
  99.6 1.4 %reshape_transpose_reshape.7 = bf16[128,20,128]{2,1,0:T(8,128)(2,1)} reshape(bf16[640,512]{1,0:T(8,128)(2,1)S(1)} %fusion.3) | data formatting | bytes 1310720 | tf_op jit(solution)/shard_map/reshape;transpose;reshape | solution.py:166
  101.0 10.6 %all-to-all-start.1 = ((bf16[128,20,128]{2,1,0:T(8,128)(2,1)}), bf16[128,20,128]{2,1,0:T(8,128)(2,1)S(1)}, u32[]{:S(2)}, u32[]{:S(2)}) async-start(bf16[128,20,128]{2,1,0:T(8,128)(2,1)} %reshape_transpose_reshape.7), calls=%async_computation.1 | async-start | bytes 1572864 | tf_op jit(solution)/shard_map/all_to_all | solution.py:163
  112.6 1.6 %convolution_convert_fusion.5 = bf16[32,16,128]{2,1,0:T(8,128)(2,1)} fusion(bf16[32,128,1,128]{3,1,2,0:T(8,128)(2,1)S(1)} %copy-done.15, f32[32,16]{1,0:T(8,128)S(1)} %fusion.75, f32[32,16,128]{2,1,0:T(8,128)S(1)} %fusion.13), kind=kOutput, calls=%fused_computation.27 | convolution fusion | flops 17040000 | bytes 1443840 | tf_op jit(solution)/shard_map/rkgl,rlkd->rkgd/dot_general | solution.py:45
  114.9 22.7 %all-to-all-done.1 = bf16[128,20,128]{2,1,0:T(8,128)(2,1)S(1)} async-done(((bf16[128,20,128]{2,1,0:T(8,128)(2,1)}), bf16[128,20,128]{2,1,0:T(8,128)(2,1)S(1)}, u32[]{:S(2)}, u32[]{:S(2)}) %all-to-all-start.1) | async-done | bytes 655392 | tf_op jit(solution)/shard_map/all_to_all | solution.py:163
  138.2 0.9 convolution_convert_fusion.6
  (76 shorter events, 11.1 us)
Async XLA Ops:
  0.6 111.1 %copy-start = (bf16[32,128,1,128]{3,1,2,0:T(8,128)(2,1)S(1)}, bf16[32,128,1,128]{3,1,2,0:T(8,128)(2,1)}, u32[]{:S(2)}) copy-start(bf16[32,128,1,128]{3,1,2,0:T(8,128)(2,1)} %param.17) | copy-start | bytes 3145732
  2.9 19.9 %copy-start.1 = (bf16[1,192,2048]{2,1,0:T(8,128)(2,1)S(1)}, bf16[1,192,2048]{2,1,0:T(8,128)(2,1)}, u32[]{:S(2)}) copy-start(bf16[1,192,2048]{2,1,0:T(8,128)(2,1)} %param.15) | copy-start | bytes 2359300
  4.3 44.4 %all-to-all-start = ((bf16[128,20,128]{2,1,0:T(8,128)(2,1)}), bf16[128,20,128]{2,1,0:T(8,128)(2,1)S(1)}, u32[]{:S(2)}, u32[]{:S(2)}) async-start(bf16[128,20,128]{2,1,0:T(8,128)(2,1)} %reshape.183), calls=%async_computation | async-start | bytes 1572864 | tf_op jit(solution)/shard_map/all_to_all | solution.py:146
  22.9 10.1 %collective-permute-start = (bf16[1,192,512]{2,1,0:T(8,128)(2,1)S(1)}, bf16[1,192,512]{2,1,0:T(8,128)(2,1)S(1)}, u32[]{:S(2)}, u32[]{:S(2)}) collective-permute-start(bf16[1,192,512]{2,1,0:T(8,128)(2,1)S(1)} %get-tuple-element.19), channel_id=1, source_target_pairs={{0,2},{2,4},{4,6},{6,0},{1,3},{3,5},{5,7},{7,1},{8,10},{10,12},{12... | collective-permute-start | bytes 589832 | tf_op jit(solution)/shard_map/ppermute | solution.py:50
  26.0 7.1 %collective-permute-start.1 = (bf16[1,192,512]{2,1,0:T(8,128)(2,1)S(1)}, bf16[1,192,512]{2,1,0:T(8,128)(2,1)S(1)}, u32[]{:S(2)}, u32[]{:S(2)}) collective-permute-start(bf16[1,192,512]{2,1,0:T(8,128)(2,1)S(1)} %get-tuple-element.21), channel_id=1, source_target_pairs={{0,6},{2,0},{4,2},{6,4},{1,7},{3,1},{5,3},{7,5},{8,14},{10,8},{12,... | collective-permute-start | bytes 589832 | tf_op jit(solution)/shard_map/ppermute | solution.py:50
  29.4 8.3 %collective-permute-start.2 = (bf16[1,192,512]{2,1,0:T(8,128)(2,1)S(1)}, bf16[1,192,512]{2,1,0:T(8,128)(2,1)S(1)}, u32[]{:S(2)}, u32[]{:S(2)}) collective-permute-start(bf16[1,192,512]{2,1,0:T(8,128)(2,1)S(1)} %get-tuple-element.18), channel_id=1, source_target_pairs={{0,4},{2,6},{4,0},{6,2},{1,5},{3,7},{5,1},{7,3},{8,12},{10,14},{12... | collective-permute-start | bytes 589832 | tf_op jit(solution)/shard_map/ppermute | solution.py:50
  33.0 15.7 %copy-start.3 = (bf16[1,192,512]{2,1,0:T(8,128)(2,1)}, bf16[1,192,512]{2,1,0:T(8,128)(2,1)S(1)}, u32[]{:S(2)}) copy-start(bf16[1,192,512]{2,1,0:T(8,128)(2,1)S(1)} %collective-permute-done) | copy-start | bytes 589828
  33.1 15.5 %copy-start.5 = (bf16[1,192,512]{2,1,0:T(8,128)(2,1)}, bf16[1,192,512]{2,1,0:T(8,128)(2,1)S(1)}, u32[]{:S(2)}) copy-start(bf16[1,192,512]{2,1,0:T(8,128)(2,1)S(1)} %collective-permute-done.1) | copy-start | bytes 589828
  37.8 10.9 %copy-start.8 = (bf16[1,192,512]{2,1,0:T(8,128)(2,1)}, bf16[1,192,512]{2,1,0:T(8,128)(2,1)S(1)}, u32[]{:S(2)}) copy-start(bf16[1,192,512]{2,1,0:T(8,128)(2,1)S(1)} %collective-permute-done.2) | copy-start | bytes 589828
  49.3 12.6 %collective-permute-start.4 = (bf16[1,320,512]{2,1,0:T(8,128)(2,1)S(1)}, bf16[1,320,512]{2,1,0:T(8,128)(2,1)}, u32[]{:S(2)}, u32[]{:S(2)}) collective-permute-start(bf16[1,320,512]{2,1,0:T(8,128)(2,1)S(1)} %get-tuple-element.23), channel_id=1, source_target_pairs={{0,2},{2,4},{4,6},{6,0},{1,3},{3,5},{5,7},{7,1},{8,10},{10,12},{12... | collective-permute-start | bytes 983048 | tf_op jit(solution)/shard_map/ppermute | solution.py:50
  52.4 16.5 %collective-permute-start.3 = (bf16[1,320,512]{2,1,0:T(8,128)(2,1)S(1)}, bf16[1,320,512]{2,1,0:T(8,128)(2,1)}, u32[]{:S(2)}, u32[]{:S(2)}) collective-permute-start(bf16[1,320,512]{2,1,0:T(8,128)(2,1)S(1)} %get-tuple-element.22), channel_id=1, source_target_pairs={{0,2},{2,4},{4,6},{6,0},{1,3},{3,5},{5,7},{7,1},{8,10},{10,12},{12... | collective-permute-start | bytes 983048 | tf_op jit(solution)/shard_map/ppermute | solution.py:50
  56.1 15.7 %copy-start.2 = (bf16[1,2048,192]{1,2,0:T(8,128)(2,1)S(1)}, bf16[1,2048,192]{1,2,0:T(8,128)(2,1)}, u32[]{:S(2)}) copy-start(bf16[1,2048,192]{1,2,0:T(8,128)(2,1)} %param.13) | copy-start | bytes 2359300
  56.1 22.9 %collective-permute-start.6 = (bf16[1,320,512]{2,1,0:T(8,128)(2,1)S(1)}, bf16[1,320,512]{2,1,0:T(8,128)(2,1)S(1)}, u32[]{:S(2)}, u32[]{:S(2)}) collective-permute-start(bf16[1,320,512]{2,1,0:T(8,128)(2,1)S(1)} %get-tuple-element.23), channel_id=1, source_target_pairs={{0,6},{2,0},{4,2},{6,4},{1,7},{3,1},{5,3},{7,5},{8,14},{10,8},{12,... | collective-permute-start | bytes 983048 | tf_op jit(solution)/shard_map/ppermute | solution.py:50
  59.6 14.4 %collective-permute-start.5 = (bf16[1,320,512]{2,1,0:T(8,128)(2,1)S(1)}, bf16[1,320,512]{2,1,0:T(8,128)(2,1)S(1)}, u32[]{:S(2)}, u32[]{:S(2)}) collective-permute-start(bf16[1,320,512]{2,1,0:T(8,128)(2,1)S(1)} %get-tuple-element.22), channel_id=1, source_target_pairs={{0,6},{2,0},{4,2},{6,4},{1,7},{3,1},{5,3},{7,5},{8,14},{10,8},{12,... | collective-permute-start | bytes 983048 | tf_op jit(solution)/shard_map/ppermute | solution.py:50
  61.9 17.9 %collective-permute-start.8 = (bf16[1,320,512]{2,1,0:T(8,128)(2,1)}, bf16[1,320,512]{2,1,0:T(8,128)(2,1)S(1)}, u32[]{:S(2)}, u32[]{:S(2)}) collective-permute-start(bf16[1,320,512]{2,1,0:T(8,128)(2,1)} %collective-permute-done.4), channel_id=1, source_target_pairs={{0,2},{2,4},{4,6},{6,0},{1,3},{3,5},{5,7},{7,1},{8,10},{10,12},{12... | collective-permute-start | bytes 983048 | tf_op jit(solution)/shard_map/ppermute | solution.py:50
  71.7 7.2 %copy-start.7 = (bf16[1,2048,192]{1,2,0:T(8,128)(2,1)S(1)}, bf16[1,2048,192]{1,2,0:T(8,128)(2,1)}, u32[]{:S(2)}) copy-start(bf16[1,2048,192]{1,2,0:T(8,128)(2,1)} %param.14) | copy-start | bytes 2359300
  74.0 10.3 %collective-permute-start.7 = (bf16[1,320,512]{2,1,0:T(8,128)(2,1)S(1)}, bf16[1,320,512]{2,1,0:T(8,128)(2,1)S(1)}, u32[]{:S(2)}, u32[]{:S(2)}) collective-permute-start(bf16[1,320,512]{2,1,0:T(8,128)(2,1)S(1)} %collective-permute-done.5), channel_id=1, source_target_pairs={{0,6},{2,0},{4,2},{6,4},{1,7},{3,1},{5,3},{7,5},{8,14},{10,8},{12,... | collective-permute-start | bytes 983048 | tf_op jit(solution)/shard_map/ppermute | solution.py:50
  85.1 12.3 %copy-start.4 = (bf16[1,192,512]{2,1,0:T(8,128)(2,1)S(1)}, bf16[1,192,512]{2,1,0:T(8,128)(2,1)}, u32[]{:S(2)}) copy-start(bf16[1,192,512]{2,1,0:T(8,128)(2,1)} %copy-done.3) | copy-start | bytes 589828
  99.6 12.1 %copy-start.14 = (s32[32]{0:T(128)S(1)}, s32[32]{0:T(128)}, u32[]{:S(2)}) copy-start(s32[32]{0:T(128)} %param.19) | copy-start | bytes 388
  99.6 12.1 %copy-start.10 = (bf16[32,16,128]{2,1,0:T(8,128)(2,1)S(1)}, bf16[32,16,128]{2,1,0:T(8,128)(2,1)}, u32[]{:S(2)}) copy-start(bf16[32,16,128]{2,1,0:T(8,128)(2,1)} %param.16) | copy-start | bytes 393220
  101.0 11.6 %copy-start.15 = (bf16[32,128,1,128]{3,1,2,0:T(8,128)(2,1)S(1)}, bf16[32,128,1,128]{3,1,2,0:T(8,128)(2,1)}, u32[]{:S(2)}) copy-start(bf16[32,128,1,128]{3,1,2,0:T(8,128)(2,1)} %param.18) | copy-start | bytes 3145732
  101.0 36.6 %all-to-all-start.1 = ((bf16[128,20,128]{2,1,0:T(8,128)(2,1)}), bf16[128,20,128]{2,1,0:T(8,128)(2,1)S(1)}, u32[]{:S(2)}, u32[]{:S(2)}) async-start(bf16[128,20,128]{2,1,0:T(8,128)(2,1)} %reshape_transpose_reshape.7), calls=%async_computation.1 | async-start | bytes 1572864 | tf_op jit(solution)/shard_map/all_to_all | solution.py:163
  112.4 1.9 %copy-start.13 = (f32[32,8]{0,1:T(8,128)S(1)}, f32[32,8]{0,1:T(8,128)}, u32[]{:S(2)}) copy-start(f32[32,8]{0,1:T(8,128)} %param.12) | copy-start | bytes 3076
  112.4 2.0 %copy-start.12 = (s32[32,8]{0,1:T(8,128)S(1)}, s32[32,8]{0,1:T(8,128)}, u32[]{:S(2)}) copy-start(s32[32,8]{0,1:T(8,128)} %param.11) | copy-start | bytes 3076
  (3 other events, 3.7 us)

commit v12 on v11

--- a/solution.py
+++ b/solution.py
@@ -9,8 +9,8 @@
 
 def route_slots(expert_ids, experts, capacity):
     row_count = expert_ids.shape[0]
-    named = expert_ids[:, :, None] == jnp.arange(experts, dtype=jnp.int32)[None, None, :]
-    member = jnp.sum(named.astype(jnp.float32), axis=1)
+    named = expert_ids.T[:, :, None] == jnp.arange(experts, dtype=jnp.int32)[None, None, :]
+    member = jnp.sum(named.astype(jnp.float32), axis=0)
     rows = jnp.arange(row_count, dtype=jnp.int32)
     earlier = (rows[:, None] > rows[None, :]).astype(jnp.float32)
     slot = jnp.dot(earlier, member, preferred_element_type=jnp.float32)

time: 140 us -> 140 us (level)
  no operation moved by 1% of the time
where the time goes in v12:
time: 140 us; the launch traced here: 139 us
  starting transfers between devices  58.4 us (42%)
  waiting for transfers between devices  47.7 us (34%)
  blocking collectives  11.9 us (8%)
  matrix products  11.4 us (8%)
  local copies, waits for them, and re-layouts  6.7 us (5%)
  other arithmetic  1.59 us (1%)
    ppermute x9, starting transfers between devices, shifted(): lax.ppermute(x, 'tensor', perm=[(i, (i + step) % count) for i in range(co...  29.4 us
    all_to_all x1, waiting for transfers between devices, local(): lax.all_to_all(summed.reshape(own_experts, owners, CAP, last).transpose(1...  22.7 us
    all_to_all x1, starting transfers between devices, local(): lax.all_to_all(local_buffer, ('dp', 'sect'), split_axis=0, concat_axis=0,...  18.4 us
    ppermute x9, waiting for transfers between devices, shifted(): lax.ppermute(x, 'tensor', perm=[(i, (i + step) % count) for i in range(co...  14.1 us
    all_gather x1, blocking collectives, down_projection(): hidden_all = lax.all_gather(hidden_t, 'tensor', axis=0, tiled=False)  11.9 us
    all_to_all x1, waiting for transfers between devices, local(): lax.all_to_all(local_buffer, ('dp', 'sect'), split_axis=0, concat_axis=0,...  10.9 us
    all_to_all x1, starting transfers between devices, local(): lax.all_to_all(summed.reshape(own_experts, owners, CAP, last).transpose(1...  10.6 us
    dot_general x4, matrix products, ring_projections(): jnp.einsum('end,edf->enf', piece, up_rows, preferred_element_type=jnp.flo...  3.59 us
  transfers between devices with their start and end apart: 11, of which 8 were waited for; matrix products, arithmetic and copies ran while one was open for 7% of the time, Pallas kernels for 0%

profile of v12, /device:TPU:1, one launch (start us, length us, event | category | flops | bytes accessed | tf_op | source)
XLA Modules:
  0.0 138.9 jit_solution(7715747630896694517)
XLA Ops:
  0.7 0.9 convert_reduce_fusion
  2.8 1.4 %reshape.183 = bf16[128,20,128]{2,1,0:T(8,128)(2,1)} reshape(bf16[640,512]{1,0:T(8,128)(2,1)S(1)} %convolution_convert_fusion) | data formatting | bytes 1310720 | tf_op jit(solution)/shard_map/reshape | solution.py:144
  4.2 18.4 %all-to-all-start = ((bf16[128,20,128]{2,1,0:T(8,128)(2,1)}), bf16[128,20,128]{2,1,0:T(8,128)(2,1)S(1)}, u32[]{:S(2)}, u32[]{:S(2)}) async-start(bf16[128,20,128]{2,1,0:T(8,128)(2,1)} %reshape.183), calls=%async_computation | async-start | bytes 1572864 | tf_op jit(solution)/shard_map/all_to_all | solution.py:146
  22.8 3.1 %collective-permute-start = (bf16[1,192,512]{2,1,0:T(8,128)(2,1)S(1)}, bf16[1,192,512]{2,1,0:T(8,128)(2,1)S(1)}, u32[]{:S(2)}, u32[]{:S(2)}) collective-permute-start(bf16[1,192,512]{2,1,0:T(8,128)(2,1)S(1)} %get-tuple-element.19), channel_id=1, source_target_pairs={{0,2},{2,4},{4,6},{6,0},{1,3},{3,5},{5,7},{7,1},{8,10},{10,12},{12... | collective-permute-start | bytes 589832 | tf_op jit(solution)/shard_map/ppermute | solution.py:50
  25.9 3.4 %collective-permute-start.1 = (bf16[1,192,512]{2,1,0:T(8,128)(2,1)S(1)}, bf16[1,192,512]{2,1,0:T(8,128)(2,1)S(1)}, u32[]{:S(2)}, u32[]{:S(2)}) collective-permute-start(bf16[1,192,512]{2,1,0:T(8,128)(2,1)S(1)} %get-tuple-element.21), channel_id=1, source_target_pairs={{0,6},{2,0},{4,2},{6,4},{1,7},{3,1},{5,3},{7,5},{8,14},{10,8},{12,... | collective-permute-start | bytes 589832 | tf_op jit(solution)/shard_map/ppermute | solution.py:50
  29.3 3.4 %collective-permute-start.2 = (bf16[1,192,512]{2,1,0:T(8,128)(2,1)S(1)}, bf16[1,192,512]{2,1,0:T(8,128)(2,1)S(1)}, u32[]{:S(2)}, u32[]{:S(2)}) collective-permute-start(bf16[1,192,512]{2,1,0:T(8,128)(2,1)S(1)} %get-tuple-element.18), channel_id=1, source_target_pairs={{0,4},{2,6},{4,0},{6,2},{1,5},{3,7},{5,1},{7,3},{8,12},{10,14},{12... | collective-permute-start | bytes 589832 | tf_op jit(solution)/shard_map/ppermute | solution.py:50
  33.1 4.6 %collective-permute-done.2 = bf16[1,192,512]{2,1,0:T(8,128)(2,1)S(1)} collective-permute-done((bf16[1,192,512]{2,1,0:T(8,128)(2,1)S(1)}, bf16[1,192,512]{2,1,0:T(8,128)(2,1)S(1)}, u32[]{:S(2)}, u32[]{:S(2)}) %collective-permute-start.2) | collective-permute-done | bytes 196640 | tf_op jit(solution)/shard_map/ppermute | solution.py:50
  37.7 10.9 %all-to-all-done = bf16[128,20,128]{2,1,0:T(8,128)(2,1)S(1)} async-done(((bf16[128,20,128]{2,1,0:T(8,128)(2,1)}), bf16[128,20,128]{2,1,0:T(8,128)(2,1)S(1)}, u32[]{:S(2)}, u32[]{:S(2)}) %all-to-all-start) | async-done | bytes 655392 | tf_op jit(solution)/shard_map/all_to_all | solution.py:146
  49.2 3.1 %collective-permute-start.4 = (bf16[1,320,512]{2,1,0:T(8,128)(2,1)S(1)}, bf16[1,320,512]{2,1,0:T(8,128)(2,1)}, u32[]{:S(2)}, u32[]{:S(2)}) collective-permute-start(bf16[1,320,512]{2,1,0:T(8,128)(2,1)S(1)} %get-tuple-element.23), channel_id=1, source_target_pairs={{0,2},{2,4},{4,6},{6,0},{1,3},{3,5},{5,7},{7,1},{8,10},{10,12},{12... | collective-permute-start | bytes 983048 | tf_op jit(solution)/shard_map/ppermute | solution.py:50
  52.3 3.1 %collective-permute-start.3 = (bf16[1,320,512]{2,1,0:T(8,128)(2,1)S(1)}, bf16[1,320,512]{2,1,0:T(8,128)(2,1)}, u32[]{:S(2)}, u32[]{:S(2)}) collective-permute-start(bf16[1,320,512]{2,1,0:T(8,128)(2,1)S(1)} %get-tuple-element.22), channel_id=1, source_target_pairs={{0,2},{2,4},{4,6},{6,0},{1,3},{3,5},{5,7},{7,1},{8,10},{10,12},{12... | collective-permute-start | bytes 983048 | tf_op jit(solution)/shard_map/ppermute | solution.py:50
  56.0 3.5 %collective-permute-start.6 = (bf16[1,320,512]{2,1,0:T(8,128)(2,1)S(1)}, bf16[1,320,512]{2,1,0:T(8,128)(2,1)S(1)}, u32[]{:S(2)}, u32[]{:S(2)}) collective-permute-start(bf16[1,320,512]{2,1,0:T(8,128)(2,1)S(1)} %get-tuple-element.23), channel_id=1, source_target_pairs={{0,6},{2,0},{4,2},{6,4},{1,7},{3,1},{5,3},{7,5},{8,14},{10,8},{12,... | collective-permute-start | bytes 983048 | tf_op jit(solution)/shard_map/ppermute | solution.py:50
  59.5 2.2 %collective-permute-start.5 = (bf16[1,320,512]{2,1,0:T(8,128)(2,1)S(1)}, bf16[1,320,512]{2,1,0:T(8,128)(2,1)S(1)}, u32[]{:S(2)}, u32[]{:S(2)}) collective-permute-start(bf16[1,320,512]{2,1,0:T(8,128)(2,1)S(1)} %get-tuple-element.22), channel_id=1, source_target_pairs={{0,6},{2,0},{4,2},{6,4},{1,7},{3,1},{5,3},{7,5},{8,14},{10,8},{12,... | collective-permute-start | bytes 983048 | tf_op jit(solution)/shard_map/ppermute | solution.py:50
  61.8 3.0 %collective-permute-start.8 = (bf16[1,320,512]{2,1,0:T(8,128)(2,1)}, bf16[1,320,512]{2,1,0:T(8,128)(2,1)S(1)}, u32[]{:S(2)}, u32[]{:S(2)}) collective-permute-start(bf16[1,320,512]{2,1,0:T(8,128)(2,1)} %collective-permute-done.4), channel_id=1, source_target_pairs={{0,2},{2,4},{4,6},{6,0},{1,3},{3,5},{5,7},{7,1},{8,10},{10,12},{12... | collective-permute-start | bytes 983048 | tf_op jit(solution)/shard_map/ppermute | solution.py:50
  64.8 4.0 %collective-permute-done.3 = bf16[1,320,512]{2,1,0:T(8,128)(2,1)} collective-permute-done((bf16[1,320,512]{2,1,0:T(8,128)(2,1)S(1)}, bf16[1,320,512]{2,1,0:T(8,128)(2,1)}, u32[]{:S(2)}, u32[]{:S(2)}) %collective-permute-start.3) | collective-permute-done | bytes 327712 | tf_op jit(solution)/shard_map/ppermute | solution.py:50
  68.8 1.5 %fusion.18 = f32[640,192]{0,1:T(8,128)S(1)} fusion(bf16[1,320,512]{2,1,0:T(8,128)(2,1)} %collective-permute-done.4, bf16[1,320,512]{2,1,0:T(8,128)(2,1)} %collective-permute-done.3, bf16[1,2048,192]{1,2,0:T(8,128)(2,1)} %param.14, s32[]{:T(128)S(6)} %select_n.92), kind=kOutput, calls=%fused_computation.37 | convolution fusion | flops 127139840 | bytes 1343492 | tf_op jit(solution)/shard_map/end,edf->enf/dot_general | solution.py:75
  70.3 1.3 convolution_add_fusion.2
  71.7 1.5 %fusion.19 = f32[640,192]{0,1:T(8,128)S(1)} fusion(bf16[1,320,512]{2,1,0:T(8,128)(2,1)} %collective-permute-done.4, bf16[1,320,512]{2,1,0:T(8,128)(2,1)} %collective-permute-done.3, bf16[1,2048,192]{1,2,0:T(8,128)(2,1)S(1)} %copy-done.2, s32[]{:T(128)S(6)} %select_n.92), kind=kOutput, calls=%fused_computation.38 | convolution fusion | flops 127139840 | bytes 1343492 | tf_op jit(solution)/shard_map/end,edf->enf/dot_general | solution.py:74
  73.9 4.6 %collective-permute-start.7 = (bf16[1,320,512]{2,1,0:T(8,128)(2,1)S(1)}, bf16[1,320,512]{2,1,0:T(8,128)(2,1)S(1)}, u32[]{:S(2)}, u32[]{:S(2)}) collective-permute-start(bf16[1,320,512]{2,1,0:T(8,128)(2,1)S(1)} %collective-permute-done.5), channel_id=1, source_target_pairs={{0,6},{2,0},{4,2},{6,4},{1,7},{3,1},{5,3},{7,5},{8,14},{10,8},{12,... | collective-permute-start | bytes 983048 | tf_op jit(solution)/shard_map/ppermute | solution.py:50
  79.7 4.5 %collective-permute-done.7 = bf16[1,320,512]{2,1,0:T(8,128)(2,1)S(1)} collective-permute-done((bf16[1,320,512]{2,1,0:T(8,128)(2,1)S(1)}, bf16[1,320,512]{2,1,0:T(8,128)(2,1)S(1)}, u32[]{:S(2)}, u32[]{:S(2)}) %collective-permute-start.7) | collective-permute-done | bytes 327712 | tf_op jit(solution)/shard_map/ppermute | solution.py:50
  85.0 11.9 %all-gather = bf16[4,192,640]{2,1,0:T(8,128)(2,1)S(1)} all-gather(bf16[1,192,640]{2,1,0:T(8,128)(2,1)S(1)} %fusion.14), channel_id=2, replica_groups=mesh['dp'=64,'tensor'=4,'sect'=2] {'tensor'}, dimensions={0}, use_global_device_ids=true | all-gather | bytes 1228800 | tf_op jit(solution)/shard_map/all_gather | solution.py:107
  99.5 1.4 %reshape_transpose_reshape.7 = bf16[128,20,128]{2,1,0:T(8,128)(2,1)} reshape(bf16[640,512]{1,0:T(8,128)(2,1)S(1)} %fusion.3) | data formatting | bytes 1310720 | tf_op jit(solution)/shard_map/reshape;transpose;reshape | solution.py:166
  100.9 10.6 %all-to-all-start.1 = ((bf16[128,20,128]{2,1,0:T(8,128)(2,1)}), bf16[128,20,128]{2,1,0:T(8,128)(2,1)S(1)}, u32[]{:S(2)}, u32[]{:S(2)}) async-start(bf16[128,20,128]{2,1,0:T(8,128)(2,1)} %reshape_transpose_reshape.7), calls=%async_computation.1 | async-start | bytes 1572864 | tf_op jit(solution)/shard_map/all_to_all | solution.py:163
  112.5 1.6 %convolution_convert_fusion.5 = bf16[32,16,128]{2,1,0:T(8,128)(2,1)} fusion(bf16[32,128,1,128]{3,1,2,0:T(8,128)(2,1)S(1)} %copy-done.15, f32[32,16]{1,0:T(8,128)S(1)} %fusion.75, f32[32,16,128]{2,1,0:T(8,128)S(1)} %fusion.13), kind=kOutput, calls=%fused_computation.27 | convolution fusion | flops 17040000 | bytes 1443840 | tf_op jit(solution)/shard_map/rkgl,rlkd->rkgd/dot_general | solution.py:45
  114.8 22.7 %all-to-all-done.1 = bf16[128,20,128]{2,1,0:T(8,128)(2,1)S(1)} async-done(((bf16[128,20,128]{2,1,0:T(8,128)(2,1)}), bf16[128,20,128]{2,1,0:T(8,128)(2,1)S(1)}, u32[]{:S(2)}, u32[]{:S(2)}) %all-to-all-start.1) | async-done | bytes 655392 | tf_op jit(solution)/shard_map/all_to_all | solution.py:163
  (75 shorter events, 11.0 us)
Async XLA Ops:
  0.6 111.0 %copy-start = (bf16[32,128,1,128]{3,1,2,0:T(8,128)(2,1)S(1)}, bf16[32,128,1,128]{3,1,2,0:T(8,128)(2,1)}, u32[]{:S(2)}) copy-start(bf16[32,128,1,128]{3,1,2,0:T(8,128)(2,1)} %param.17) | copy-start | bytes 3145732
  2.8 19.9 %copy-start.1 = (bf16[1,192,2048]{2,1,0:T(8,128)(2,1)S(1)}, bf16[1,192,2048]{2,1,0:T(8,128)(2,1)}, u32[]{:S(2)}) copy-start(bf16[1,192,2048]{2,1,0:T(8,128)(2,1)} %param.15) | copy-start | bytes 2359300
  4.2 44.4 %all-to-all-start = ((bf16[128,20,128]{2,1,0:T(8,128)(2,1)}), bf16[128,20,128]{2,1,0:T(8,128)(2,1)S(1)}, u32[]{:S(2)}, u32[]{:S(2)}) async-start(bf16[128,20,128]{2,1,0:T(8,128)(2,1)} %reshape.183), calls=%async_computation | async-start | bytes 1572864 | tf_op jit(solution)/shard_map/all_to_all | solution.py:146
  22.8 10.1 %collective-permute-start = (bf16[1,192,512]{2,1,0:T(8,128)(2,1)S(1)}, bf16[1,192,512]{2,1,0:T(8,128)(2,1)S(1)}, u32[]{:S(2)}, u32[]{:S(2)}) collective-permute-start(bf16[1,192,512]{2,1,0:T(8,128)(2,1)S(1)} %get-tuple-element.19), channel_id=1, source_target_pairs={{0,2},{2,4},{4,6},{6,0},{1,3},{3,5},{5,7},{7,1},{8,10},{10,12},{12... | collective-permute-start | bytes 589832 | tf_op jit(solution)/shard_map/ppermute | solution.py:50
  25.9 7.1 %collective-permute-start.1 = (bf16[1,192,512]{2,1,0:T(8,128)(2,1)S(1)}, bf16[1,192,512]{2,1,0:T(8,128)(2,1)S(1)}, u32[]{:S(2)}, u32[]{:S(2)}) collective-permute-start(bf16[1,192,512]{2,1,0:T(8,128)(2,1)S(1)} %get-tuple-element.21), channel_id=1, source_target_pairs={{0,6},{2,0},{4,2},{6,4},{1,7},{3,1},{5,3},{7,5},{8,14},{10,8},{12,... | collective-permute-start | bytes 589832 | tf_op jit(solution)/shard_map/ppermute | solution.py:50
  29.3 8.3 %collective-permute-start.2 = (bf16[1,192,512]{2,1,0:T(8,128)(2,1)S(1)}, bf16[1,192,512]{2,1,0:T(8,128)(2,1)S(1)}, u32[]{:S(2)}, u32[]{:S(2)}) collective-permute-start(bf16[1,192,512]{2,1,0:T(8,128)(2,1)S(1)} %get-tuple-element.18), channel_id=1, source_target_pairs={{0,4},{2,6},{4,0},{6,2},{1,5},{3,7},{5,1},{7,3},{8,12},{10,14},{12... | collective-permute-start | bytes 589832 | tf_op jit(solution)/shard_map/ppermute | solution.py:50
  32.9 15.7 %copy-start.3 = (bf16[1,192,512]{2,1,0:T(8,128)(2,1)}, bf16[1,192,512]{2,1,0:T(8,128)(2,1)S(1)}, u32[]{:S(2)}) copy-start(bf16[1,192,512]{2,1,0:T(8,128)(2,1)S(1)} %collective-permute-done) | copy-start | bytes 589828
  33.1 15.5 %copy-start.5 = (bf16[1,192,512]{2,1,0:T(8,128)(2,1)}, bf16[1,192,512]{2,1,0:T(8,128)(2,1)S(1)}, u32[]{:S(2)}) copy-start(bf16[1,192,512]{2,1,0:T(8,128)(2,1)S(1)} %collective-permute-done.1) | copy-start | bytes 589828
  37.7 10.9 %copy-start.8 = (bf16[1,192,512]{2,1,0:T(8,128)(2,1)}, bf16[1,192,512]{2,1,0:T(8,128)(2,1)S(1)}, u32[]{:S(2)}) copy-start(bf16[1,192,512]{2,1,0:T(8,128)(2,1)S(1)} %collective-permute-done.2) | copy-start | bytes 589828
  49.2 12.6 %collective-permute-start.4 = (bf16[1,320,512]{2,1,0:T(8,128)(2,1)S(1)}, bf16[1,320,512]{2,1,0:T(8,128)(2,1)}, u32[]{:S(2)}, u32[]{:S(2)}) collective-permute-start(bf16[1,320,512]{2,1,0:T(8,128)(2,1)S(1)} %get-tuple-element.23), channel_id=1, source_target_pairs={{0,2},{2,4},{4,6},{6,0},{1,3},{3,5},{5,7},{7,1},{8,10},{10,12},{12... | collective-permute-start | bytes 983048 | tf_op jit(solution)/shard_map/ppermute | solution.py:50
  52.3 16.5 %collective-permute-start.3 = (bf16[1,320,512]{2,1,0:T(8,128)(2,1)S(1)}, bf16[1,320,512]{2,1,0:T(8,128)(2,1)}, u32[]{:S(2)}, u32[]{:S(2)}) collective-permute-start(bf16[1,320,512]{2,1,0:T(8,128)(2,1)S(1)} %get-tuple-element.22), channel_id=1, source_target_pairs={{0,2},{2,4},{4,6},{6,0},{1,3},{3,5},{5,7},{7,1},{8,10},{10,12},{12... | collective-permute-start | bytes 983048 | tf_op jit(solution)/shard_map/ppermute | solution.py:50
  56.0 15.7 %copy-start.2 = (bf16[1,2048,192]{1,2,0:T(8,128)(2,1)S(1)}, bf16[1,2048,192]{1,2,0:T(8,128)(2,1)}, u32[]{:S(2)}) copy-start(bf16[1,2048,192]{1,2,0:T(8,128)(2,1)} %param.13) | copy-start | bytes 2359300
  56.0 22.9 %collective-permute-start.6 = (bf16[1,320,512]{2,1,0:T(8,128)(2,1)S(1)}, bf16[1,320,512]{2,1,0:T(8,128)(2,1)S(1)}, u32[]{:S(2)}, u32[]{:S(2)}) collective-permute-start(bf16[1,320,512]{2,1,0:T(8,128)(2,1)S(1)} %get-tuple-element.23), channel_id=1, source_target_pairs={{0,6},{2,0},{4,2},{6,4},{1,7},{3,1},{5,3},{7,5},{8,14},{10,8},{12,... | collective-permute-start | bytes 983048 | tf_op jit(solution)/shard_map/ppermute | solution.py:50
  59.5 14.4 %collective-permute-start.5 = (bf16[1,320,512]{2,1,0:T(8,128)(2,1)S(1)}, bf16[1,320,512]{2,1,0:T(8,128)(2,1)S(1)}, u32[]{:S(2)}, u32[]{:S(2)}) collective-permute-start(bf16[1,320,512]{2,1,0:T(8,128)(2,1)S(1)} %get-tuple-element.22), channel_id=1, source_target_pairs={{0,6},{2,0},{4,2},{6,4},{1,7},{3,1},{5,3},{7,5},{8,14},{10,8},{12,... | collective-permute-start | bytes 983048 | tf_op jit(solution)/shard_map/ppermute | solution.py:50
  61.8 17.9 %collective-permute-start.8 = (bf16[1,320,512]{2,1,0:T(8,128)(2,1)}, bf16[1,320,512]{2,1,0:T(8,128)(2,1)S(1)}, u32[]{:S(2)}, u32[]{:S(2)}) collective-permute-start(bf16[1,320,512]{2,1,0:T(8,128)(2,1)} %collective-permute-done.4), channel_id=1, source_target_pairs={{0,2},{2,4},{4,6},{6,0},{1,3},{3,5},{5,7},{7,1},{8,10},{10,12},{12... | collective-permute-start | bytes 983048 | tf_op jit(solution)/shard_map/ppermute | solution.py:50
  71.7 7.2 %copy-start.7 = (bf16[1,2048,192]{1,2,0:T(8,128)(2,1)S(1)}, bf16[1,2048,192]{1,2,0:T(8,128)(2,1)}, u32[]{:S(2)}) copy-start(bf16[1,2048,192]{1,2,0:T(8,128)(2,1)} %param.14) | copy-start | bytes 2359300
  73.9 10.3 %collective-permute-start.7 = (bf16[1,320,512]{2,1,0:T(8,128)(2,1)S(1)}, bf16[1,320,512]{2,1,0:T(8,128)(2,1)S(1)}, u32[]{:S(2)}, u32[]{:S(2)}) collective-permute-start(bf16[1,320,512]{2,1,0:T(8,128)(2,1)S(1)} %collective-permute-done.5), channel_id=1, source_target_pairs={{0,6},{2,0},{4,2},{6,4},{1,7},{3,1},{5,3},{7,5},{8,14},{10,8},{12,... | collective-permute-start | bytes 983048 | tf_op jit(solution)/shard_map/ppermute | solution.py:50
  85.0 12.2 %copy-start.4 = (bf16[1,192,512]{2,1,0:T(8,128)(2,1)S(1)}, bf16[1,192,512]{2,1,0:T(8,128)(2,1)}, u32[]{:S(2)}) copy-start(bf16[1,192,512]{2,1,0:T(8,128)(2,1)} %copy-done.3) | copy-start | bytes 589828
  99.5 12.0 %copy-start.14 = (s32[32]{0:T(128)S(1)}, s32[32]{0:T(128)}, u32[]{:S(2)}) copy-start(s32[32]{0:T(128)} %param.19) | copy-start | bytes 388
  99.5 12.1 %copy-start.10 = (bf16[32,16,128]{2,1,0:T(8,128)(2,1)S(1)}, bf16[32,16,128]{2,1,0:T(8,128)(2,1)}, u32[]{:S(2)}) copy-start(bf16[32,16,128]{2,1,0:T(8,128)(2,1)} %param.16) | copy-start | bytes 393220
  100.9 11.6 %copy-start.15 = (bf16[32,128,1,128]{3,1,2,0:T(8,128)(2,1)S(1)}, bf16[32,128,1,128]{3,1,2,0:T(8,128)(2,1)}, u32[]{:S(2)}) copy-start(bf16[32,128,1,128]{3,1,2,0:T(8,128)(2,1)} %param.18) | copy-start | bytes 3145732
  100.9 36.6 %all-to-all-start.1 = ((bf16[128,20,128]{2,1,0:T(8,128)(2,1)}), bf16[128,20,128]{2,1,0:T(8,128)(2,1)S(1)}, u32[]{:S(2)}, u32[]{:S(2)}) async-start(bf16[128,20,128]{2,1,0:T(8,128)(2,1)} %reshape_transpose_reshape.7), calls=%async_computation.1 | async-start | bytes 1572864 | tf_op jit(solution)/shard_map/all_to_all | solution.py:163
  112.3 1.9 %copy-start.13 = (f32[32,8]{0,1:T(8,128)S(1)}, f32[32,8]{0,1:T(8,128)}, u32[]{:S(2)}) copy-start(f32[32,8]{0,1:T(8,128)} %param.12) | copy-start | bytes 3076
  112.3 2.0 %copy-start.12 = (s32[32,8]{0,1:T(8,128)S(1)}, s32[32,8]{0,1:T(8,128)}, u32[]{:S(2)}) copy-start(s32[32,8]{0,1:T(8,128)} %param.11) | copy-start | bytes 3076
  (3 other events, 3.6 us)

commit v13 on v11

--- a/solution.py
+++ b/solution.py
@@ -61,8 +61,8 @@
     half = inputs.shape[1] // 2
     top, bottom = inputs[:, :half], inputs[:, half:]
     right_top = shifted(top, -1, count)
-    left_bottom = shifted(bottom, 1, count)
-    from_left = jnp.concatenate([shifted(top, 1, count), left_bottom], axis=1)
+    from_left = shifted(inputs, 1, count)
+    left_bottom = from_left[:, half:]
     from_right = jnp.concatenate([right_top, shifted(bottom, -1, count)], axis=1)
     far = jnp.concatenate([shifted(right_top, -1, count), shifted(left_bottom, 1, count)], axis=1)
     gate = None

time: 140 us -> 138 us (0.986)
  local copies, waits for them, and re-layouts: 7.55 us -> 11.8 us
  starting transfers between devices: 58.4 us -> 55.1 us
  waiting for transfers between devices: 47.8 us -> 45 us
    ppermute x9 -> x8, starting transfers between devices: 29.4 us -> 26.3 us  [shifted(): lax.ppermute(x, 'tensor', perm=[(i, (i + step) % count) for i in range(co...]
    slice x1, local copies, waits for them, and re-layouts: 0.04 us -> 1.98 us  [ring_projections(): top, bottom = (inputs[:, :half], inputs[:, half:])]
    ppermute x9 -> x8, waiting for transfers between devices: 14.1 us -> 12.2 us  [shifted(): lax.ppermute(x, 'tensor', perm=[(i, (i + step) % count) for i in range(co...]
  transfers between devices with their start and end apart: 11 -> 10, of which waited for: 8 -> 6; matrix products, arithmetic and copies ran while one was open for 7% -> 8% of each run, Pallas kernels for 0% -> 0%
where the time goes in v13:
time: 138 us; the launch traced here: 137 us
  starting transfers between devices  55.1 us (40%)
  waiting for transfers between devices  45 us (33%)
  blocking collectives  12.4 us (9%)
  local copies, waits for them, and re-layouts  11.8 us (9%)
  matrix products  10.1 us (7%)
  other arithmetic  1.44 us (1%)
    ppermute x8, starting transfers between devices, shifted(): lax.ppermute(x, 'tensor', perm=[(i, (i + step) % count) for i in range(co...  26.3 us
    all_to_all x1, waiting for transfers between devices, local(): lax.all_to_all(summed.reshape(own_experts, owners, CAP, last).transpose(1...  22.7 us
    all_to_all x1, starting transfers between devices, local(): lax.all_to_all(local_buffer, ('dp', 'sect'), split_axis=0, concat_axis=0,...  18.4 us
    all_gather x1, blocking collectives, down_projection(): hidden_all = lax.all_gather(hidden_t, 'tensor', axis=0, tiled=False)  12.4 us
    ppermute x8, waiting for transfers between devices, shifted(): lax.ppermute(x, 'tensor', perm=[(i, (i + step) % count) for i in range(co...  12.2 us
    all_to_all x1, starting transfers between devices, local(): lax.all_to_all(summed.reshape(own_experts, owners, CAP, last).transpose(1...  10.4 us
    all_to_all x1, waiting for transfers between devices, local(): lax.all_to_all(local_buffer, ('dp', 'sect'), split_axis=0, concat_axis=0,...  10.1 us
    unnamed x33, local copies, waits for them, and re-layouts  2.84 us
  transfers between devices with their start and end apart: 10, of which 6 were waited for; matrix products, arithmetic and copies ran while one was open for 8% of the time, Pallas kernels for 0%

profile of v13, /device:TPU:1, one launch (start us, length us, event | category | flops | bytes accessed | tf_op | source)
XLA Modules:
  0.0 137.1 jit_solution(11734358211365666900)
XLA Ops:
  2.9 1.4 %reshape.183 = bf16[128,20,128]{2,1,0:T(8,128)(2,1)} reshape(bf16[640,512]{1,0:T(8,128)(2,1)S(1)} %convolution_convert_fusion) | data formatting | bytes 1310720 | tf_op jit(solution)/shard_map/reshape | solution.py:144
  4.3 18.4 %all-to-all-start = ((bf16[128,20,128]{2,1,0:T(8,128)(2,1)}), bf16[128,20,128]{2,1,0:T(8,128)(2,1)S(1)}, u32[]{:S(2)}, u32[]{:S(2)}) async-start(bf16[128,20,128]{2,1,0:T(8,128)(2,1)} %reshape.183), calls=%async_computation | async-start | bytes 1572864 | tf_op jit(solution)/shard_map/all_to_all | solution.py:146
  23.6 3.1 %collective-permute-start = (bf16[1,192,512]{2,1,0:T(8,128)(2,1)S(1)}, bf16[1,192,512]{2,1,0:T(8,128)(2,1)S(1)}, u32[]{:S(2)}, u32[]{:S(2)}) collective-permute-start(bf16[1,192,512]{2,1,0:T(8,128)(2,1)S(1)} %get-tuple-element.19), channel_id=1, source_target_pairs={{0,2},{2,4},{4,6},{6,0},{1,3},{3,5},{5,7},{7,1},{8,10},{10,12},{12... | collective-permute-start | bytes 589832 | tf_op jit(solution)/shard_map/ppermute | solution.py:50
  26.7 3.4 %collective-permute-start.1 = (bf16[1,192,512]{2,1,0:T(8,128)(2,1)S(1)}, bf16[1,192,512]{2,1,0:T(8,128)(2,1)S(1)}, u32[]{:S(2)}, u32[]{:S(2)}) collective-permute-start(bf16[1,192,512]{2,1,0:T(8,128)(2,1)S(1)} %get-tuple-element.21), channel_id=1, source_target_pairs={{0,6},{2,0},{4,2},{6,4},{1,7},{3,1},{5,3},{7,5},{8,14},{10,8},{12,... | collective-permute-start | bytes 589832 | tf_op jit(solution)/shard_map/ppermute | solution.py:50
  30.1 3.4 %collective-permute-start.2 = (bf16[1,192,512]{2,1,0:T(8,128)(2,1)S(1)}, bf16[1,192,512]{2,1,0:T(8,128)(2,1)}, u32[]{:S(2)}, u32[]{:S(2)}) collective-permute-start(bf16[1,192,512]{2,1,0:T(8,128)(2,1)S(1)} %get-tuple-element.18), channel_id=1, source_target_pairs={{0,4},{2,6},{4,0},{6,2},{1,5},{3,7},{5,1},{7,3},{8,12},{10,14},{12... | collective-permute-start | bytes 589832 | tf_op jit(solution)/shard_map/ppermute | solution.py:50
  35.7 2.9 %collective-permute-done.2 = bf16[1,192,512]{2,1,0:T(8,128)(2,1)} collective-permute-done((bf16[1,192,512]{2,1,0:T(8,128)(2,1)S(1)}, bf16[1,192,512]{2,1,0:T(8,128)(2,1)}, u32[]{:S(2)}, u32[]{:S(2)}) %collective-permute-start.2) | collective-permute-done | bytes 196640 | tf_op jit(solution)/shard_map/ppermute | solution.py:50
  38.5 10.1 %all-to-all-done = bf16[128,20,128]{2,1,0:T(8,128)(2,1)S(1)} async-done(((bf16[128,20,128]{2,1,0:T(8,128)(2,1)}), bf16[128,20,128]{2,1,0:T(8,128)(2,1)S(1)}, u32[]{:S(2)}, u32[]{:S(2)}) %all-to-all-start) | async-done | bytes 655392 | tf_op jit(solution)/shard_map/all_to_all | solution.py:146
  48.7 1.4 reshape_transpose_reshape.6
  50.0 3.1 %collective-permute-start.3 = (bf16[1,640,512]{2,1,0:T(8,128)(2,1)}, bf16[1,640,512]{2,1,0:T(8,128)(2,1)S(1)}, u32[]{:S(2)}, u32[]{:S(2)}) collective-permute-start(bf16[1,640,512]{2,1,0:T(8,128)(2,1)} %reshape_transpose_reshape.6), channel_id=1, source_target_pairs={{0,2},{2,4},{4,6},{6,0},{1,3},{3,5},{5,7},{7,1},{8,10},{10,12},{12... | collective-permute-start | bytes 1966088 | tf_op jit(solution)/shard_map/ppermute | solution.py:50
  53.1 2.0 %fusion.74 = (bf16[1,320,512]{2,1,0:T(8,128)(2,1)}, bf16[1,320,512]{2,1,0:T(8,128)(2,1)}) fusion(bf16[1,640,512]{2,1,0:T(8,128)(2,1)} %reshape_transpose_reshape.6), kind=kLoop, calls=%fused_computation.106 | loop fusion | bytes 1310720 | tf_op jit(solution)/shard_map/slice | solution.py:62
  55.1 3.4 %collective-permute-start.4 = (bf16[1,320,512]{2,1,0:T(8,128)(2,1)}, bf16[1,320,512]{2,1,0:T(8,128)(2,1)S(1)}, u32[]{:S(2)}, u32[]{:S(2)}) collective-permute-start(bf16[1,320,512]{2,1,0:T(8,128)(2,1)} %get-tuple-element.22), channel_id=1, source_target_pairs={{0,6},{2,0},{4,2},{6,4},{1,7},{3,1},{5,3},{7,5},{8,14},{10,8},{12,... | collective-permute-start | bytes 983048 | tf_op jit(solution)/shard_map/ppermute | solution.py:50
  59.1 3.3 %collective-permute-start.5 = (bf16[1,320,512]{2,1,0:T(8,128)(2,1)}, bf16[1,320,512]{2,1,0:T(8,128)(2,1)S(1)}, u32[]{:S(2)}, u32[]{:S(2)}) collective-permute-start(bf16[1,320,512]{2,1,0:T(8,128)(2,1)} %get-tuple-element.23), channel_id=1, source_target_pairs={{0,6},{2,0},{4,2},{6,4},{1,7},{3,1},{5,3},{7,5},{8,14},{10,8},{12,... | collective-permute-start | bytes 983048 | tf_op jit(solution)/shard_map/ppermute | solution.py:50
  62.4 4.0 %collective-permute-done.4 = bf16[1,320,512]{2,1,0:T(8,128)(2,1)S(1)} collective-permute-done((bf16[1,320,512]{2,1,0:T(8,128)(2,1)}, bf16[1,320,512]{2,1,0:T(8,128)(2,1)S(1)}, u32[]{:S(2)}, u32[]{:S(2)}) %collective-permute-start.4) | collective-permute-done | bytes 327712 | tf_op jit(solution)/shard_map/ppermute | solution.py:50
  66.4 4.6 %collective-permute-start.6 = (bf16[1,320,512]{2,1,0:T(8,128)(2,1)S(1)}, bf16[1,320,512]{2,1,0:T(8,128)(2,1)S(1)}, u32[]{:S(2)}, u32[]{:S(2)}) collective-permute-start(bf16[1,320,512]{2,1,0:T(8,128)(2,1)S(1)} %collective-permute-done.4), channel_id=1, source_target_pairs={{0,6},{2,0},{4,2},{6,4},{1,7},{3,1},{5,3},{7,5},{8,14},{10,8},{12,... | collective-permute-start | bytes 983048 | tf_op jit(solution)/shard_map/ppermute | solution.py:50
  71.0 2.1 %collective-permute-start.7 = (bf16[1,320,512]{2,1,0:T(8,128)(2,1)S(1)}, bf16[1,320,512]{2,1,0:T(8,128)(2,1)S(1)}, u32[]{:S(2)}, u32[]{:S(2)}) collective-permute-start(bf16[1,320,512]{2,1,0:T(8,128)(2,1)S(1)} %slice.14), channel_id=1, source_target_pairs={{0,2},{2,4},{4,6},{6,0},{1,3},{3,5},{5,7},{7,1},{8,10},{10,12},{12... | collective-permute-start | bytes 983048 | tf_op jit(solution)/shard_map/ppermute | solution.py:50
  73.1 1.3 fusion.17
  76.3 4.1 %collective-permute-done.6 = bf16[1,320,512]{2,1,0:T(8,128)(2,1)S(1)} collective-permute-done((bf16[1,320,512]{2,1,0:T(8,128)(2,1)S(1)}, bf16[1,320,512]{2,1,0:T(8,128)(2,1)S(1)}, u32[]{:S(2)}, u32[]{:S(2)}) %collective-permute-start.6) | collective-permute-done | bytes 327712 | tf_op jit(solution)/shard_map/ppermute | solution.py:50
  80.4 1.3 collective-permute-done.7
  82.5 12.4 %all-gather = bf16[4,192,640]{2,1,0:T(8,128)(2,1)S(1)} all-gather(bf16[1,192,640]{2,1,0:T(8,128)(2,1)S(1)} %fusion.14), channel_id=2, replica_groups=mesh['dp'=64,'tensor'=4,'sect'=2] {'tensor'}, dimensions={0}, use_global_device_ids=true | all-gather | bytes 1228800 | tf_op jit(solution)/shard_map/all_gather | solution.py:107
  96.5 1.3 fusion.3
  97.9 1.4 %reshape_transpose_reshape.7 = bf16[128,20,128]{2,1,0:T(8,128)(2,1)} reshape(bf16[640,512]{1,0:T(8,128)(2,1)S(1)} %fusion.3) | data formatting | bytes 1310720 | tf_op jit(solution)/shard_map/reshape;transpose;reshape | solution.py:166
  99.3 10.4 %all-to-all-start.1 = ((bf16[128,20,128]{2,1,0:T(8,128)(2,1)}), bf16[128,20,128]{2,1,0:T(8,128)(2,1)S(1)}, u32[]{:S(2)}, u32[]{:S(2)}) async-start(bf16[128,20,128]{2,1,0:T(8,128)(2,1)} %reshape_transpose_reshape.7), calls=%async_computation.1 | async-start | bytes 1572864 | tf_op jit(solution)/shard_map/all_to_all | solution.py:163
  110.7 1.6 %convolution_convert_fusion.5 = bf16[32,16,128]{2,1,0:T(8,128)(2,1)} fusion(bf16[32,128,1,128]{3,1,2,0:T(8,128)(2,1)S(1)} %copy-done.15, f32[32,16]{1,0:T(8,128)S(1)} %fusion.75, f32[32,16,128]{2,1,0:T(8,128)S(1)} %fusion.13), kind=kOutput, calls=%fused_computation.27 | convolution fusion | flops 17040000 | bytes 1443840 | tf_op jit(solution)/shard_map/rkgl,rlkd->rkgd/dot_general | solution.py:45
  113.0 22.7 %all-to-all-done.1 = bf16[128,20,128]{2,1,0:T(8,128)(2,1)S(1)} async-done(((bf16[128,20,128]{2,1,0:T(8,128)(2,1)}), bf16[128,20,128]{2,1,0:T(8,128)(2,1)S(1)}, u32[]{:S(2)}, u32[]{:S(2)}) %all-to-all-start.1) | async-done | bytes 655392 | tf_op jit(solution)/shard_map/all_to_all | solution.py:163
  (75 shorter events, 13.0 us)
Async XLA Ops:
  0.6 109.1 %copy-start = (bf16[32,128,1,128]{3,1,2,0:T(8,128)(2,1)S(1)}, bf16[32,128,1,128]{3,1,2,0:T(8,128)(2,1)}, u32[]{:S(2)}) copy-start(bf16[32,128,1,128]{3,1,2,0:T(8,128)(2,1)} %param.17) | copy-start | bytes 3145732
  0.6 1.8 %copy-start.11 = (bf16[32,512]{1,0:T(8,128)(2,1)S(1)}, bf16[32,512]{1,0:T(8,128)(2,1)}, u32[]{:S(2)}) copy-start(bf16[32,512]{1,0:T(8,128)(2,1)} %param.10) | copy-start | bytes 98308
  2.9 19.9 %copy-start.2 = (bf16[1,192,2048]{2,1,0:T(8,128)(2,1)S(1)}, bf16[1,192,2048]{2,1,0:T(8,128)(2,1)}, u32[]{:S(2)}) copy-start(bf16[1,192,2048]{2,1,0:T(8,128)(2,1)} %param.15) | copy-start | bytes 2359300
  4.3 44.4 %all-to-all-start = ((bf16[128,20,128]{2,1,0:T(8,128)(2,1)}), bf16[128,20,128]{2,1,0:T(8,128)(2,1)S(1)}, u32[]{:S(2)}, u32[]{:S(2)}) async-start(bf16[128,20,128]{2,1,0:T(8,128)(2,1)} %reshape.183), calls=%async_computation | async-start | bytes 1572864 | tf_op jit(solution)/shard_map/all_to_all | solution.py:146
  23.6 10.7 %collective-permute-start = (bf16[1,192,512]{2,1,0:T(8,128)(2,1)S(1)}, bf16[1,192,512]{2,1,0:T(8,128)(2,1)S(1)}, u32[]{:S(2)}, u32[]{:S(2)}) collective-permute-start(bf16[1,192,512]{2,1,0:T(8,128)(2,1)S(1)} %get-tuple-element.19), channel_id=1, source_target_pairs={{0,2},{2,4},{4,6},{6,0},{1,3},{3,5},{5,7},{7,1},{8,10},{10,12},{12... | collective-permute-start | bytes 589832 | tf_op jit(solution)/shard_map/ppermute | solution.py:50
  26.7 7.6 %collective-permute-start.1 = (bf16[1,192,512]{2,1,0:T(8,128)(2,1)S(1)}, bf16[1,192,512]{2,1,0:T(8,128)(2,1)S(1)}, u32[]{:S(2)}, u32[]{:S(2)}) collective-permute-start(bf16[1,192,512]{2,1,0:T(8,128)(2,1)S(1)} %get-tuple-element.21), channel_id=1, source_target_pairs={{0,6},{2,0},{4,2},{6,4},{1,7},{3,1},{5,3},{7,5},{8,14},{10,8},{12,... | collective-permute-start | bytes 589832 | tf_op jit(solution)/shard_map/ppermute | solution.py:50
  30.1 8.4 %collective-permute-start.2 = (bf16[1,192,512]{2,1,0:T(8,128)(2,1)S(1)}, bf16[1,192,512]{2,1,0:T(8,128)(2,1)}, u32[]{:S(2)}, u32[]{:S(2)}) collective-permute-start(bf16[1,192,512]{2,1,0:T(8,128)(2,1)S(1)} %get-tuple-element.18), channel_id=1, source_target_pairs={{0,4},{2,6},{4,0},{6,2},{1,5},{3,7},{5,1},{7,3},{8,12},{10,14},{12... | collective-permute-start | bytes 589832 | tf_op jit(solution)/shard_map/ppermute | solution.py:50
  50.0 20.9 %collective-permute-start.3 = (bf16[1,640,512]{2,1,0:T(8,128)(2,1)}, bf16[1,640,512]{2,1,0:T(8,128)(2,1)S(1)}, u32[]{:S(2)}, u32[]{:S(2)}) collective-permute-start(bf16[1,640,512]{2,1,0:T(8,128)(2,1)} %reshape_transpose_reshape.6), channel_id=1, source_target_pairs={{0,2},{2,4},{4,6},{6,0},{1,3},{3,5},{5,7},{7,1},{8,10},{10,12},{12... | collective-permute-start | bytes 1966088 | tf_op jit(solution)/shard_map/ppermute | solution.py:50
  55.1 11.3 %collective-permute-start.4 = (bf16[1,320,512]{2,1,0:T(8,128)(2,1)}, bf16[1,320,512]{2,1,0:T(8,128)(2,1)S(1)}, u32[]{:S(2)}, u32[]{:S(2)}) collective-permute-start(bf16[1,320,512]{2,1,0:T(8,128)(2,1)} %get-tuple-element.22), channel_id=1, source_target_pairs={{0,6},{2,0},{4,2},{6,4},{1,7},{3,1},{5,3},{7,5},{8,14},{10,8},{12,... | collective-permute-start | bytes 983048 | tf_op jit(solution)/shard_map/ppermute | solution.py:50
  59.0 15.3 %copy-start.5 = (bf16[1,2048,192]{1,2,0:T(8,128)(2,1)S(1)}, bf16[1,2048,192]{1,2,0:T(8,128)(2,1)}, u32[]{:S(2)}) copy-start(bf16[1,2048,192]{1,2,0:T(8,128)(2,1)} %param.14) | copy-start | bytes 2359300
  59.1 16.5 %collective-permute-start.5 = (bf16[1,320,512]{2,1,0:T(8,128)(2,1)}, bf16[1,320,512]{2,1,0:T(8,128)(2,1)S(1)}, u32[]{:S(2)}, u32[]{:S(2)}) collective-permute-start(bf16[1,320,512]{2,1,0:T(8,128)(2,1)} %get-tuple-element.23), channel_id=1, source_target_pairs={{0,6},{2,0},{4,2},{6,4},{1,7},{3,1},{5,3},{7,5},{8,14},{10,8},{12,... | collective-permute-start | bytes 983048 | tf_op jit(solution)/shard_map/ppermute | solution.py:50
  66.4 14.0 %collective-permute-start.6 = (bf16[1,320,512]{2,1,0:T(8,128)(2,1)S(1)}, bf16[1,320,512]{2,1,0:T(8,128)(2,1)S(1)}, u32[]{:S(2)}, u32[]{:S(2)}) collective-permute-start(bf16[1,320,512]{2,1,0:T(8,128)(2,1)S(1)} %collective-permute-done.4), channel_id=1, source_target_pairs={{0,6},{2,0},{4,2},{6,4},{1,7},{3,1},{5,3},{7,5},{8,14},{10,8},{12,... | collective-permute-start | bytes 983048 | tf_op jit(solution)/shard_map/ppermute | solution.py:50
  71.0 3.8 %copy-start.3 = (bf16[1,2048,192]{1,2,0:T(8,128)(2,1)S(1)}, bf16[1,2048,192]{1,2,0:T(8,128)(2,1)}, u32[]{:S(2)}) copy-start(bf16[1,2048,192]{1,2,0:T(8,128)(2,1)} %param.13) | copy-start | bytes 2359300
  71.0 10.7 %collective-permute-start.7 = (bf16[1,320,512]{2,1,0:T(8,128)(2,1)S(1)}, bf16[1,320,512]{2,1,0:T(8,128)(2,1)S(1)}, u32[]{:S(2)}, u32[]{:S(2)}) collective-permute-start(bf16[1,320,512]{2,1,0:T(8,128)(2,1)S(1)} %slice.14), channel_id=1, source_target_pairs={{0,2},{2,4},{4,6},{6,0},{1,3},{3,5},{5,7},{7,1},{8,10},{10,12},{12... | collective-permute-start | bytes 983048 | tf_op jit(solution)/shard_map/ppermute | solution.py:50
  82.4 12.4 %copy-start.1 = (bf16[1,192,512]{2,1,0:T(8,128)(2,1)S(1)}, bf16[1,192,512]{2,1,0:T(8,128)(2,1)}, u32[]{:S(2)}) copy-start(bf16[1,192,512]{2,1,0:T(8,128)(2,1)} %get-tuple-element.14) | copy-start | bytes 589828
  82.5 12.8 %copy-start.7 = (bf16[1,192,512]{2,1,0:T(8,128)(2,1)S(1)}, bf16[1,192,512]{2,1,0:T(8,128)(2,1)}, u32[]{:S(2)}) copy-start(bf16[1,192,512]{2,1,0:T(8,128)(2,1)} %copy-done.6) | copy-start | bytes 589828
  95.2 0.9 copy-start.9
  97.8 11.8 %copy-start.14 = (s32[32]{0:T(128)S(1)}, s32[32]{0:T(128)}, u32[]{:S(2)}) copy-start(s32[32]{0:T(128)} %param.19) | copy-start | bytes 388
  97.8 11.9 %copy-start.10 = (bf16[32,16,128]{2,1,0:T(8,128)(2,1)S(1)}, bf16[32,16,128]{2,1,0:T(8,128)(2,1)}, u32[]{:S(2)}) copy-start(bf16[32,16,128]{2,1,0:T(8,128)(2,1)} %param.16) | copy-start | bytes 393220
  99.3 11.4 %copy-start.15 = (bf16[32,128,1,128]{3,1,2,0:T(8,128)(2,1)S(1)}, bf16[32,128,1,128]{3,1,2,0:T(8,128)(2,1)}, u32[]{:S(2)}) copy-start(bf16[32,128,1,128]{3,1,2,0:T(8,128)(2,1)} %param.18) | copy-start | bytes 3145732
  99.3 36.4 %all-to-all-start.1 = ((bf16[128,20,128]{2,1,0:T(8,128)(2,1)}), bf16[128,20,128]{2,1,0:T(8,128)(2,1)S(1)}, u32[]{:S(2)}, u32[]{:S(2)}) async-start(bf16[128,20,128]{2,1,0:T(8,128)(2,1)} %reshape_transpose_reshape.7), calls=%async_computation.1 | async-start | bytes 1572864 | tf_op jit(solution)/shard_map/all_to_all | solution.py:163
  110.4 1.9 %copy-start.13 = (f32[32,8]{0,1:T(8,128)S(1)}, f32[32,8]{0,1:T(8,128)}, u32[]{:S(2)}) copy-start(f32[32,8]{0,1:T(8,128)} %param.12) | copy-start | bytes 3076
  110.4 2.0 %copy-start.12 = (s32[32,8]{0,1:T(8,128)S(1)}, s32[32,8]{0,1:T(8,128)}, u32[]{:S(2)}) copy-start(s32[32,8]{0,1:T(8,128)} %param.11) | copy-start | bytes 3076
  110.4 2.3 %copy-start.4 = (pred[128,5,32]{2,1,0:T(8,128)(4,1)S(1)}, pred[128,5,32]{2,1,0:T(8,128)(4,1)}, u32[]{:S(2)}) copy-start(pred[128,5,32]{2,1,0:T(8,128)(4,1)} %fusion.21) | copy-start | bytes 61444
  (2 other events, 1.4 us)

commit v14 on v10

--- a/solution.py
+++ b/solution.py
@@ -60,10 +60,7 @@
     me = lax.axis_index("tensor")
     from_left = shifted(inputs, 1, count)
     from_right = shifted(inputs, -1, count)
-    half = inputs.shape[1] // 2
-    far = jnp.concatenate(
-        [shifted(from_right[:, :half], -1, count), shifted(from_left[:, half:], 1, count)], axis=1
-    )
+    far = shifted(from_right, -1, count)
     gate = None
     up = None
     for piece, offset in ((inputs, 0), (from_left, count - 1), (from_right, 1), (far, 2)):

time: 144 us -> 145 us (level)
  waiting for transfers between devices: 58.3 us -> 63.1 us
  starting transfers between devices: 52.1 us -> 49.1 us
    ppermute x7 -> x6, waiting for transfers between devices: 24.6 us -> 29.5 us  [shifted(): lax.ppermute(x, 'tensor', perm=[(i, (i + step) % count) for i in range(co...]
    ppermute x7 -> x6, starting transfers between devices: 23.6 us -> 21.1 us  [shifted(): lax.ppermute(x, 'tensor', perm=[(i, (i + step) % count) for i in range(co...]
  transfers between devices with their start and end apart: 9 -> 8, of which waited for: 7 -> 7; matrix products, arithmetic and copies ran while one was open for 5% -> 5% of each run, Pallas kernels for 0% -> 0%
where the time goes in v14:
time: 145 us; the launch traced here: 144 us
  waiting for transfers between devices  63.1 us (44%)
  starting transfers between devices  49.1 us (34%)
  blocking collectives  12.3 us (8%)
  matrix products  9.18 us (6%)
  local copies, waits for them, and re-layouts  8.31 us (6%)
    ppermute x6, waiting for transfers between devices, shifted(): lax.ppermute(x, 'tensor', perm=[(i, (i + step) % count) for i in range(co...  29.5 us
    all_to_all x1, waiting for transfers between devices, local(): lax.all_to_all(summed.reshape(own_experts, owners, CAP, last).transpose(1...  22.7 us
    ppermute x6, starting transfers between devices, shifted(): lax.ppermute(x, 'tensor', perm=[(i, (i + step) % count) for i in range(co...  21.1 us
    all_to_all x1, starting transfers between devices, local(): lax.all_to_all(local_buffer, ('dp', 'sect'), split_axis=0, concat_axis=0,...  18.4 us
    all_gather x1, blocking collectives, down_projection(): hidden_all = lax.all_gather(hidden_t, 'tensor', axis=0, tiled=False)  12.3 us
    all_to_all x1, waiting for transfers between devices, local(): lax.all_to_all(local_buffer, ('dp', 'sect'), split_axis=0, concat_axis=0,...  10.9 us
    all_to_all x1, starting transfers between devices, local(): lax.all_to_all(summed.reshape(own_experts, owners, CAP, last).transpose(1...  9.62 us
  transfers between devices with their start and end apart: 8, of which 7 were waited for; matrix products, arithmetic and copies ran while one was open for 5% of the time, Pallas kernels for 0%

profile of v14, /device:TPU:1, one launch (start us, length us, event | category | flops | bytes accessed | tf_op | source)
XLA Modules:
  0.0 144.0 jit_solution(14308560648181927237)
XLA Ops:
  0.7 0.9 copy.25
  2.9 1.4 reshape.183
  4.3 18.4 %all-to-all-start = ((bf16[128,20,128]{2,1,0:T(8,128)(2,1)}), bf16[128,20,128]{2,1,0:T(8,128)(2,1)S(1)}, u32[]{:S(2)}, u32[]{:S(2)}) async-start(bf16[128,20,128]{2,1,0:T(8,128)(2,1)} %reshape.183), calls=%async_computation | async-start | bytes 1572864 | tf_op jit(solution)/shard_map/all_to_all | solution.py:142
  22.9 3.1 %collective-permute-start = (bf16[1,192,512]{2,1,0:T(8,128)(2,1)S(1)}, bf16[1,192,512]{2,1,0:T(8,128)(2,1)S(1)}, u32[]{:S(2)}, u32[]{:S(2)}) collective-permute-start(bf16[1,192,512]{2,1,0:T(8,128)(2,1)S(1)} %get-tuple-element.19), channel_id=1, source_target_pairs={{0,2},{2,4},{4,6},{6,0},{1,3},{3,5},{5,7},{7,1},{8,10},{10,12},{12... | collective-permute-start | bytes 589832 | tf_op jit(solution)/shard_map/ppermute | solution.py:50
  26.0 3.4 %collective-permute-start.1 = (bf16[1,192,512]{2,1,0:T(8,128)(2,1)S(1)}, bf16[1,192,512]{2,1,0:T(8,128)(2,1)S(1)}, u32[]{:S(2)}, u32[]{:S(2)}) collective-permute-start(bf16[1,192,512]{2,1,0:T(8,128)(2,1)S(1)} %get-tuple-element.21), channel_id=1, source_target_pairs={{0,6},{2,0},{4,2},{6,4},{1,7},{3,1},{5,3},{7,5},{8,14},{10,8},{12,... | collective-permute-start | bytes 589832 | tf_op jit(solution)/shard_map/ppermute | solution.py:50
  29.4 3.4 %collective-permute-start.2 = (bf16[1,192,512]{2,1,0:T(8,128)(2,1)S(1)}, bf16[1,192,512]{2,1,0:T(8,128)(2,1)S(1)}, u32[]{:S(2)}, u32[]{:S(2)}) collective-permute-start(bf16[1,192,512]{2,1,0:T(8,128)(2,1)S(1)} %get-tuple-element.18), channel_id=1, source_target_pairs={{0,4},{2,6},{4,0},{6,2},{1,5},{3,7},{5,1},{7,3},{8,12},{10,14},{12... | collective-permute-start | bytes 589832 | tf_op jit(solution)/shard_map/ppermute | solution.py:50
  33.1 4.6 %collective-permute-done.2 = bf16[1,192,512]{2,1,0:T(8,128)(2,1)S(1)} collective-permute-done((bf16[1,192,512]{2,1,0:T(8,128)(2,1)S(1)}, bf16[1,192,512]{2,1,0:T(8,128)(2,1)S(1)}, u32[]{:S(2)}, u32[]{:S(2)}) %collective-permute-start.2) | collective-permute-done | bytes 196640 | tf_op jit(solution)/shard_map/ppermute | solution.py:50
  37.7 10.9 %all-to-all-done = bf16[128,20,128]{2,1,0:T(8,128)(2,1)S(1)} async-done(((bf16[128,20,128]{2,1,0:T(8,128)(2,1)}), bf16[128,20,128]{2,1,0:T(8,128)(2,1)S(1)}, u32[]{:S(2)}, u32[]{:S(2)}) %all-to-all-start) | async-done | bytes 655392 | tf_op jit(solution)/shard_map/all_to_all | solution.py:142
  48.7 1.4 reshape_transpose_reshape.6
  50.0 3.1 %collective-permute-start.3 = (bf16[1,640,512]{2,1,0:T(8,128)(2,1)}, bf16[1,640,512]{2,1,0:T(8,128)(2,1)S(1)}, u32[]{:S(2)}, u32[]{:S(2)}) collective-permute-start(bf16[1,640,512]{2,1,0:T(8,128)(2,1)} %reshape_transpose_reshape.6), channel_id=1, source_target_pairs={{0,2},{2,4},{4,6},{6,0},{1,3},{3,5},{5,7},{7,1},{8,10},{10,12},{12... | collective-permute-start | bytes 1966088 | tf_op jit(solution)/shard_map/ppermute | solution.py:50
  53.7 3.5 %collective-permute-start.4 = (bf16[1,640,512]{2,1,0:T(8,128)(2,1)}, bf16[1,640,512]{2,1,0:T(8,128)(2,1)S(1)}, u32[]{:S(2)}, u32[]{:S(2)}) collective-permute-start(bf16[1,640,512]{2,1,0:T(8,128)(2,1)} %reshape_transpose_reshape.6), channel_id=1, source_target_pairs={{0,6},{2,0},{4,2},{6,4},{1,7},{3,1},{5,3},{7,5},{8,14},{10,8},{12,... | collective-permute-start | bytes 1966088 | tf_op jit(solution)/shard_map/ppermute | solution.py:50
  57.2 12.5 %collective-permute-done.3 = bf16[1,640,512]{2,1,0:T(8,128)(2,1)S(1)} collective-permute-done((bf16[1,640,512]{2,1,0:T(8,128)(2,1)}, bf16[1,640,512]{2,1,0:T(8,128)(2,1)S(1)}, u32[]{:S(2)}, u32[]{:S(2)}) %collective-permute-start.3) | collective-permute-done | bytes 655392 | tf_op jit(solution)/shard_map/ppermute | solution.py:50
  69.8 1.3 fusion.18
  72.2 4.6 %collective-permute-start.5 = (bf16[1,640,512]{2,1,0:T(8,128)(2,1)S(1)}, bf16[1,640,512]{2,1,0:T(8,128)(2,1)S(1)}, u32[]{:S(2)}, u32[]{:S(2)}) collective-permute-start(bf16[1,640,512]{2,1,0:T(8,128)(2,1)S(1)} %collective-permute-done.4), channel_id=1, source_target_pairs={{0,6},{2,0},{4,2},{6,4},{1,7},{3,1},{5,3},{7,5},{8,14},{10,8},{12,... | collective-permute-start | bytes 1966088 | tf_op jit(solution)/shard_map/ppermute | solution.py:50
  77.9 11.9 %collective-permute-done.5 = bf16[1,640,512]{2,1,0:T(8,128)(2,1)S(1)} collective-permute-done((bf16[1,640,512]{2,1,0:T(8,128)(2,1)S(1)}, bf16[1,640,512]{2,1,0:T(8,128)(2,1)S(1)}, u32[]{:S(2)}, u32[]{:S(2)}) %collective-permute-start.5) | collective-permute-done | bytes 655392 | tf_op jit(solution)/shard_map/ppermute | solution.py:50
  90.6 12.3 %all-gather = bf16[4,192,640]{2,1,0:T(8,128)(2,1)S(1)} all-gather(bf16[1,192,640]{2,1,0:T(8,128)(2,1)S(1)} %fusion.31), channel_id=2, replica_groups=mesh['dp'=64,'tensor'=4,'sect'=2] {'tensor'}, dimensions={0}, use_global_device_ids=true | all-gather | bytes 1228800 | tf_op jit(solution)/shard_map/all_gather | solution.py:103
  103.6 0.5 copy-done.7
  104.6 0.5 copy-done.9
  105.5 1.4 reshape_transpose_reshape.7
  106.9 9.6 %all-to-all-start.1 = ((bf16[128,20,128]{2,1,0:T(8,128)(2,1)}), bf16[128,20,128]{2,1,0:T(8,128)(2,1)S(1)}, u32[]{:S(2)}, u32[]{:S(2)}) async-start(bf16[128,20,128]{2,1,0:T(8,128)(2,1)} %reshape_transpose_reshape.7), calls=%async_computation.1 | async-start | bytes 1572864 | tf_op jit(solution)/shard_map/all_to_all | solution.py:159
  116.6 0.7 fusion.11
  117.5 1.6 %convolution_convert_fusion.5 = bf16[32,16,128]{2,1,0:T(8,128)(2,1)} fusion(bf16[32,128,1,128]{3,1,2,0:T(8,128)(2,1)S(1)} %copy-done.15, f32[32,16]{1,0:T(8,128)S(1)} %fusion.76, f32[32,16,128]{2,1,0:T(8,128)S(1)} %fusion.11), kind=kOutput, calls=%fused_computation.24 | convolution fusion | flops 17040000 | bytes 1443840 | tf_op jit(solution)/shard_map/rkgl,rlkd->rkgd/dot_general | solution.py:45
  119.8 22.7 %all-to-all-done.1 = bf16[128,20,128]{2,1,0:T(8,128)(2,1)S(1)} async-done(((bf16[128,20,128]{2,1,0:T(8,128)(2,1)}), bf16[128,20,128]{2,1,0:T(8,128)(2,1)S(1)}, u32[]{:S(2)}, u32[]{:S(2)}) %all-to-all-start.1) | async-done | bytes 655392 | tf_op jit(solution)/shard_map/all_to_all | solution.py:159
  143.1 0.9 convolution_convert_fusion.6
  (69 shorter events, 8.2 us)
Async XLA Ops:
  0.6 116.0 %copy-start = (bf16[32,128,1,128]{3,1,2,0:T(8,128)(2,1)S(1)}, bf16[32,128,1,128]{3,1,2,0:T(8,128)(2,1)}, u32[]{:S(2)}) copy-start(bf16[32,128,1,128]{3,1,2,0:T(8,128)(2,1)} %param.17) | copy-start | bytes 3145732
  0.6 1.8 %copy-start.11 = (bf16[32,512]{1,0:T(8,128)(2,1)S(1)}, bf16[32,512]{1,0:T(8,128)(2,1)}, u32[]{:S(2)}) copy-start(bf16[32,512]{1,0:T(8,128)(2,1)} %param.10) | copy-start | bytes 98308
  2.9 19.9 %copy-start.1 = (bf16[1,192,2048]{2,1,0:T(8,128)(2,1)S(1)}, bf16[1,192,2048]{2,1,0:T(8,128)(2,1)}, u32[]{:S(2)}) copy-start(bf16[1,192,2048]{2,1,0:T(8,128)(2,1)} %param.15) | copy-start | bytes 2359300
  4.3 44.3 %all-to-all-start = ((bf16[128,20,128]{2,1,0:T(8,128)(2,1)}), bf16[128,20,128]{2,1,0:T(8,128)(2,1)S(1)}, u32[]{:S(2)}, u32[]{:S(2)}) async-start(bf16[128,20,128]{2,1,0:T(8,128)(2,1)} %reshape.183), calls=%async_computation | async-start | bytes 1572864 | tf_op jit(solution)/shard_map/all_to_all | solution.py:142
  22.9 10.1 %collective-permute-start = (bf16[1,192,512]{2,1,0:T(8,128)(2,1)S(1)}, bf16[1,192,512]{2,1,0:T(8,128)(2,1)S(1)}, u32[]{:S(2)}, u32[]{:S(2)}) collective-permute-start(bf16[1,192,512]{2,1,0:T(8,128)(2,1)S(1)} %get-tuple-element.19), channel_id=1, source_target_pairs={{0,2},{2,4},{4,6},{6,0},{1,3},{3,5},{5,7},{7,1},{8,10},{10,12},{12... | collective-permute-start | bytes 589832 | tf_op jit(solution)/shard_map/ppermute | solution.py:50
  26.0 7.1 %collective-permute-start.1 = (bf16[1,192,512]{2,1,0:T(8,128)(2,1)S(1)}, bf16[1,192,512]{2,1,0:T(8,128)(2,1)S(1)}, u32[]{:S(2)}, u32[]{:S(2)}) collective-permute-start(bf16[1,192,512]{2,1,0:T(8,128)(2,1)S(1)} %get-tuple-element.21), channel_id=1, source_target_pairs={{0,6},{2,0},{4,2},{6,4},{1,7},{3,1},{5,3},{7,5},{8,14},{10,8},{12,... | collective-permute-start | bytes 589832 | tf_op jit(solution)/shard_map/ppermute | solution.py:50
  29.4 8.3 %collective-permute-start.2 = (bf16[1,192,512]{2,1,0:T(8,128)(2,1)S(1)}, bf16[1,192,512]{2,1,0:T(8,128)(2,1)S(1)}, u32[]{:S(2)}, u32[]{:S(2)}) collective-permute-start(bf16[1,192,512]{2,1,0:T(8,128)(2,1)S(1)} %get-tuple-element.18), channel_id=1, source_target_pairs={{0,4},{2,6},{4,0},{6,2},{1,5},{3,7},{5,1},{7,3},{8,12},{10,14},{12... | collective-permute-start | bytes 589832 | tf_op jit(solution)/shard_map/ppermute | solution.py:50
  33.0 15.7 %copy-start.4 = (bf16[1,192,512]{2,1,0:T(8,128)(2,1)}, bf16[1,192,512]{2,1,0:T(8,128)(2,1)S(1)}, u32[]{:S(2)}) copy-start(bf16[1,192,512]{2,1,0:T(8,128)(2,1)S(1)} %collective-permute-done) | copy-start | bytes 589828
  33.1 15.5 %copy-start.6 = (bf16[1,192,512]{2,1,0:T(8,128)(2,1)}, bf16[1,192,512]{2,1,0:T(8,128)(2,1)S(1)}, u32[]{:S(2)}) copy-start(bf16[1,192,512]{2,1,0:T(8,128)(2,1)S(1)} %collective-permute-done.1) | copy-start | bytes 589828
  37.7 10.9 %copy-start.8 = (bf16[1,192,512]{2,1,0:T(8,128)(2,1)}, bf16[1,192,512]{2,1,0:T(8,128)(2,1)S(1)}, u32[]{:S(2)}) copy-start(bf16[1,192,512]{2,1,0:T(8,128)(2,1)S(1)} %collective-permute-done.2) | copy-start | bytes 589828
  50.0 19.7 %collective-permute-start.3 = (bf16[1,640,512]{2,1,0:T(8,128)(2,1)}, bf16[1,640,512]{2,1,0:T(8,128)(2,1)S(1)}, u32[]{:S(2)}, u32[]{:S(2)}) collective-permute-start(bf16[1,640,512]{2,1,0:T(8,128)(2,1)} %reshape_transpose_reshape.6), channel_id=1, source_target_pairs={{0,2},{2,4},{4,6},{6,0},{1,3},{3,5},{5,7},{7,1},{8,10},{10,12},{12... | collective-permute-start | bytes 1966088 | tf_op jit(solution)/shard_map/ppermute | solution.py:50
  53.7 17.4 %copy-start.2 = (bf16[1,2048,192]{1,2,0:T(8,128)(2,1)S(1)}, bf16[1,2048,192]{1,2,0:T(8,128)(2,1)}, u32[]{:S(2)}) copy-start(bf16[1,2048,192]{1,2,0:T(8,128)(2,1)} %param.13) | copy-start | bytes 2359300
  53.7 17.8 %copy-start.3 = (bf16[1,2048,192]{1,2,0:T(8,128)(2,1)S(1)}, bf16[1,2048,192]{1,2,0:T(8,128)(2,1)}, u32[]{:S(2)}) copy-start(bf16[1,2048,192]{1,2,0:T(8,128)(2,1)} %param.14) | copy-start | bytes 2359300
  53.7 18.4 %collective-permute-start.4 = (bf16[1,640,512]{2,1,0:T(8,128)(2,1)}, bf16[1,640,512]{2,1,0:T(8,128)(2,1)S(1)}, u32[]{:S(2)}, u32[]{:S(2)}) collective-permute-start(bf16[1,640,512]{2,1,0:T(8,128)(2,1)} %reshape_transpose_reshape.6), channel_id=1, source_target_pairs={{0,6},{2,0},{4,2},{6,4},{1,7},{3,1},{5,3},{7,5},{8,14},{10,8},{12,... | collective-permute-start | bytes 1966088 | tf_op jit(solution)/shard_map/ppermute | solution.py:50
  72.2 17.6 %collective-permute-start.5 = (bf16[1,640,512]{2,1,0:T(8,128)(2,1)S(1)}, bf16[1,640,512]{2,1,0:T(8,128)(2,1)S(1)}, u32[]{:S(2)}, u32[]{:S(2)}) collective-permute-start(bf16[1,640,512]{2,1,0:T(8,128)(2,1)S(1)} %collective-permute-done.4), channel_id=1, source_target_pairs={{0,6},{2,0},{4,2},{6,4},{1,7},{3,1},{5,3},{7,5},{8,14},{10,8},{12,... | collective-permute-start | bytes 1966088 | tf_op jit(solution)/shard_map/ppermute | solution.py:50
  90.6 12.6 %copy-start.5 = (bf16[1,192,512]{2,1,0:T(8,128)(2,1)S(1)}, bf16[1,192,512]{2,1,0:T(8,128)(2,1)}, u32[]{:S(2)}) copy-start(bf16[1,192,512]{2,1,0:T(8,128)(2,1)} %copy-done.4) | copy-start | bytes 589828
  103.2 0.9 copy-start.7
  104.2 0.9 copy-start.9
  105.5 11.1 %copy-start.14 = (s32[32]{0:T(128)S(1)}, s32[32]{0:T(128)}, u32[]{:S(2)}) copy-start(s32[32]{0:T(128)} %param.19) | copy-start | bytes 388
  105.5 11.1 %copy-start.10 = (bf16[32,16,128]{2,1,0:T(8,128)(2,1)S(1)}, bf16[32,16,128]{2,1,0:T(8,128)(2,1)}, u32[]{:S(2)}) copy-start(bf16[32,16,128]{2,1,0:T(8,128)(2,1)} %param.16) | copy-start | bytes 393220
  106.9 10.6 %copy-start.15 = (bf16[32,128,1,128]{3,1,2,0:T(8,128)(2,1)S(1)}, bf16[32,128,1,128]{3,1,2,0:T(8,128)(2,1)}, u32[]{:S(2)}) copy-start(bf16[32,128,1,128]{3,1,2,0:T(8,128)(2,1)} %param.18) | copy-start | bytes 3145732
  106.9 35.7 %all-to-all-start.1 = ((bf16[128,20,128]{2,1,0:T(8,128)(2,1)}), bf16[128,20,128]{2,1,0:T(8,128)(2,1)S(1)}, u32[]{:S(2)}, u32[]{:S(2)}) async-start(bf16[128,20,128]{2,1,0:T(8,128)(2,1)} %reshape_transpose_reshape.7), calls=%async_computation.1 | async-start | bytes 1572864 | tf_op jit(solution)/shard_map/all_to_all | solution.py:159
  117.3 1.9 %copy-start.13 = (f32[32,8]{0,1:T(8,128)S(1)}, f32[32,8]{0,1:T(8,128)}, u32[]{:S(2)}) copy-start(f32[32,8]{0,1:T(8,128)} %param.12) | copy-start | bytes 3076
  117.3 2.0 %copy-start.12 = (s32[32,8]{0,1:T(8,128)S(1)}, s32[32,8]{0,1:T(8,128)}, u32[]{:S(2)}) copy-start(s32[32,8]{0,1:T(8,128)} %param.11) | copy-start | bytes 3076

commit v15 on v11

--- a/solution.py
+++ b/solution.py
@@ -60,10 +60,10 @@
     me = lax.axis_index("tensor")
     half = inputs.shape[1] // 2
     top, bottom = inputs[:, :half], inputs[:, half:]
-    right_top = shifted(top, -1, count)
     left_bottom = shifted(bottom, 1, count)
+    from_right = shifted(inputs, -1, count)
+    right_top = from_right[:, :half]
     from_left = jnp.concatenate([shifted(top, 1, count), left_bottom], axis=1)
-    from_right = jnp.concatenate([right_top, shifted(bottom, -1, count)], axis=1)
     far = jnp.concatenate([shifted(right_top, -1, count), shifted(left_bottom, 1, count)], axis=1)
     gate = None
     up = None

time: 140 us -> 140 us (level)
  waiting for transfers between devices: 47.8 us -> 52.1 us
  starting transfers between devices: 58.4 us -> 55.2 us
    ppermute x9 -> x8, waiting for transfers between devices: 14.1 us -> 18.4 us  [shifted(): lax.ppermute(x, 'tensor', perm=[(i, (i + step) % count) for i in range(co...]
    ppermute x9 -> x8, starting transfers between devices: 29.4 us -> 26.1 us  [shifted(): lax.ppermute(x, 'tensor', perm=[(i, (i + step) % count) for i in range(co...]
  transfers between devices with their start and end apart: 11 -> 10, of which waited for: 8 -> 8; matrix products, arithmetic and copies ran while one was open for 7% -> 6% of each run, Pallas kernels for 0% -> 0%
where the time goes in v15:
time: 140 us
  starting transfers between devices  55.2 us (39%)
  waiting for transfers between devices  52.1 us (37%)
  blocking collectives  11.9 us (8%)
  matrix products  10.4 us (7%)
  local copies, waits for them, and re-layouts  8.39 us (6%)
    ppermute x8, starting transfers between devices, shifted(): lax.ppermute(x, 'tensor', perm=[(i, (i + step) % count) for i in range(co...  26.1 us
    all_to_all x1, waiting for transfers between devices, local(): lax.all_to_all(summed.reshape(own_experts, owners, CAP, last).transpose(1...  22.7 us
    all_to_all x1, starting transfers between devices, local(): lax.all_to_all(local_buffer, ('dp', 'sect'), split_axis=0, concat_axis=0,...  18.4 us
    ppermute x8, waiting for transfers between devices, shifted(): lax.ppermute(x, 'tensor', perm=[(i, (i + step) % count) for i in range(co...  18.4 us
    all_gather x1, blocking collectives, down_projection(): hidden_all = lax.all_gather(hidden_t, 'tensor', axis=0, tiled=False)  11.9 us
    all_to_all x1, waiting for transfers between devices, local(): lax.all_to_all(local_buffer, ('dp', 'sect'), split_axis=0, concat_axis=0,...  10.9 us
    all_to_all x1, starting transfers between devices, local(): lax.all_to_all(summed.reshape(own_experts, owners, CAP, last).transpose(1...  10.6 us
  transfers between devices with their start and end apart: 10, of which 8 were waited for; matrix products, arithmetic and copies ran while one was open for 6% of the time, Pallas kernels for 0%

profile of v15, /device:TPU:1, one launch (start us, length us, event | category | flops | bytes accessed | tf_op | source)
XLA Modules:
  0.0 139.9 jit_solution(8957519554233121825)
XLA Ops:
  2.9 1.4 %reshape.183 = bf16[128,20,128]{2,1,0:T(8,128)(2,1)} reshape(bf16[640,512]{1,0:T(8,128)(2,1)S(1)} %convolution_convert_fusion) | data formatting | bytes 1310720 | tf_op jit(solution)/shard_map/reshape | solution.py:144
  4.3 18.4 %all-to-all-start = ((bf16[128,20,128]{2,1,0:T(8,128)(2,1)}), bf16[128,20,128]{2,1,0:T(8,128)(2,1)S(1)}, u32[]{:S(2)}, u32[]{:S(2)}) async-start(bf16[128,20,128]{2,1,0:T(8,128)(2,1)} %reshape.183), calls=%async_computation | async-start | bytes 1572864 | tf_op jit(solution)/shard_map/all_to_all | solution.py:146
  22.9 3.1 %collective-permute-start = (bf16[1,192,512]{2,1,0:T(8,128)(2,1)S(1)}, bf16[1,192,512]{2,1,0:T(8,128)(2,1)S(1)}, u32[]{:S(2)}, u32[]{:S(2)}) collective-permute-start(bf16[1,192,512]{2,1,0:T(8,128)(2,1)S(1)} %get-tuple-element.19), channel_id=1, source_target_pairs={{0,2},{2,4},{4,6},{6,0},{1,3},{3,5},{5,7},{7,1},{8,10},{10,12},{12... | collective-permute-start | bytes 589832 | tf_op jit(solution)/shard_map/ppermute | solution.py:50
  26.0 3.4 %collective-permute-start.1 = (bf16[1,192,512]{2,1,0:T(8,128)(2,1)S(1)}, bf16[1,192,512]{2,1,0:T(8,128)(2,1)S(1)}, u32[]{:S(2)}, u32[]{:S(2)}) collective-permute-start(bf16[1,192,512]{2,1,0:T(8,128)(2,1)S(1)} %get-tuple-element.21), channel_id=1, source_target_pairs={{0,6},{2,0},{4,2},{6,4},{1,7},{3,1},{5,3},{7,5},{8,14},{10,8},{12,... | collective-permute-start | bytes 589832 | tf_op jit(solution)/shard_map/ppermute | solution.py:50
  29.4 3.4 %collective-permute-start.2 = (bf16[1,192,512]{2,1,0:T(8,128)(2,1)S(1)}, bf16[1,192,512]{2,1,0:T(8,128)(2,1)S(1)}, u32[]{:S(2)}, u32[]{:S(2)}) collective-permute-start(bf16[1,192,512]{2,1,0:T(8,128)(2,1)S(1)} %get-tuple-element.18), channel_id=1, source_target_pairs={{0,4},{2,6},{4,0},{6,2},{1,5},{3,7},{5,1},{7,3},{8,12},{10,14},{12... | collective-permute-start | bytes 589832 | tf_op jit(solution)/shard_map/ppermute | solution.py:50
  33.1 4.6 %collective-permute-done.2 = bf16[1,192,512]{2,1,0:T(8,128)(2,1)S(1)} collective-permute-done((bf16[1,192,512]{2,1,0:T(8,128)(2,1)S(1)}, bf16[1,192,512]{2,1,0:T(8,128)(2,1)S(1)}, u32[]{:S(2)}, u32[]{:S(2)}) %collective-permute-start.2) | collective-permute-done | bytes 196640 | tf_op jit(solution)/shard_map/ppermute | solution.py:50
  37.7 10.9 %all-to-all-done = bf16[128,20,128]{2,1,0:T(8,128)(2,1)S(1)} async-done(((bf16[128,20,128]{2,1,0:T(8,128)(2,1)}), bf16[128,20,128]{2,1,0:T(8,128)(2,1)S(1)}, u32[]{:S(2)}, u32[]{:S(2)}) %all-to-all-start) | async-done | bytes 655392 | tf_op jit(solution)/shard_map/all_to_all | solution.py:146
  49.2 0.9 fusion.74
  50.1 3.1 %collective-permute-start.4 = (bf16[1,320,512]{2,1,0:T(8,128)(2,1)}, bf16[1,320,512]{2,1,0:T(8,128)(2,1)}, u32[]{:S(2)}, u32[]{:S(2)}) collective-permute-start(bf16[1,320,512]{2,1,0:T(8,128)(2,1)} %get-tuple-element.23), channel_id=1, source_target_pairs={{0,2},{2,4},{4,6},{6,0},{1,3},{3,5},{5,7},{7,1},{8,10},{10,12},{12... | collective-permute-start | bytes 983048 | tf_op jit(solution)/shard_map/ppermute | solution.py:50
  53.2 3.1 %collective-permute-start.3 = (bf16[1,320,512]{2,1,0:T(8,128)(2,1)}, bf16[1,320,512]{2,1,0:T(8,128)(2,1)}, u32[]{:S(2)}, u32[]{:S(2)}) collective-permute-start(bf16[1,320,512]{2,1,0:T(8,128)(2,1)} %get-tuple-element.22), channel_id=1, source_target_pairs={{0,2},{2,4},{4,6},{6,0},{1,3},{3,5},{5,7},{7,1},{8,10},{10,12},{12... | collective-permute-start | bytes 983048 | tf_op jit(solution)/shard_map/ppermute | solution.py:50
  56.9 3.5 %collective-permute-start.5 = (bf16[1,640,512]{2,1,0:T(8,128)(2,1)S(1)}, bf16[1,640,512]{2,1,0:T(8,128)(2,1)S(1)}, u32[]{:S(2)}, u32[]{:S(2)}) collective-permute-start(bf16[1,640,512]{2,1,0:T(8,128)(2,1)S(1)} %reshape_transpose_reshape.6), channel_id=1, source_target_pairs={{0,6},{2,0},{4,2},{6,4},{1,7},{3,1},{5,3},{7,5},{8,14},{10,8},{12,... | collective-permute-start | bytes 1966088 | tf_op jit(solution)/shard_map/ppermute | solution.py:50
  60.4 2.5 %collective-permute-done.4 = bf16[1,320,512]{2,1,0:T(8,128)(2,1)} collective-permute-done((bf16[1,320,512]{2,1,0:T(8,128)(2,1)}, bf16[1,320,512]{2,1,0:T(8,128)(2,1)}, u32[]{:S(2)}, u32[]{:S(2)}) %collective-permute-start.4) | collective-permute-done | bytes 327712 | tf_op jit(solution)/shard_map/ppermute | solution.py:50
  62.9 1.9 %collective-permute-start.7 = (bf16[1,320,512]{2,1,0:T(8,128)(2,1)}, bf16[1,320,512]{2,1,0:T(8,128)(2,1)S(1)}, u32[]{:S(2)}, u32[]{:S(2)}) collective-permute-start(bf16[1,320,512]{2,1,0:T(8,128)(2,1)} %collective-permute-done.4), channel_id=1, source_target_pairs={{0,2},{2,4},{4,6},{6,0},{1,3},{3,5},{5,7},{7,1},{8,10},{10,12},{12... | collective-permute-start | bytes 983048 | tf_op jit(solution)/shard_map/ppermute | solution.py:50
  64.8 5.1 %collective-permute-done.3 = bf16[1,320,512]{2,1,0:T(8,128)(2,1)} collective-permute-done((bf16[1,320,512]{2,1,0:T(8,128)(2,1)}, bf16[1,320,512]{2,1,0:T(8,128)(2,1)}, u32[]{:S(2)}, u32[]{:S(2)}) %collective-permute-start.3) | collective-permute-done | bytes 327712 | tf_op jit(solution)/shard_map/ppermute | solution.py:50
  69.9 1.5 %fusion.20 = f32[640,192]{0,1:T(8,128)S(1)} fusion(bf16[1,320,512]{2,1,0:T(8,128)(2,1)} %collective-permute-done.4, bf16[1,320,512]{2,1,0:T(8,128)(2,1)} %collective-permute-done.3, bf16[1,2048,192]{1,2,0:T(8,128)(2,1)} %param.14, s32[]{:T(128)S(6)} %select_n.92), kind=kOutput, calls=%fused_computation.38 | convolution fusion | flops 127139840 | bytes 1343492 | tf_op jit(solution)/shard_map/end,edf->enf/dot_general | solution.py:75
  71.4 1.4 %fusion.21 = f32[640,192]{0,1:T(8,128)S(1)} fusion(bf16[1,320,512]{2,1,0:T(8,128)(2,1)} %collective-permute-done.4, bf16[1,320,512]{2,1,0:T(8,128)(2,1)} %collective-permute-done.3, bf16[1,2048,192]{1,2,0:T(8,128)(2,1)S(1)} %copy-done.2, s32[]{:T(128)S(6)} %select_n.92), kind=kOutput, calls=%fused_computation.39 | convolution fusion | flops 127139840 | bytes 1343492 | tf_op jit(solution)/shard_map/end,edf->enf/dot_general | solution.py:74
  73.7 1.1 collective-permute-done.5
  74.8 4.6 %collective-permute-start.6 = (bf16[1,320,512]{2,1,0:T(8,128)(2,1)S(1)}, bf16[1,320,512]{2,1,0:T(8,128)(2,1)S(1)}, u32[]{:S(2)}, u32[]{:S(2)}) collective-permute-start(bf16[1,320,512]{2,1,0:T(8,128)(2,1)S(1)} %slice.14), channel_id=1, source_target_pairs={{0,6},{2,0},{4,2},{6,4},{1,7},{3,1},{5,3},{7,5},{8,14},{10,8},{12,... | collective-permute-start | bytes 983048 | tf_op jit(solution)/shard_map/ppermute | solution.py:50
  80.2 4.9 %collective-permute-done.6 = bf16[1,320,512]{2,1,0:T(8,128)(2,1)S(1)} collective-permute-done((bf16[1,320,512]{2,1,0:T(8,128)(2,1)S(1)}, bf16[1,320,512]{2,1,0:T(8,128)(2,1)S(1)}, u32[]{:S(2)}, u32[]{:S(2)}) %collective-permute-start.6) | collective-permute-done | bytes 327712 | tf_op jit(solution)/shard_map/ppermute | solution.py:50
  85.9 11.9 %all-gather = bf16[4,192,640]{2,1,0:T(8,128)(2,1)S(1)} all-gather(bf16[1,192,640]{2,1,0:T(8,128)(2,1)S(1)} %fusion.14), channel_id=2, replica_groups=mesh['dp'=64,'tensor'=4,'sect'=2] {'tensor'}, dimensions={0}, use_global_device_ids=true | all-gather | bytes 1228800 | tf_op jit(solution)/shard_map/all_gather | solution.py:107
  100.5 1.4 %reshape_transpose_reshape.7 = bf16[128,20,128]{2,1,0:T(8,128)(2,1)} reshape(bf16[640,512]{1,0:T(8,128)(2,1)S(1)} %fusion.3) | data formatting | bytes 1310720 | tf_op jit(solution)/shard_map/reshape;transpose;reshape | solution.py:166
  101.9 10.6 %all-to-all-start.1 = ((bf16[128,20,128]{2,1,0:T(8,128)(2,1)}), bf16[128,20,128]{2,1,0:T(8,128)(2,1)S(1)}, u32[]{:S(2)}, u32[]{:S(2)}) async-start(bf16[128,20,128]{2,1,0:T(8,128)(2,1)} %reshape_transpose_reshape.7), calls=%async_computation.1 | async-start | bytes 1572864 | tf_op jit(solution)/shard_map/all_to_all | solution.py:163
  113.5 1.6 %convolution_convert_fusion.5 = bf16[32,16,128]{2,1,0:T(8,128)(2,1)} fusion(bf16[32,128,1,128]{3,1,2,0:T(8,128)(2,1)S(1)} %copy-done.15, f32[32,16]{1,0:T(8,128)S(1)} %fusion.75, f32[32,16,128]{2,1,0:T(8,128)S(1)} %fusion.13), kind=kOutput, calls=%fused_computation.27 | convolution fusion | flops 17040000 | bytes 1443840 | tf_op jit(solution)/shard_map/rkgl,rlkd->rkgd/dot_general | solution.py:45
  115.8 22.7 %all-to-all-done.1 = bf16[128,20,128]{2,1,0:T(8,128)(2,1)S(1)} async-done(((bf16[128,20,128]{2,1,0:T(8,128)(2,1)}), bf16[128,20,128]{2,1,0:T(8,128)(2,1)S(1)}, u32[]{:S(2)}, u32[]{:S(2)}) %all-to-all-start.1) | async-done | bytes 655392 | tf_op jit(solution)/shard_map/all_to_all | solution.py:163
  (75 shorter events, 11.5 us)
Async XLA Ops:
  0.6 111.9 %copy-start = (bf16[32,128,1,128]{3,1,2,0:T(8,128)(2,1)S(1)}, bf16[32,128,1,128]{3,1,2,0:T(8,128)(2,1)}, u32[]{:S(2)}) copy-start(bf16[32,128,1,128]{3,1,2,0:T(8,128)(2,1)} %param.17) | copy-start | bytes 3145732
  0.6 1.8 %copy-start.11 = (bf16[32,512]{1,0:T(8,128)(2,1)S(1)}, bf16[32,512]{1,0:T(8,128)(2,1)}, u32[]{:S(2)}) copy-start(bf16[32,512]{1,0:T(8,128)(2,1)} %param.10) | copy-start | bytes 98308
  2.9 19.9 %copy-start.1 = (bf16[1,192,2048]{2,1,0:T(8,128)(2,1)S(1)}, bf16[1,192,2048]{2,1,0:T(8,128)(2,1)}, u32[]{:S(2)}) copy-start(bf16[1,192,2048]{2,1,0:T(8,128)(2,1)} %param.15) | copy-start | bytes 2359300
  4.3 44.4 %all-to-all-start = ((bf16[128,20,128]{2,1,0:T(8,128)(2,1)}), bf16[128,20,128]{2,1,0:T(8,128)(2,1)S(1)}, u32[]{:S(2)}, u32[]{:S(2)}) async-start(bf16[128,20,128]{2,1,0:T(8,128)(2,1)} %reshape.183), calls=%async_computation | async-start | bytes 1572864 | tf_op jit(solution)/shard_map/all_to_all | solution.py:146
  22.9 10.1 %collective-permute-start = (bf16[1,192,512]{2,1,0:T(8,128)(2,1)S(1)}, bf16[1,192,512]{2,1,0:T(8,128)(2,1)S(1)}, u32[]{:S(2)}, u32[]{:S(2)}) collective-permute-start(bf16[1,192,512]{2,1,0:T(8,128)(2,1)S(1)} %get-tuple-element.19), channel_id=1, source_target_pairs={{0,2},{2,4},{4,6},{6,0},{1,3},{3,5},{5,7},{7,1},{8,10},{10,12},{12... | collective-permute-start | bytes 589832 | tf_op jit(solution)/shard_map/ppermute | solution.py:50
  26.0 7.1 %collective-permute-start.1 = (bf16[1,192,512]{2,1,0:T(8,128)(2,1)S(1)}, bf16[1,192,512]{2,1,0:T(8,128)(2,1)S(1)}, u32[]{:S(2)}, u32[]{:S(2)}) collective-permute-start(bf16[1,192,512]{2,1,0:T(8,128)(2,1)S(1)} %get-tuple-element.21), channel_id=1, source_target_pairs={{0,6},{2,0},{4,2},{6,4},{1,7},{3,1},{5,3},{7,5},{8,14},{10,8},{12,... | collective-permute-start | bytes 589832 | tf_op jit(solution)/shard_map/ppermute | solution.py:50
  29.4 8.3 %collective-permute-start.2 = (bf16[1,192,512]{2,1,0:T(8,128)(2,1)S(1)}, bf16[1,192,512]{2,1,0:T(8,128)(2,1)S(1)}, u32[]{:S(2)}, u32[]{:S(2)}) collective-permute-start(bf16[1,192,512]{2,1,0:T(8,128)(2,1)S(1)} %get-tuple-element.18), channel_id=1, source_target_pairs={{0,4},{2,6},{4,0},{6,2},{1,5},{3,7},{5,1},{7,3},{8,12},{10,14},{12... | collective-permute-start | bytes 589832 | tf_op jit(solution)/shard_map/ppermute | solution.py:50
  33.0 15.7 %copy-start.3 = (bf16[1,192,512]{2,1,0:T(8,128)(2,1)}, bf16[1,192,512]{2,1,0:T(8,128)(2,1)S(1)}, u32[]{:S(2)}) copy-start(bf16[1,192,512]{2,1,0:T(8,128)(2,1)S(1)} %collective-permute-done) | copy-start | bytes 589828
  33.1 15.5 %copy-start.5 = (bf16[1,192,512]{2,1,0:T(8,128)(2,1)}, bf16[1,192,512]{2,1,0:T(8,128)(2,1)S(1)}, u32[]{:S(2)}) copy-start(bf16[1,192,512]{2,1,0:T(8,128)(2,1)S(1)} %collective-permute-done.1) | copy-start | bytes 589828
  37.7 10.9 %copy-start.8 = (bf16[1,192,512]{2,1,0:T(8,128)(2,1)}, bf16[1,192,512]{2,1,0:T(8,128)(2,1)S(1)}, u32[]{:S(2)}) copy-start(bf16[1,192,512]{2,1,0:T(8,128)(2,1)S(1)} %collective-permute-done.2) | copy-start | bytes 589828
  50.1 12.8 %collective-permute-start.4 = (bf16[1,320,512]{2,1,0:T(8,128)(2,1)}, bf16[1,320,512]{2,1,0:T(8,128)(2,1)}, u32[]{:S(2)}, u32[]{:S(2)}) collective-permute-start(bf16[1,320,512]{2,1,0:T(8,128)(2,1)} %get-tuple-element.23), channel_id=1, source_target_pairs={{0,2},{2,4},{4,6},{6,0},{1,3},{3,5},{5,7},{7,1},{8,10},{10,12},{12... | collective-permute-start | bytes 983048 | tf_op jit(solution)/shard_map/ppermute | solution.py:50
  53.2 16.7 %collective-permute-start.3 = (bf16[1,320,512]{2,1,0:T(8,128)(2,1)}, bf16[1,320,512]{2,1,0:T(8,128)(2,1)}, u32[]{:S(2)}, u32[]{:S(2)}) collective-permute-start(bf16[1,320,512]{2,1,0:T(8,128)(2,1)} %get-tuple-element.22), channel_id=1, source_target_pairs={{0,2},{2,4},{4,6},{6,0},{1,3},{3,5},{5,7},{7,1},{8,10},{10,12},{12... | collective-permute-start | bytes 983048 | tf_op jit(solution)/shard_map/ppermute | solution.py:50
  56.9 14.5 %copy-start.2 = (bf16[1,2048,192]{1,2,0:T(8,128)(2,1)S(1)}, bf16[1,2048,192]{1,2,0:T(8,128)(2,1)}, u32[]{:S(2)}) copy-start(bf16[1,2048,192]{1,2,0:T(8,128)(2,1)} %param.13) | copy-start | bytes 2359300
  56.9 16.0 %copy-start.7 = (bf16[1,2048,192]{1,2,0:T(8,128)(2,1)S(1)}, bf16[1,2048,192]{1,2,0:T(8,128)(2,1)}, u32[]{:S(2)}) copy-start(bf16[1,2048,192]{1,2,0:T(8,128)(2,1)} %param.14) | copy-start | bytes 2359300
  56.9 17.9 %collective-permute-start.5 = (bf16[1,640,512]{2,1,0:T(8,128)(2,1)S(1)}, bf16[1,640,512]{2,1,0:T(8,128)(2,1)S(1)}, u32[]{:S(2)}, u32[]{:S(2)}) collective-permute-start(bf16[1,640,512]{2,1,0:T(8,128)(2,1)S(1)} %reshape_transpose_reshape.6), channel_id=1, source_target_pairs={{0,6},{2,0},{4,2},{6,4},{1,7},{3,1},{5,3},{7,5},{8,14},{10,8},{12,... | collective-permute-start | bytes 1966088 | tf_op jit(solution)/shard_map/ppermute | solution.py:50
  62.9 17.3 %collective-permute-start.7 = (bf16[1,320,512]{2,1,0:T(8,128)(2,1)}, bf16[1,320,512]{2,1,0:T(8,128)(2,1)S(1)}, u32[]{:S(2)}, u32[]{:S(2)}) collective-permute-start(bf16[1,320,512]{2,1,0:T(8,128)(2,1)} %collective-permute-done.4), channel_id=1, source_target_pairs={{0,2},{2,4},{4,6},{6,0},{1,3},{3,5},{5,7},{7,1},{8,10},{10,12},{12... | collective-permute-start | bytes 983048 | tf_op jit(solution)/shard_map/ppermute | solution.py:50
  74.8 10.3 %collective-permute-start.6 = (bf16[1,320,512]{2,1,0:T(8,128)(2,1)S(1)}, bf16[1,320,512]{2,1,0:T(8,128)(2,1)S(1)}, u32[]{:S(2)}, u32[]{:S(2)}) collective-permute-start(bf16[1,320,512]{2,1,0:T(8,128)(2,1)S(1)} %slice.14), channel_id=1, source_target_pairs={{0,6},{2,0},{4,2},{6,4},{1,7},{3,1},{5,3},{7,5},{8,14},{10,8},{12,... | collective-permute-start | bytes 983048 | tf_op jit(solution)/shard_map/ppermute | solution.py:50
  85.9 12.3 %copy-start.4 = (bf16[1,192,512]{2,1,0:T(8,128)(2,1)S(1)}, bf16[1,192,512]{2,1,0:T(8,128)(2,1)}, u32[]{:S(2)}) copy-start(bf16[1,192,512]{2,1,0:T(8,128)(2,1)} %copy-done.3) | copy-start | bytes 589828
  100.4 12.0 %copy-start.14 = (s32[32]{0:T(128)S(1)}, s32[32]{0:T(128)}, u32[]{:S(2)}) copy-start(s32[32]{0:T(128)} %param.19) | copy-start | bytes 388
  100.4 12.1 %copy-start.10 = (bf16[32,16,128]{2,1,0:T(8,128)(2,1)S(1)}, bf16[32,16,128]{2,1,0:T(8,128)(2,1)}, u32[]{:S(2)}) copy-start(bf16[32,16,128]{2,1,0:T(8,128)(2,1)} %param.16) | copy-start | bytes 393220
  101.9 11.6 %copy-start.15 = (bf16[32,128,1,128]{3,1,2,0:T(8,128)(2,1)S(1)}, bf16[32,128,1,128]{3,1,2,0:T(8,128)(2,1)}, u32[]{:S(2)}) copy-start(bf16[32,128,1,128]{3,1,2,0:T(8,128)(2,1)} %param.18) | copy-start | bytes 3145732
  101.9 36.6 %all-to-all-start.1 = ((bf16[128,20,128]{2,1,0:T(8,128)(2,1)}), bf16[128,20,128]{2,1,0:T(8,128)(2,1)S(1)}, u32[]{:S(2)}, u32[]{:S(2)}) async-start(bf16[128,20,128]{2,1,0:T(8,128)(2,1)} %reshape_transpose_reshape.7), calls=%async_computation.1 | async-start | bytes 1572864 | tf_op jit(solution)/shard_map/all_to_all | solution.py:163
  113.2 1.9 %copy-start.13 = (f32[32,8]{0,1:T(8,128)S(1)}, f32[32,8]{0,1:T(8,128)}, u32[]{:S(2)}) copy-start(f32[32,8]{0,1:T(8,128)} %param.12) | copy-start | bytes 3076
  113.2 2.0 %copy-start.12 = (s32[32,8]{0,1:T(8,128)S(1)}, s32[32,8]{0,1:T(8,128)}, u32[]{:S(2)}) copy-start(s32[32,8]{0,1:T(8,128)} %param.11) | copy-start | bytes 3076
  (2 other events, 1.9 us)
